TPU v7x, 512 devices: a whole 4x4x16 slice. The times are simulated.
512 devices in a mesh: tm: 16 (over z_hi, x), space: 32 (over y, z_lo, core).
Axes of the slice: x: 4, y: 4, z: 16 (z_hi: 4, z_lo: 4; z = z_hi * 4 + z_lo), core: 2. Of those that a mesh axis runs over, the one named last changes fastest.
Arguments:
- queries: bfloat16 [32, 4096, 1536], P('tm', 'space'), may hold values from -110 to 110
- keys: bfloat16 [32, 4096, 1536], P('tm', 'space'), may hold values from -5.1 to 5.1
- values: bfloat16 [32, 4096, 1536], P('tm', 'space'), may hold values from -15 to 15
- tile_mask: int32 [32, 32, 5, 5], P('tm', 'space'), may hold values from 0 to 1, as said below
Outputs:
- attended: bfloat16 [32, 4096, 1536], P('tm', 'space')
Inputs may be any that keep to these rules, and one draw needn't show every extreme that they name: tile_mask[i, b, 2 + d, 2 + e] is 1 where tile (i, b) attends tile (i + d, b + e). It is 0 where |e| > 2 >> |d| or where the key tile lies outside the 32 x 32 tiles, and 1 for d = e = 0.
All inputs are finite; a program needn't handle non-finite values.
Results may differ from a plain program's by a relative error of at most 0.012.
Values may be sent and summed in bfloat16 or wider, within the bound.
No kernel may reach another device: no remote copies, remote signals or barrier semaphores. Data moves between devices by JAX's collectives and lax.ppermute only.
A program may use at most 192 MiB of HBM per device.

v0:
```python
import math

import jax
import jax.numpy as jnp
from jax import lax
from jax.sharding import PartitionSpec as P

HD = 128
TR = 2
W = 2


def shifted(block, axis, distance):
    devices = range(lax.axis_size(axis))
    route = [(i - distance, i) for i in devices if i - distance in devices]
    return lax.ppermute(block, axis, route)


def band_list():
    pairs = []
    for d in range(-TR, TR + 1):
        spread = W >> abs(d)
        for e in range(-spread, spread + 1):
            pairs.append((d, e))
    return pairs


def frame_reach(e):
    best = 0
    for d in range(TR + 1):
        if W >> d >= abs(e):
            best = d
    return best


def fetch_rows_first(stacked):
    frame_count = stacked.shape[1]
    nearby = {0: stacked}
    for e in range(-W, W + 1):
        if e != 0:
            nearby[e] = shifted(stacked, "space", -e)
    ordered = [e for e in range(-W, W + 1) if frame_reach(e) > 0]
    sent_forward = jnp.concatenate(
        [nearby[e][:, frame_count - frame_reach(e) :] for e in ordered], axis=1
    )
    sent_backward = jnp.concatenate([nearby[e][:, : frame_reach(e)] for e in ordered], axis=1)
    earlier = shifted(sent_forward, "tm", 1)
    following = shifted(sent_backward, "tm", -1)
    columns = {}
    position = 0
    for e in range(-W, W + 1):
        extent = frame_reach(e)
        if extent > 0:
            columns[e] = jnp.concatenate(
                [
                    earlier[:, position : position + extent],
                    nearby[e],
                    following[:, position : position + extent],
                ],
                axis=1,
            )
            position = position + extent
        else:
            columns[e] = nearby[e]
    return columns


def attend(queries, columns, tile_flags):
    frame_count, row_count, feature_width = queries.shape
    head_count = feature_width // HD
    head_group = 4
    span = head_group * HD
    score_scale = 1.0 / math.sqrt(HD)
    pairs = band_list()
    outputs = []
    for index in range(head_count // head_group):
        first_col = index * span
        query = queries[:, :, first_col : first_col + span].reshape(
            frame_count, row_count, head_group, HD
        )
        score_list = []
        value_list = []
        kept_list = []
        for d, e in pairs:
            start = d + frame_reach(e)
            key_tile = columns[e][:, start : start + frame_count, :, first_col : first_col + span]
            key_tile = key_tile.reshape(2, frame_count, row_count, head_group, HD)
            kept = tile_flags[:, TR + d, W + e] > 0

            def compute(query=query, key_tile=key_tile, kept=kept):
                raw = (
                    jnp.einsum(
                        "fqhc,fkhc->fhqk", query, key_tile[0], preferred_element_type=jnp.float32
                    )
                    * score_scale
                )
                return jnp.where(kept[:, None, None, None], raw, -jnp.inf)

            scores = compute()
            score_list.append(scores)
            value_list.append(key_tile[1])
            kept_list.append(kept)
        row_max = jnp.max(score_list[0], axis=3, keepdims=True)
        for scores in score_list[1:]:
            row_max = jnp.maximum(row_max, jnp.max(scores, axis=3, keepdims=True))
        denominator = jnp.zeros((frame_count, head_group, row_count), jnp.float32)
        summed = jnp.zeros((frame_count, row_count, head_group, HD), jnp.float32)
        for number in range(len(pairs)):
            weights = jnp.exp(score_list[number] - row_max)
            denominator = denominator + jnp.sum(weights, axis=3)
            rounded = weights.astype(jnp.bfloat16)

            def product(portion=rounded, value_tile=value_list[number]):
                return jnp.einsum(
                    "fhqk,fkhc->fqhc", portion, value_tile, preferred_element_type=jnp.float32
                )

            summed = summed + product()
        result = summed / jnp.transpose(denominator, (0, 2, 1))[..., None]
        outputs.append(result.reshape(frame_count, row_count, span))
    return jnp.concatenate(outputs, axis=2).astype(jnp.bfloat16)


def on_device(queries, keys, values, tile_mask):
    stacked = jnp.stack([keys, values], 0)
    columns = fetch_rows_first(stacked)
    tile_flags = tile_mask[:, 0]
    return attend(queries, columns, tile_flags)


def solution(mesh):
    in_specs = (
        P("tm", "space", None),
        P("tm", "space", None),
        P("tm", "space", None),
        P("tm", "space", None, None),
    )
    out_specs = P("tm", "space", None)
    return jax.shard_map(
        on_device, mesh=mesh, in_specs=in_specs, out_specs=out_specs, check_vma=False
    )
```

profile of v0, /device:TPU:329, one launch (start us, length us, event | category | flops | bytes accessed | tf_op | source)
XLA Modules:
  0.0 452.5 jit_solution(12305889595684928480)
XLA Ops:
  0.0 1.6 copy.93
  2.0 1.3 pad_maximum_fusion.3
  3.3 3.2 collective-permute-start
  6.5 1.9 collective-permute-start.1
  8.5 2.6 collective-permute-start.4
  11.1 3.8 collective-permute-start.3
  15.0 68.6 %collective-permute-done = bf16[2,2,128,1536]{2,3,1,0:T(8,128)(2,1)S(1)} collective-permute-done((bf16[2,2,128,1536]{2,3,1,0:T(8,128)(2,1)}, bf16[2,2,128,1536]{2,3,1,0:T(8,128)(2,1)S(1)}, u32[]{:S(2)}, u32[]{:S(2)}) %collective-permute-start) | collective-permute-done | bytes 1572896 | tf_op jit(solution)/shard_map/ppermute | solution.py:16
  83.8 1.0 copy-done
  84.9 1.1 copy-done.2
  86.0 2.9 pad_maximum_fusion
  88.9 41.6 %collective-permute-start.5 = (bf16[2,4,128,1536]{2,3,1,0:T(8,128)(2,1)}, bf16[2,4,128,1536]{2,3,1,0:T(8,128)(2,1)}, u32[]{:S(2)}, u32[]{:S(2)}) collective-permute-start(bf16[2,4,128,1536]{2,3,1,0:T(8,128)(2,1)} %get-tuple-element.134), channel_id=1, source_target_pairs={{32,0},{64,32},{96,64},{128,96},{160,128},{192,160},{224,192},{256... | collective-permute-start | bytes 9437192 | tf_op jit(solution)/shard_map/ppermute | solution.py:16
  130.6 1.9 collective-permute-start.2
  133.5 0.8 fusion.292
  134.6 1.1 fusion.312
  135.7 2.3 fusion.287
  138.3 1.1 fusion.310
  139.3 2.3 fusion.286
  141.9 1.1 fusion.314
  143.6 104.1 %collective-permute-done.5 = bf16[2,4,128,1536]{2,3,1,0:T(8,128)(2,1)} collective-permute-done((bf16[2,4,128,1536]{2,3,1,0:T(8,128)(2,1)}, bf16[2,4,128,1536]{2,3,1,0:T(8,128)(2,1)}, u32[]{:S(2)}, u32[]{:S(2)}) %collective-permute-start.5) | collective-permute-done | bytes 3145760 | tf_op jit(solution)/shard_map/ppermute | solution.py:16
  247.6 1.5 slice.693
  249.2 1.1 pad_maximum_fusion.32
  250.2 151.6 %collective-permute-done.2 = bf16[2,4,128,1536]{2,3,1,0:T(8,128)(2,1)} collective-permute-done((bf16[2,4,128,1536]{2,3,1,0:T(8,128)(2,1)}, bf16[2,4,128,1536]{2,3,1,0:T(8,128)(2,1)}, u32[]{:S(2)}, u32[]{:S(2)}) %collective-permute-start.2) | collective-permute-done | bytes 3145760 | tf_op jit(solution)/shard_map/ppermute | solution.py:16
  401.9 1.5 slice.675
  403.4 1.1 pad_maximum_fusion.35
  404.5 1.6 fusion.284
  406.4 1.5 pad_maximum_fusion.36
  408.4 0.8 copy-done.3
  409.2 1.3 pad_maximum_fusion.34
  411.1 1.5 fusion.285
  412.6 1.1 pad_maximum_fusion.31
  414.0 1.0 pad_maximum_fusion.33
  416.0 2.4 fusion.283
  418.6 2.4 fusion.282
  423.7 1.6 fusion.116
  426.2 0.8 copy.222
  428.1 0.5 fusion.315
  431.1 0.4 copy-done.6
  432.6 0.4 copy-done.5
  433.8 0.5 copy-done.28
  434.8 1.6 fusion.142
  436.7 0.7 copy-done.51
  437.7 0.6 copy-done.25
  438.6 0.9 copy.223
  447.0 1.6 fusion.168
  448.9 0.7 copy-done.50
  449.9 0.6 copy-done.17
  451.0 0.5 copy-done.48
  451.6 0.9 pad_maximum_fusion.4
  (201 shorter events, 24.4 us)
Async XLA Ops:
  0.0 1.6 copy-start.56
  2.0 13.0 %copy-start.58 = (s32[2,1,5,5]{3,1,2,0:T(1,128)S(1)}, s32[2,1,5,5]{3,1,2,0:T(1,128)}, u32[]{:S(2)}) copy-start(s32[2,1,5,5]{3,1,2,0:T(1,128)} %param.7) | copy-start | bytes 604
  2.0 13.0 %copy-start.57 = (bf16[2,128,1536]{2,1,0:T(8,128)(2,1)S(1)}, bf16[2,128,1536]{2,1,0:T(8,128)(2,1)}, u32[]{:S(2)}) copy-start(bf16[2,128,1536]{2,1,0:T(8,128)(2,1)} %param.4) | copy-start | bytes 2359300
  3.3 80.3 %collective-permute-start = (bf16[2,2,128,1536]{2,3,1,0:T(8,128)(2,1)}, bf16[2,2,128,1536]{2,3,1,0:T(8,128)(2,1)S(1)}, u32[]{:S(2)}, u32[]{:S(2)}) collective-permute-start(bf16[2,2,128,1536]{2,3,1,0:T(8,128)(2,1)} %pad_maximum_fusion.3), channel_id=1, source_target_pairs={{0,1},{1,2},{2,3},{3,4},{4,5},{5,6},{6,7},{7,8},{8,9},{9,10},{10,1... | collective-permute-start | bytes 4718600 | tf_op jit(solution)/shard_map/ppermute | solution.py:16
  6.5 78.3 %collective-permute-start.1 = (bf16[2,2,128,1536]{2,3,1,0:T(8,128)(2,1)}, bf16[2,2,128,1536]{2,3,1,0:T(8,128)(2,1)S(1)}, u32[]{:S(2)}, u32[]{:S(2)}) collective-permute-start(bf16[2,2,128,1536]{2,3,1,0:T(8,128)(2,1)} %pad_maximum_fusion.3), channel_id=1, source_target_pairs={{1,0},{2,1},{3,2},{4,3},{5,4},{6,5},{7,6},{8,7},{9,8},{10,9},{11,1... | collective-permute-start | bytes 4718600 | tf_op jit(solution)/shard_map/ppermute | solution.py:16
  8.5 127.2 %collective-permute-start.4 = (bf16[2,2,128,1536]{2,3,1,0:T(8,128)(2,1)}, bf16[2,2,128,1536]{2,3,1,0:T(8,128)(2,1)}, u32[]{:S(2)}, u32[]{:S(2)}) collective-permute-start(bf16[2,2,128,1536]{2,3,1,0:T(8,128)(2,1)} %pad_maximum_fusion.3), channel_id=1, source_target_pairs={{2,0},{3,1},{4,2},{5,3},{6,4},{7,5},{8,6},{9,7},{10,8},{11,9},{12,... | collective-permute-start | bytes 4718600 | tf_op jit(solution)/shard_map/ppermute | solution.py:16
  11.1 128.2 %collective-permute-start.3 = (bf16[2,2,128,1536]{2,3,1,0:T(8,128)(2,1)}, bf16[2,2,128,1536]{2,3,1,0:T(8,128)(2,1)}, u32[]{:S(2)}, u32[]{:S(2)}) collective-permute-start(bf16[2,2,128,1536]{2,3,1,0:T(8,128)(2,1)} %pad_maximum_fusion.3), channel_id=1, source_target_pairs={{0,2},{1,3},{2,4},{3,5},{4,6},{5,7},{6,8},{7,9},{8,10},{9,11},{10,... | collective-permute-start | bytes 4718600 | tf_op jit(solution)/shard_map/ppermute | solution.py:16
  83.7 1.1 copy-start
  84.8 1.2 copy-start.2
  88.9 158.7 %collective-permute-start.5 = (bf16[2,4,128,1536]{2,3,1,0:T(8,128)(2,1)}, bf16[2,4,128,1536]{2,3,1,0:T(8,128)(2,1)}, u32[]{:S(2)}, u32[]{:S(2)}) collective-permute-start(bf16[2,4,128,1536]{2,3,1,0:T(8,128)(2,1)} %get-tuple-element.134), channel_id=1, source_target_pairs={{32,0},{64,32},{96,64},{128,96},{160,128},{192,160},{224,192},{256... | collective-permute-start | bytes 9437192 | tf_op jit(solution)/shard_map/ppermute | solution.py:16
  130.6 271.3 %collective-permute-start.2 = (bf16[2,4,128,1536]{2,3,1,0:T(8,128)(2,1)}, bf16[2,4,128,1536]{2,3,1,0:T(8,128)(2,1)}, u32[]{:S(2)}, u32[]{:S(2)}) collective-permute-start(bf16[2,4,128,1536]{2,3,1,0:T(8,128)(2,1)} %get-tuple-element.133), channel_id=1, source_target_pairs={{0,32},{32,64},{64,96},{96,128},{128,160},{160,192},{192,224},{224... | collective-permute-start | bytes 9437192 | tf_op jit(solution)/shard_map/ppermute | solution.py:16
  404.5 1.9 copy-start.1
  407.8 1.4 copy-start.3
  425.9 1.2 copy-start.14
  426.2 1.2 copy-start.13
  426.2 1.5 copy-start.44
  427.1 1.0 copy-start.43
  427.4 1.2 copy-start.45
  427.7 1.2 copy-start.55
  428.1 1.1 copy-start.41
  428.6 1.0 copy-start.42
  428.9 1.0 copy-start.46
  429.2 1.0 copy-start.47
  429.9 1.0 copy-start.27
  430.5 1.1 copy-start.6
  430.5 1.1 copy-start.24
  430.8 1.1 copy-start.9
  431.1 1.1 copy-start.4
  431.1 1.2 copy-start.35
  431.9 1.1 copy-start.5
  431.9 1.2 copy-start.23
  432.1 1.1 copy-start.53
  432.5 1.0 copy-start.26
  434.8 1.7 copy-start.29
  438.3 1.2 copy-start.12
  438.6 1.2 copy-start.11
  438.6 1.5 copy-start.37
  439.5 1.0 copy-start.36
  440.1 1.0 copy-start.54
  440.8 1.0 copy-start.34
  441.1 1.0 copy-start.33
  441.5 1.0 copy-start.39
  442.1 1.0 copy-start.8
  443.4 1.0 copy-start.7
  443.7 1.0 copy-start.31
  444.9 1.0 copy-start.18
  447.0 1.6 copy-start.21
  450.6 1.0 copy-start.49
  (17 other events, 16.6 us)
where the time goes:
time: 453 us
  waiting for transfers between devices  324 us (72%)
  starting transfers between devices  55.1 us (12%)
  local copies, waits for them, and re-layouts  30.9 us (7%)
  matrix products  23.6 us (5%)
  other arithmetic  17.7 us (4%)
    ppermute x6, waiting for transfers between devices, shifted(): return lax.ppermute(block, axis, route)  324 us
    ppermute x6, starting transfers between devices, shifted(): return lax.ppermute(block, axis, route)  55.1 us
    dot_general x39, matrix products, compute(): jnp.einsum('fqhc,fkhc->fhqk', query, key_tile[0], preferred_element_type=...  14.2 us
    unnamed x124, local copies, waits for them, and re-layouts  12.5 us
    dot_general x39, matrix products, product(): jnp.einsum('fhqk,fkhc->fqhc', portion, value_tile, preferred_element_type...  9.39 us
  transfers between devices with their start and end apart: 6, of which 3 were waited for; matrix products, arithmetic and copies ran while one was open for 4% of the time, Pallas kernels for 0%

commit v1 on v0

--- a/solution.py
+++ b/solution.py
@@ -33,35 +33,39 @@
     return best
 
 
+def swap_cores(block):
+    devices = range(lax.axis_size("space"))
+    return lax.ppermute(block, "space", [(i, i ^ 1) for i in devices])
+
+
 def fetch_rows_first(stacked):
     frame_count = stacked.shape[1]
-    nearby = {0: stacked}
-    for e in range(-W, W + 1):
-        if e != 0:
-            nearby[e] = shifted(stacked, "space", -e)
-    ordered = [e for e in range(-W, W + 1) if frame_reach(e) > 0]
-    sent_forward = jnp.concatenate(
-        [nearby[e][:, frame_count - frame_reach(e) :] for e in ordered], axis=1
-    )
-    sent_backward = jnp.concatenate([nearby[e][:, : frame_reach(e)] for e in ordered], axis=1)
-    earlier = shifted(sent_forward, "tm", 1)
-    following = shifted(sent_backward, "tm", -1)
+    earlier = shifted(stacked[:, frame_count - TR :], "tm", 1)
+    following = shifted(stacked[:, :TR], "tm", -1)
+    far_next = shifted(stacked, "space", -2)
+    far_prev = shifted(stacked, "space", 2)
+    core_zero = lax.axis_index("space") % 2 == 0
+    partner_own = swap_cores(stacked)
+    partner_far = swap_cores(jnp.where(core_zero, far_next, far_prev))
+    nearby = {
+        0: stacked,
+        2: far_next,
+        -2: far_prev,
+        1: jnp.where(core_zero, partner_own, partner_far),
+        -1: jnp.where(core_zero, partner_far, partner_own),
+    }
+    band = jnp.concatenate([earlier[:, TR - 1 :], following[:, :1]], axis=1)
+    diagonal = {1: shifted(band, "space", -1), -1: shifted(band, "space", 1)}
     columns = {}
-    position = 0
     for e in range(-W, W + 1):
         extent = frame_reach(e)
-        if extent > 0:
-            columns[e] = jnp.concatenate(
-                [
-                    earlier[:, position : position + extent],
-                    nearby[e],
-                    following[:, position : position + extent],
-                ],
-                axis=1,
-            )
-            position = position + extent
+        if e == 0:
+            parts = [earlier, nearby[0], following]
+        elif extent > 0:
+            parts = [diagonal[e][:, :1], nearby[e], diagonal[e][:, 1:]]
         else:
-            columns[e] = nearby[e]
+            parts = [nearby[e]]
+        columns[e] = jnp.concatenate(parts, axis=1)
     return columns
 
 

time: 453 us -> 299 us (0.66)
  the two profiles are of different devices: /device:TPU:329 before, /device:TPU:297 now
where the time goes in v1:
time: 299 us; the launch traced here: 298 us
  waiting for transfers between devices  161 us (54%)
  starting transfers between devices  60.8 us (20%)
  matrix products  29.9 us (10%)
  local copies, waits for them, and re-layouts  24.4 us (8%)
  other arithmetic  20.3 us (7%)
    ppermute x6, waiting for transfers between devices, shifted(): return lax.ppermute(block, axis, route)  161 us
    ppermute x6, starting transfers between devices, shifted(): return lax.ppermute(block, axis, route)  55.6 us
    dot_general x39, matrix products, compute(): jnp.einsum('fqhc,fkhc->fhqk', query, key_tile[0], preferred_element_type=...  20 us
    dot_general x39, matrix products, product(): jnp.einsum('fhqk,fkhc->fqhc', portion, value_tile, preferred_element_type...  9.96 us
    slice x6, other arithmetic, attend(): value_list.append(key_tile[1])  9.28 us
    unnamed x108, local copies, waits for them, and re-layouts  9.22 us
  transfers between devices with their start and end apart: 8, of which 2 were waited for; matrix products, arithmetic and copies ran while one was open for 12% of the time, Pallas kernels for 0%

profile of v1, /device:TPU:297, one launch (start us, length us, event | category | flops | bytes accessed | tf_op | source)
XLA Modules:
  0.0 297.6 jit_solution(2473655670791658926)
XLA Ops:
  0.0 1.6 copy.93
  2.0 1.3 pad_maximum_fusion
  3.3 2.6 collective-permute-start.3
  5.9 2.6 collective-permute-start.4
  8.6 3.1 %collective-permute-start.6 = (bf16[2,2,128,1536]{2,3,1,0:T(8,128)(2,1)}, bf16[2,2,128,1536]{2,3,1,0:T(8,128)(2,1)}, u32[]{:S(2)}, u32[]{:S(2)}) collective-permute-start(bf16[2,2,128,1536]{2,3,1,0:T(8,128)(2,1)} %pad_maximum_fusion), channel_id=1, source_target_pairs={{0,1},{1,0},{2,3},{3,2},{4,5},{5,4},{6,7},{7,6},{8,9},{9,8},{10,11... | collective-permute-start | bytes 4718600 | tf_op jit(solution)/shard_map/ppermute | solution.py:38
  11.7 3.1 %collective-permute-start = (bf16[2,2,128,1536]{2,3,1,0:T(8,128)(2,1)}, bf16[2,2,128,1536]{2,3,1,0:T(8,128)(2,1)}, u32[]{:S(2)}, u32[]{:S(2)}) collective-permute-start(bf16[2,2,128,1536]{2,3,1,0:T(8,128)(2,1)} %pad_maximum_fusion), channel_id=1, source_target_pairs={{0,32},{32,64},{64,96},{96,128},{128,160},{160,192},{192,224},{224... | collective-permute-start | bytes 4718600 | tf_op jit(solution)/shard_map/ppermute | solution.py:16
  14.9 8.2 %collective-permute-start.1 = (bf16[2,2,128,1536]{2,3,1,0:T(8,128)(2,1)}, bf16[2,2,128,1536]{2,3,1,0:T(8,128)(2,1)}, u32[]{:S(2)}, u32[]{:S(2)}) collective-permute-start(bf16[2,2,128,1536]{2,3,1,0:T(8,128)(2,1)} %pad_maximum_fusion), channel_id=1, source_target_pairs={{32,0},{64,32},{96,64},{128,96},{160,128},{192,160},{224,192},{256... | collective-permute-start | bytes 4718600 | tf_op jit(solution)/shard_map/ppermute | solution.py:16
  24.2 0.9 fusion.288
  25.9 154.8 %collective-permute-done = bf16[2,2,128,1536]{2,3,1,0:T(8,128)(2,1)} collective-permute-done((bf16[2,2,128,1536]{2,3,1,0:T(8,128)(2,1)}, bf16[2,2,128,1536]{2,3,1,0:T(8,128)(2,1)}, u32[]{:S(2)}, u32[]{:S(2)}) %collective-permute-start) | collective-permute-done | bytes 1572896 | tf_op jit(solution)/shard_map/ppermute | solution.py:16
  180.7 1.2 slice.649
  181.9 1.2 slice.650
  183.3 37.1 %collective-permute-start.2 = (bf16[2,2,128,1536]{2,3,1,0:T(8,128)(2,1)S(1)}, bf16[2,2,128,1536]{2,3,1,0:T(8,128)(2,1)S(1)}, u32[]{:S(2)}, u32[]{:S(2)}) collective-permute-start(bf16[2,2,128,1536]{2,3,1,0:T(8,128)(2,1)S(1)} %pad_maximum_fusion.1), channel_id=1, source_target_pairs={{0,1},{1,2},{2,3},{3,4},{4,5},{5,6},{6,7},{7,8},{8,9},{9,10},{10,1... | collective-permute-start | bytes 4718600 | tf_op jit(solution)/shard_map/ppermute | solution.py:16
  220.3 1.9 collective-permute-start.7
  222.3 1.6 broadcast_select_fusion.2
  223.9 2.1 collective-permute-start.5
  226.0 2.2 pad_maximum_fusion.33
  228.5 1.1 fusion.314
  229.6 2.2 pad_maximum_fusion.30
  232.1 1.1 fusion.306
  233.2 2.3 fusion.283
  235.8 1.1 fusion.308
  236.9 2.3 fusion.282
  239.5 1.1 fusion.312
  240.6 2.1 fusion.285
  242.9 1.1 fusion.304
  244.0 2.2 fusion.284
  246.5 1.1 fusion.315
  248.5 1.1 fusion.299
  249.6 1.1 fusion.291
  250.6 1.1 fusion.302
  251.7 6.3 %collective-permute-done.7 = bf16[2,2,128,1536]{2,3,1,0:T(8,128)(2,1)S(1)} collective-permute-done((bf16[2,2,128,1536]{2,3,1,0:T(8,128)(2,1)S(1)}, bf16[2,2,128,1536]{2,3,1,0:T(8,128)(2,1)S(1)}, u32[]{:S(2)}, u32[]{:S(2)}) %collective-permute-start.7) | collective-permute-done | bytes 1572896 | tf_op jit(solution)/shard_map/ppermute | solution.py:16
  258.2 1.6 broadcast_select_fusion.1
  259.8 1.1 pad_maximum_fusion.29
  260.9 1.4 pad_maximum_fusion.32
  262.4 1.4 pad_maximum_fusion.34
  263.7 1.0 pad_maximum_fusion.31
  268.7 1.7 fusion.116
  271.1 1.0 fusion.113
  272.1 1.8 copy.222
  274.0 1.5 fusion.311
  281.4 1.6 fusion.142
  283.3 0.7 copy-done.23
  285.3 0.8 copy.223
  291.1 0.5 copy-done
  292.1 1.6 fusion.168
  294.0 0.7 copy-done.16
  296.1 0.5 copy-done.40
  296.6 0.9 pad_maximum_fusion.2
  (189 shorter events, 24.1 us)
Async XLA Ops:
  0.0 1.6 copy-start.48
  2.0 21.1 %copy-start.50 = (s32[2,1,5,5]{3,1,2,0:T(1,128)S(1)}, s32[2,1,5,5]{3,1,2,0:T(1,128)}, u32[]{:S(2)}) copy-start(s32[2,1,5,5]{3,1,2,0:T(1,128)} %param.7) | copy-start | bytes 604
  2.0 21.1 %copy-start.49 = (bf16[2,128,1536]{2,1,0:T(8,128)(2,1)S(1)}, bf16[2,128,1536]{2,1,0:T(8,128)(2,1)}, u32[]{:S(2)}) copy-start(bf16[2,128,1536]{2,1,0:T(8,128)(2,1)} %param.4) | copy-start | bytes 2359300
  3.3 219.0 %collective-permute-start.3 = (bf16[2,2,128,1536]{2,3,1,0:T(8,128)(2,1)}, bf16[2,2,128,1536]{2,3,1,0:T(8,128)(2,1)}, u32[]{:S(2)}, u32[]{:S(2)}) collective-permute-start(bf16[2,2,128,1536]{2,3,1,0:T(8,128)(2,1)} %pad_maximum_fusion), channel_id=1, source_target_pairs={{2,0},{3,1},{4,2},{5,3},{6,4},{7,5},{8,6},{9,7},{10,8},{11,9},{12,... | collective-permute-start | bytes 4718600 | tf_op jit(solution)/shard_map/ppermute | solution.py:16
  5.9 216.4 %collective-permute-start.4 = (bf16[2,2,128,1536]{2,3,1,0:T(8,128)(2,1)}, bf16[2,2,128,1536]{2,3,1,0:T(8,128)(2,1)}, u32[]{:S(2)}, u32[]{:S(2)}) collective-permute-start(bf16[2,2,128,1536]{2,3,1,0:T(8,128)(2,1)} %pad_maximum_fusion), channel_id=1, source_target_pairs={{0,2},{1,3},{2,4},{3,5},{4,6},{5,7},{6,8},{7,9},{8,10},{9,11},{10,... | collective-permute-start | bytes 4718600 | tf_op jit(solution)/shard_map/ppermute | solution.py:16
  8.6 249.6 %collective-permute-start.6 = (bf16[2,2,128,1536]{2,3,1,0:T(8,128)(2,1)}, bf16[2,2,128,1536]{2,3,1,0:T(8,128)(2,1)}, u32[]{:S(2)}, u32[]{:S(2)}) collective-permute-start(bf16[2,2,128,1536]{2,3,1,0:T(8,128)(2,1)} %pad_maximum_fusion), channel_id=1, source_target_pairs={{0,1},{1,0},{2,3},{3,2},{4,5},{5,4},{6,7},{7,6},{8,9},{9,8},{10,11... | collective-permute-start | bytes 4718600 | tf_op jit(solution)/shard_map/ppermute | solution.py:38
  11.7 169.0 %collective-permute-start = (bf16[2,2,128,1536]{2,3,1,0:T(8,128)(2,1)}, bf16[2,2,128,1536]{2,3,1,0:T(8,128)(2,1)}, u32[]{:S(2)}, u32[]{:S(2)}) collective-permute-start(bf16[2,2,128,1536]{2,3,1,0:T(8,128)(2,1)} %pad_maximum_fusion), channel_id=1, source_target_pairs={{0,32},{32,64},{64,96},{96,128},{128,160},{160,192},{192,224},{224... | collective-permute-start | bytes 4718600 | tf_op jit(solution)/shard_map/ppermute | solution.py:16
  14.9 167.1 %collective-permute-start.1 = (bf16[2,2,128,1536]{2,3,1,0:T(8,128)(2,1)}, bf16[2,2,128,1536]{2,3,1,0:T(8,128)(2,1)}, u32[]{:S(2)}, u32[]{:S(2)}) collective-permute-start(bf16[2,2,128,1536]{2,3,1,0:T(8,128)(2,1)} %pad_maximum_fusion), channel_id=1, source_target_pairs={{32,0},{64,32},{96,64},{128,96},{160,128},{192,160},{224,192},{256... | collective-permute-start | bytes 4718600 | tf_op jit(solution)/shard_map/ppermute | solution.py:16
  183.3 79.0 %collective-permute-start.2 = (bf16[2,2,128,1536]{2,3,1,0:T(8,128)(2,1)S(1)}, bf16[2,2,128,1536]{2,3,1,0:T(8,128)(2,1)S(1)}, u32[]{:S(2)}, u32[]{:S(2)}) collective-permute-start(bf16[2,2,128,1536]{2,3,1,0:T(8,128)(2,1)S(1)} %pad_maximum_fusion.1), channel_id=1, source_target_pairs={{0,1},{1,2},{2,3},{3,4},{4,5},{5,6},{6,7},{7,8},{8,9},{9,10},{10,1... | collective-permute-start | bytes 4718600 | tf_op jit(solution)/shard_map/ppermute | solution.py:16
  220.3 37.7 %collective-permute-start.7 = (bf16[2,2,128,1536]{2,3,1,0:T(8,128)(2,1)S(1)}, bf16[2,2,128,1536]{2,3,1,0:T(8,128)(2,1)S(1)}, u32[]{:S(2)}, u32[]{:S(2)}) collective-permute-start(bf16[2,2,128,1536]{2,3,1,0:T(8,128)(2,1)S(1)} %pad_maximum_fusion.1), channel_id=1, source_target_pairs={{1,0},{2,1},{3,2},{4,3},{5,4},{6,5},{7,6},{8,7},{9,8},{10,9},{11,1... | collective-permute-start | bytes 4718600 | tf_op jit(solution)/shard_map/ppermute | solution.py:16
  223.9 34.3 %collective-permute-start.5 = (bf16[2,2,128,1536]{2,3,1,0:T(8,128)(2,1)S(1)}, bf16[2,2,128,1536]{2,3,1,0:T(8,128)(2,1)S(1)}, u32[]{:S(2)}, u32[]{:S(2)}) collective-permute-start(bf16[2,2,128,1536]{2,3,1,0:T(8,128)(2,1)S(1)} %broadcast_select_fusion.2), channel_id=1, source_target_pairs={{0,1},{1,0},{2,3},{3,2},{4,5},{5,4},{6,7},{7,6},{8,9},{9,8},{10,11... | collective-permute-start | bytes 4718600 | tf_op jit(solution)/shard_map/ppermute | solution.py:38
  272.1 3.4 %copy-start.15 = (bf16[1,2,128,512]{2,3,1,0:T(8,128)(2,1)S(1)}, bf16[1,2,128,512]{2,3,1,0:T(8,128)(2,1)}, u32[]{:S(2)}) copy-start(bf16[1,2,128,512]{2,3,1,0:T(8,128)(2,1)} %get-tuple-element.74) | copy-start | bytes 786436
  274.0 1.8 copy-start.39
  274.0 2.2 copy-start.38
  276.1 1.0 copy-start.12
  276.5 1.1 copy-start.1
  276.5 1.1 copy-start.24
  277.1 1.0 copy-start.31
  277.4 1.0 copy-start.11
  277.8 1.1 copy-start.3
  277.9 1.1 copy-start.27
  278.4 1.0 copy-start.45
  278.7 1.1 copy-start.2
  278.7 1.2 copy-start.25
  279.2 1.0 copy-start.30
  279.6 1.1 copy-start.4
  279.6 1.2 copy-start.28
  280.1 1.1 copy-start.7
  280.1 1.3 copy-start.8
  281.4 1.7 copy-start.43
  284.9 1.2 copy-start.14
  285.3 1.2 copy-start.13
  285.3 1.5 copy-start.36
  286.1 1.0 copy-start.35
  286.4 1.0 copy-start.34
  286.8 1.0 copy-start.46
  287.1 1.0 copy-start.10
  287.4 1.0 copy-start.19
  288.3 1.0 copy-start.9
  288.7 1.0 copy-start.20
  289.6 1.0 copy-start.18
  289.9 1.0 copy-start.22
  290.5 1.1 copy-start
  290.5 1.1 copy-start.17
  290.8 1.1 copy-start.5
  290.8 1.3 copy-start.6
  292.1 1.6 copy-start.42
  295.6 1.0 copy-start.41
  (11 other events, 10.6 us)

commit v2 on v1

v2 whole, which is shorter than its diff:
```python
import math

import jax
import jax.numpy as jnp
from jax import lax
from jax.experimental import pallas as pl
from jax.experimental.pallas import tpu as pltpu
from jax.sharding import PartitionSpec as P

HD = 128
TR = 2
W = 2


def shifted(block, axis, distance):
    devices = range(lax.axis_size(axis))
    route = [(i - distance, i) for i in devices if i - distance in devices]
    return lax.ppermute(block, axis, route)


def band_list():
    pairs = []
    for d in range(-TR, TR + 1):
        spread = W >> abs(d)
        for e in range(-spread, spread + 1):
            pairs.append((d, e))
    return pairs


def frame_reach(e):
    best = 0
    for d in range(TR + 1):
        if W >> d >= abs(e):
            best = d
    return best


def swap_cores(block):
    devices = range(lax.axis_size("space"))
    return lax.ppermute(block, "space", [(i, i ^ 1) for i in devices])


def fetch_sources(stacked):
    frame_count = stacked.shape[1]
    earlier = shifted(stacked[:, frame_count - TR :], "tm", 1)
    following = shifted(stacked[:, :TR], "tm", -1)
    far_next = shifted(stacked, "space", -2)
    far_prev = shifted(stacked, "space", 2)
    core_zero = lax.axis_index("space") % 2 == 0
    partner_own = swap_cores(stacked)
    partner_far = swap_cores(jnp.where(core_zero, far_next, far_prev))
    near_next = jnp.where(core_zero, partner_own, partner_far)
    near_prev = jnp.where(core_zero, partner_far, partner_own)
    band = jnp.concatenate([earlier[:, TR - 1 :], following[:, :1]], axis=1)
    diag_next = shifted(band, "space", -1)
    diag_prev = shifted(band, "space", 1)
    return (stacked, earlier, following, far_next, far_prev, near_next, near_prev, diag_next, diag_prev)


def locate(frame, d, e):
    offset = frame + d
    if e == 0:
        if offset < 0:
            return 1, offset + TR
        if offset < 2:
            return 0, offset
        return 2, offset - 2
    if abs(e) == 1:
        near, diag = (5, 7) if e > 0 else (6, 8)
        if offset < 0:
            return diag, 0
        if offset < 2:
            return near, offset
        return diag, 1
    return (3 if e > 0 else 4), frame


def attention_kernel(flags_ref, q_ref, *refs):
    *sources, o_ref = refs
    frame_count = q_ref.shape[0]
    score_scale = 1.0 / math.sqrt(HD)
    for frame in range(frame_count):
        query = q_ref[frame]
        score_list = []
        value_list = []
        for d, e in band_list():
            which, index = locate(frame, d, e)
            key_tile = sources[which][0, index]
            raw = (
                lax.dot_general(
                    query, key_tile, (((1,), (1,)), ((), ())), preferred_element_type=jnp.float32
                )
                * score_scale
            )
            flag = flags_ref[frame * 25 + (TR + d) * 5 + (W + e)]
            score_list.append(jnp.where(flag > 0, raw, -jnp.inf))
            value_list.append(sources[which][1, index])
        row_max = jnp.max(score_list[0], axis=1, keepdims=True)
        for scores in score_list[1:]:
            row_max = jnp.maximum(row_max, jnp.max(scores, axis=1, keepdims=True))
        denominator = jnp.zeros_like(row_max)
        summed = jnp.zeros((query.shape[0], HD), jnp.float32)
        for scores, value_tile in zip(score_list, value_list):
            weights = jnp.exp(scores - row_max)
            denominator = denominator + jnp.sum(weights, axis=1, keepdims=True)
            summed = summed + jnp.dot(
                weights.astype(jnp.bfloat16), value_tile, preferred_element_type=jnp.float32
            )
        o_ref[frame] = (summed / denominator).astype(o_ref.dtype)


def attend(queries, sources, tile_flags):
    frame_count, row_count, feature_width = queries.shape
    head_count = feature_width // HD
    flags = tile_flags.reshape(-1).astype(jnp.int32)
    source_spec = pl.BlockSpec((2, 2, row_count, HD), lambda h, flags: (0, 0, 0, h))
    tile_spec = pl.BlockSpec((frame_count, row_count, HD), lambda h, flags: (0, 0, h))
    grid_spec = pltpu.PrefetchScalarGridSpec(
        num_scalar_prefetch=1,
        grid=(head_count,),
        in_specs=[tile_spec] + [source_spec] * len(sources),
        out_specs=tile_spec,
    )
    pairs = len(band_list())
    cost = pl.CostEstimate(
        flops=4 * frame_count * head_count * pairs * row_count * row_count * HD,
        transcendentals=frame_count * head_count * pairs * row_count * row_count,
        bytes_accessed=(2 + 4 * len(sources)) * frame_count * row_count * feature_width,
    )
    return pl.pallas_call(
        attention_kernel,
        grid_spec=grid_spec,
        out_shape=jax.ShapeDtypeStruct(queries.shape, queries.dtype),
        cost_estimate=cost,
    )(flags, queries, *sources)


def on_device(queries, keys, values, tile_mask):
    stacked = jnp.stack([keys, values], 0)
    sources = fetch_sources(stacked)
    tile_flags = tile_mask[:, 0]
    return attend(queries, sources, tile_flags)


def solution(mesh):
    in_specs = (
        P("tm", "space", None),
        P("tm", "space", None),
        P("tm", "space", None),
        P("tm", "space", None, None),
    )
    out_specs = P("tm", "space", None)
    return jax.shard_map(
        on_device, mesh=mesh, in_specs=in_specs, out_specs=out_specs, check_vma=False
    )
```

time: 299 us -> 283 us (0.946)
  the two profiles are of different devices: /device:TPU:297 before, /device:TPU:30 now
where the time goes in v2:
time: 283 us; the launch traced here: 282 us
  starting transfers between devices  134 us (47%)
  waiting for transfers between devices  113 us (40%)
  Pallas kernels  21.4 us (8%)
  other arithmetic  9.36 us (3%)
  local copies, waits for them, and re-layouts  4.29 us (2%)
    ppermute x6, starting transfers between devices, shifted(): return lax.ppermute(block, axis, route)  130 us
    ppermute x6, waiting for transfers between devices, shifted(): return lax.ppermute(block, axis, route)  113 us
    pallas_call x1, Pallas kernels, attend(): pl.pallas_call(attention_kernel, grid_spec=grid_spec, out_shape=jax.Shape...  21.4 us
  transfers between devices with their start and end apart: 8, of which 5 were waited for; matrix products, arithmetic and copies ran while one was open for 3% of the time, Pallas kernels for 0%

profile of v2, /device:TPU:30, one launch (start us, length us, event | category | flops | bytes accessed | tf_op | source)
XLA Modules:
  0.0 282.3 jit_solution(10220109340439530382)
XLA Ops:
  0.0 2.7 pad_maximum_fusion.refs_0_
  2.7 6.7 %collective-permute-start.2 = (bf16[2,2,128,1536]{3,2,1,0:T(8,128)(2,1)}, bf16[2,2,128,1536]{3,2,1,0:T(8,128)(2,1)S(1)}, u32[]{:S(2)}, u32[]{:S(2)}) collective-permute-start(bf16[2,2,128,1536]{3,2,1,0:T(8,128)(2,1)} %pad_maximum_fusion.refs_0_), channel_id=1, source_target_pairs={{2,0},{3,1},{4,2},{5,3},{6,4},{7,5},{8,6},{9,7},{10,8},{11,9},{12,... | collective-permute-start | bytes 4718600 | tf_op jit(solution)/shard_map/ppermute | solution.py:18
  9.4 1.9 collective-permute-start.3
  11.3 9.0 %collective-permute-start = (bf16[2,2,128,1536]{3,2,1,0:T(8,128)(2,1)}, bf16[2,2,128,1536]{3,2,1,0:T(8,128)(2,1)}, u32[]{:S(2)}, u32[]{:S(2)}) collective-permute-start(bf16[2,2,128,1536]{3,2,1,0:T(8,128)(2,1)} %pad_maximum_fusion.refs_0_), channel_id=1, source_target_pairs={{0,32},{32,64},{64,96},{96,128},{128,160},{160,192},{192,224},{224... | collective-permute-start | bytes 4718600 | tf_op jit(solution)/shard_map/ppermute | solution.py:18
  20.3 1.9 collective-permute-start.1
  22.3 1.9 collective-permute-start.4
  24.2 20.3 %collective-permute-done.2.refs_3_ = bf16[2,2,128,1536]{3,2,1,0:T(8,128)(2,1)S(1)} collective-permute-done((bf16[2,2,128,1536]{3,2,1,0:T(8,128)(2,1)}, bf16[2,2,128,1536]{3,2,1,0:T(8,128)(2,1)S(1)}, u32[]{:S(2)}, u32[]{:S(2)}) %collective-permute-start.2) | collective-permute-done | bytes 1572896 | tf_op jit(solution)/shard_map/ppermute | solution.py:18
  44.5 0.0 copy-start
  44.5 33.7 %collective-permute-done.3.refs_4_ = bf16[2,2,128,1536]{3,2,1,0:T(8,128)(2,1)S(1)} collective-permute-done((bf16[2,2,128,1536]{3,2,1,0:T(8,128)(2,1)}, bf16[2,2,128,1536]{3,2,1,0:T(8,128)(2,1)S(1)}, u32[]{:S(2)}, u32[]{:S(2)}) %collective-permute-start.3) | collective-permute-done | bytes 1572896 | tf_op jit(solution)/shard_map/ppermute | solution.py:18
  78.2 0.0 copy-start.1
  78.2 1.5 broadcast_select_fusion.2
  79.7 0.0 copy-done
  79.7 0.1 copy-done.1
  79.8 1.9 collective-permute-start.5
  81.8 29.1 %collective-permute-done.refs_1_ = bf16[2,2,128,1536]{3,2,1,0:T(8,128)(2,1)} collective-permute-done((bf16[2,2,128,1536]{3,2,1,0:T(8,128)(2,1)}, bf16[2,2,128,1536]{3,2,1,0:T(8,128)(2,1)}, u32[]{:S(2)}, u32[]{:S(2)}) %collective-permute-start) | collective-permute-done | bytes 1572896 | tf_op jit(solution)/shard_map/ppermute | solution.py:18
  110.8 1.2 slice.8
  112.0 0.0 collective-permute-done.1.refs_2_
  112.0 1.2 slice.9
  113.2 0.0 copy-start.4
  113.2 1.3 pad_maximum_fusion.1
  114.5 108.5 %collective-permute-start.6 = (bf16[2,2,128,1536]{3,2,1,0:T(8,128)(2,1)}, bf16[2,2,128,1536]{3,2,1,0:T(8,128)(2,1)S(1)}, u32[]{:S(2)}, u32[]{:S(2)}) collective-permute-start(bf16[2,2,128,1536]{3,2,1,0:T(8,128)(2,1)} %pad_maximum_fusion.1), channel_id=1, source_target_pairs={{1,0},{2,1},{3,2},{4,3},{5,4},{6,5},{7,6},{8,7},{9,8},{10,9},{11,1... | collective-permute-start | bytes 4718600 | tf_op jit(solution)/shard_map/ppermute | solution.py:18
  223.0 1.9 collective-permute-start.7
  224.9 0.0 copy-done.4
  225.0 0.6 reshape_squeeze.3.flags_ref
  225.6 0.0 collective-permute-done.4
  225.6 0.0 collective-permute-done.5
  225.6 3.9 %broadcast_select_fusion = (bf16[2,2,128,1536]{3,2,1,0:T(8,128)(2,1)}, bf16[2,2,128,1536]{3,2,1,0:T(8,128)(2,1)}) fusion(bf16[2,2,128,1536]{3,2,1,0:T(8,128)(2,1)} %collective-permute-done.5, bf16[2,2,128,1536]{3,2,1,0:T(8,128)(2,1)} %collective-permute-done.4, pred[]{:T(512)S(6)} %eq.5), kind=kLoop, calls=%fused_computation.2 | loop fusion | flops 1572864 | bytes 6291457 | tf_op jit(solution)/shard_map/jit(_where)/select_n | solution.py:53
  229.4 11.8 %collective-permute-done.6.refs_7_ = bf16[2,2,128,1536]{3,2,1,0:T(8,128)(2,1)S(1)} collective-permute-done((bf16[2,2,128,1536]{3,2,1,0:T(8,128)(2,1)}, bf16[2,2,128,1536]{3,2,1,0:T(8,128)(2,1)S(1)}, u32[]{:S(2)}, u32[]{:S(2)}) %collective-permute-start.6) | collective-permute-done | bytes 1572896 | tf_op jit(solution)/shard_map/ppermute | solution.py:18
  241.2 0.0 copy-start.2
  241.2 18.5 %collective-permute-done.7.refs_8_ = bf16[2,2,128,1536]{3,2,1,0:T(8,128)(2,1)S(1)} collective-permute-done((bf16[2,2,128,1536]{3,2,1,0:T(8,128)(2,1)}, bf16[2,2,128,1536]{3,2,1,0:T(8,128)(2,1)S(1)}, u32[]{:S(2)}, u32[]{:S(2)}) %collective-permute-start.7) | collective-permute-done | bytes 1572896 | tf_op jit(solution)/shard_map/ppermute | solution.py:18
  259.7 0.0 copy-start.3
  259.7 0.0 copy-done.2
  259.7 1.2 copy-done.3
  260.9 21.4 %shard_map.46 = bf16[2,128,1536]{2,1,0:T(8,128)(2,1)} custom-call(s32[50]{0:T(128)} %reshape_squeeze.3.flags_ref, bf16[2,128,1536]{2,1,0:T(8,128)(2,1)} %q_ref.1, bf16[2,2,128,1536]{3,2,1,0:T(8,128)(2,1)} %pad_maximum_fusion.refs_0_, bf16[2,2,128,1536]{3,2,1,0:T(8,128)(2,1)} %collective-permute-done.refs_1_, ...), custom_call_target="tpu_custom_call" | custom-call | flops 2617245696 | bytes 14942208 | tf_op jit(solution)/shard_map/pallas_call | solution.py:130
  (1 shorter events, 0.0 us)
Async XLA Ops:
  2.7 41.8 %collective-permute-start.2 = (bf16[2,2,128,1536]{3,2,1,0:T(8,128)(2,1)}, bf16[2,2,128,1536]{3,2,1,0:T(8,128)(2,1)S(1)}, u32[]{:S(2)}, u32[]{:S(2)}) collective-permute-start(bf16[2,2,128,1536]{3,2,1,0:T(8,128)(2,1)} %pad_maximum_fusion.refs_0_), channel_id=1, source_target_pairs={{2,0},{3,1},{4,2},{5,3},{6,4},{7,5},{8,6},{9,7},{10,8},{11,9},{12,... | collective-permute-start | bytes 4718600 | tf_op jit(solution)/shard_map/ppermute | solution.py:18
  9.4 68.8 %collective-permute-start.3 = (bf16[2,2,128,1536]{3,2,1,0:T(8,128)(2,1)}, bf16[2,2,128,1536]{3,2,1,0:T(8,128)(2,1)S(1)}, u32[]{:S(2)}, u32[]{:S(2)}) collective-permute-start(bf16[2,2,128,1536]{3,2,1,0:T(8,128)(2,1)} %pad_maximum_fusion.refs_0_), channel_id=1, source_target_pairs={{0,2},{1,3},{2,4},{3,5},{4,6},{5,7},{6,8},{7,9},{8,10},{9,11},{10,... | collective-permute-start | bytes 4718600 | tf_op jit(solution)/shard_map/ppermute | solution.py:18
  11.3 99.5 %collective-permute-start = (bf16[2,2,128,1536]{3,2,1,0:T(8,128)(2,1)}, bf16[2,2,128,1536]{3,2,1,0:T(8,128)(2,1)}, u32[]{:S(2)}, u32[]{:S(2)}) collective-permute-start(bf16[2,2,128,1536]{3,2,1,0:T(8,128)(2,1)} %pad_maximum_fusion.refs_0_), channel_id=1, source_target_pairs={{0,32},{32,64},{64,96},{96,128},{128,160},{160,192},{192,224},{224... | collective-permute-start | bytes 4718600 | tf_op jit(solution)/shard_map/ppermute | solution.py:18
  20.3 91.7 %collective-permute-start.1 = (bf16[2,2,128,1536]{3,2,1,0:T(8,128)(2,1)}, bf16[2,2,128,1536]{3,2,1,0:T(8,128)(2,1)}, u32[]{:S(2)}, u32[]{:S(2)}) collective-permute-start(bf16[2,2,128,1536]{3,2,1,0:T(8,128)(2,1)} %pad_maximum_fusion.refs_0_), channel_id=1, source_target_pairs={{32,0},{64,32},{96,64},{128,96},{160,128},{192,160},{224,192},{256... | collective-permute-start | bytes 4718600 | tf_op jit(solution)/shard_map/ppermute | solution.py:18
  22.3 203.3 %collective-permute-start.4 = (bf16[2,2,128,1536]{3,2,1,0:T(8,128)(2,1)}, bf16[2,2,128,1536]{3,2,1,0:T(8,128)(2,1)}, u32[]{:S(2)}, u32[]{:S(2)}) collective-permute-start(bf16[2,2,128,1536]{3,2,1,0:T(8,128)(2,1)} %pad_maximum_fusion.refs_0_), channel_id=1, source_target_pairs={{0,1},{1,0},{2,3},{3,2},{4,5},{5,4},{6,7},{7,6},{8,9},{9,8},{10,11... | collective-permute-start | bytes 4718600 | tf_op jit(solution)/shard_map/ppermute | solution.py:40
  44.5 35.2 %copy-start = (bf16[2,2,128,1536]{3,2,1,0:T(8,128)(2,1)}, bf16[2,2,128,1536]{3,2,1,0:T(8,128)(2,1)S(1)}, u32[]{:S(2)}) copy-start(bf16[2,2,128,1536]{3,2,1,0:T(8,128)(2,1)S(1)} %collective-permute-done.2.refs_3_) | copy-start | bytes 4718596
  78.2 1.7 copy-start.1
  79.8 145.7 %collective-permute-start.5 = (bf16[2,2,128,1536]{3,2,1,0:T(8,128)(2,1)}, bf16[2,2,128,1536]{3,2,1,0:T(8,128)(2,1)}, u32[]{:S(2)}, u32[]{:S(2)}) collective-permute-start(bf16[2,2,128,1536]{3,2,1,0:T(8,128)(2,1)} %broadcast_select_fusion.2), channel_id=1, source_target_pairs={{0,1},{1,0},{2,3},{3,2},{4,5},{5,4},{6,7},{7,6},{8,9},{9,8},{10,11... | collective-permute-start | bytes 4718600 | tf_op jit(solution)/shard_map/ppermute | solution.py:40
  113.2 111.7 %copy-start.4 = (s32[2,1,5,5]{3,1,2,0:T(1,128)S(1)}, s32[2,1,5,5]{3,1,2,0:T(1,128)}, u32[]{:S(2)}) copy-start(s32[2,1,5,5]{3,1,2,0:T(1,128)} %param.7) | copy-start | bytes 604
  114.5 126.7 %collective-permute-start.6 = (bf16[2,2,128,1536]{3,2,1,0:T(8,128)(2,1)}, bf16[2,2,128,1536]{3,2,1,0:T(8,128)(2,1)S(1)}, u32[]{:S(2)}, u32[]{:S(2)}) collective-permute-start(bf16[2,2,128,1536]{3,2,1,0:T(8,128)(2,1)} %pad_maximum_fusion.1), channel_id=1, source_target_pairs={{1,0},{2,1},{3,2},{4,3},{5,4},{6,5},{7,6},{8,7},{9,8},{10,9},{11,1... | collective-permute-start | bytes 4718600 | tf_op jit(solution)/shard_map/ppermute | solution.py:18
  223.0 36.7 %collective-permute-start.7 = (bf16[2,2,128,1536]{3,2,1,0:T(8,128)(2,1)}, bf16[2,2,128,1536]{3,2,1,0:T(8,128)(2,1)S(1)}, u32[]{:S(2)}, u32[]{:S(2)}) collective-permute-start(bf16[2,2,128,1536]{3,2,1,0:T(8,128)(2,1)} %pad_maximum_fusion.1), channel_id=1, source_target_pairs={{0,1},{1,2},{2,3},{3,4},{4,5},{5,6},{6,7},{7,8},{8,9},{9,10},{10,1... | collective-permute-start | bytes 4718600 | tf_op jit(solution)/shard_map/ppermute | solution.py:18
  241.2 18.5 %copy-start.2 = (bf16[2,2,128,1536]{3,2,1,0:T(8,128)(2,1)}, bf16[2,2,128,1536]{3,2,1,0:T(8,128)(2,1)S(1)}, u32[]{:S(2)}) copy-start(bf16[2,2,128,1536]{3,2,1,0:T(8,128)(2,1)S(1)} %collective-permute-done.6.refs_7_) | copy-start | bytes 4718596
  259.7 1.2 copy-start.3

commit v3 on v2

--- a/solution.py
+++ b/solution.py
@@ -51,10 +51,17 @@
     partner_far = swap_cores(jnp.where(core_zero, far_next, far_prev))
     near_next = jnp.where(core_zero, partner_own, partner_far)
     near_prev = jnp.where(core_zero, partner_far, partner_own)
-    band = jnp.concatenate([earlier[:, TR - 1 :], following[:, :1]], axis=1)
-    diag_next = shifted(band, "space", -1)
-    diag_prev = shifted(band, "space", 1)
-    return (stacked, earlier, following, far_next, far_prev, near_next, near_prev, diag_next, diag_prev)
+    last, first = slice(frame_count - 1, frame_count), slice(0, 1)
+    diag_earlier = shifted(
+        jnp.concatenate([near_next[:, last], near_prev[:, last]], axis=1), "tm", 1
+    )
+    diag_following = shifted(
+        jnp.concatenate([near_next[:, first], near_prev[:, first]], axis=1), "tm", -1
+    )
+    return (
+        stacked, earlier, following, far_next, far_prev, near_next, near_prev, diag_earlier,
+        diag_following,
+    )
 
 
 def locate(frame, d, e):
@@ -66,12 +73,12 @@
             return 0, offset
         return 2, offset - 2
     if abs(e) == 1:
-        near, diag = (5, 7) if e > 0 else (6, 8)
+        side = 0 if e > 0 else 1
         if offset < 0:
-            return diag, 0
+            return 7, side
         if offset < 2:
-            return near, offset
-        return diag, 1
+            return 5 + side, offset
+        return 8, side
     return (3 if e > 0 else 4), frame
 
 

time: 283 us -> 396 us (1.40)
  the two profiles are of different devices: /device:TPU:30 before, /device:TPU:15 now
where the time goes in v3:
time: 396 us; the launch traced here: 395 us
  waiting for transfers between devices  259 us (65%)
  starting transfers between devices  102 us (26%)
  Pallas kernels  21.4 us (5%)
  other arithmetic  7.11 us (2%)
  local copies, waits for them, and re-layouts  5.67 us (1%)
    ppermute x6, waiting for transfers between devices, shifted(): return lax.ppermute(block, axis, route)  259 us
    ppermute x6, starting transfers between devices, shifted(): return lax.ppermute(block, axis, route)  96.1 us
    pallas_call x1, Pallas kernels, attend(): pl.pallas_call(attention_kernel, grid_spec=grid_spec, out_shape=jax.Shape...  21.4 us
  transfers between devices with their start and end apart: 8, of which 5 were waited for; matrix products, arithmetic and copies ran while one was open for 1% of the time, Pallas kernels for 0%

profile of v3, /device:TPU:15, one launch (start us, length us, event | category | flops | bytes accessed | tf_op | source)
XLA Modules:
  0.0 395.4 jit_solution(11845688439177581610)
XLA Ops:
  0.0 2.7 pad_maximum_fusion.refs_0_
  2.7 6.1 %collective-permute-start.2 = (bf16[2,2,128,1536]{3,2,1,0:T(8,128)(2,1)}, bf16[2,2,128,1536]{3,2,1,0:T(8,128)(2,1)S(1)}, u32[]{:S(2)}, u32[]{:S(2)}) collective-permute-start(bf16[2,2,128,1536]{3,2,1,0:T(8,128)(2,1)} %pad_maximum_fusion.refs_0_), channel_id=1, source_target_pairs={{2,0},{3,1},{4,2},{5,3},{6,4},{7,5},{8,6},{9,7},{10,8},{11,9},{12,... | collective-permute-start | bytes 4718600 | tf_op jit(solution)/shard_map/ppermute | solution.py:18
  8.8 1.9 collective-permute-start.3
  10.7 2.9 collective-permute-start.4
  13.6 28.7 %collective-permute-done.2.refs_3_ = bf16[2,2,128,1536]{3,2,1,0:T(8,128)(2,1)S(1)} collective-permute-done((bf16[2,2,128,1536]{3,2,1,0:T(8,128)(2,1)}, bf16[2,2,128,1536]{3,2,1,0:T(8,128)(2,1)S(1)}, u32[]{:S(2)}, u32[]{:S(2)}) %collective-permute-start.2) | collective-permute-done | bytes 1572896 | tf_op jit(solution)/shard_map/ppermute | solution.py:18
  42.3 0.0 copy-start.2
  42.3 34.4 %collective-permute-done.3.refs_4_ = bf16[2,2,128,1536]{3,2,1,0:T(8,128)(2,1)S(1)} collective-permute-done((bf16[2,2,128,1536]{3,2,1,0:T(8,128)(2,1)}, bf16[2,2,128,1536]{3,2,1,0:T(8,128)(2,1)S(1)}, u32[]{:S(2)}, u32[]{:S(2)}) %collective-permute-start.3) | collective-permute-done | bytes 1572896 | tf_op jit(solution)/shard_map/ppermute | solution.py:18
  76.7 0.0 copy-start.3
  76.7 0.2 broadcast_select_fusion.2
  76.9 0.0 copy-done.2
  76.9 1.0 copy-done.3
  77.9 3.2 collective-permute-start.5
  81.1 74.9 %collective-permute-start = (bf16[2,2,128,1536]{3,2,1,0:T(8,128)(2,1)}, bf16[2,2,128,1536]{3,2,1,0:T(8,128)(2,1)}, u32[]{:S(2)}, u32[]{:S(2)}) collective-permute-start(bf16[2,2,128,1536]{3,2,1,0:T(8,128)(2,1)} %pad_maximum_fusion.refs_0_), channel_id=1, source_target_pairs={{0,32},{32,64},{64,96},{96,128},{128,160},{160,192},{192,224},{224... | collective-permute-start | bytes 4718600 | tf_op jit(solution)/shard_map/ppermute | solution.py:18
  156.0 1.9 collective-permute-start.1
  157.9 0.0 collective-permute-done.4
  158.0 0.0 collective-permute-done.5
  158.0 1.6 broadcast_select_fusion
  159.6 0.0 copy-start
  159.6 0.0 copy-start.1
  159.6 0.2 fusion
  159.8 0.9 copy-done
  160.7 0.6 copy-done.1
  161.4 1.3 pad_maximum_fusion.2
  162.7 1.9 collective-permute-start.7
  164.6 0.0 copy-start.6
  164.6 1.3 pad_maximum_fusion.1
  165.9 9.4 %collective-permute-start.6 = (bf16[2,2,128,1536]{3,2,1,0:T(8,128)(2,1)}, bf16[2,2,128,1536]{3,2,1,0:T(8,128)(2,1)S(1)}, u32[]{:S(2)}, u32[]{:S(2)}) collective-permute-start(bf16[2,2,128,1536]{3,2,1,0:T(8,128)(2,1)} %pad_maximum_fusion.1), channel_id=1, source_target_pairs={{0,32},{32,64},{64,96},{96,128},{128,160},{160,192},{192,224},{224... | collective-permute-start | bytes 4718600 | tf_op jit(solution)/shard_map/ppermute | solution.py:18
  175.3 0.0 copy-done.6
  175.3 0.6 reshape_squeeze.3.flags_ref
  175.9 14.2 %collective-permute-done.refs_1_ = bf16[2,2,128,1536]{3,2,1,0:T(8,128)(2,1)} collective-permute-done((bf16[2,2,128,1536]{3,2,1,0:T(8,128)(2,1)}, bf16[2,2,128,1536]{3,2,1,0:T(8,128)(2,1)}, u32[]{:S(2)}, u32[]{:S(2)}) %collective-permute-start) | collective-permute-done | bytes 1572896 | tf_op jit(solution)/shard_map/ppermute | solution.py:18
  190.1 147.9 %collective-permute-done.1.refs_2_ = bf16[2,2,128,1536]{3,2,1,0:T(8,128)(2,1)} collective-permute-done((bf16[2,2,128,1536]{3,2,1,0:T(8,128)(2,1)}, bf16[2,2,128,1536]{3,2,1,0:T(8,128)(2,1)}, u32[]{:S(2)}, u32[]{:S(2)}) %collective-permute-start.1) | collective-permute-done | bytes 1572896 | tf_op jit(solution)/shard_map/ppermute | solution.py:18
  338.0 33.6 %collective-permute-done.7.refs_8_ = bf16[2,2,128,1536]{3,2,1,0:T(8,128)(2,1)S(1)} collective-permute-done((bf16[2,2,128,1536]{3,2,1,0:T(8,128)(2,1)}, bf16[2,2,128,1536]{3,2,1,0:T(8,128)(2,1)S(1)}, u32[]{:S(2)}, u32[]{:S(2)}) %collective-permute-start.7) | collective-permute-done | bytes 1572896 | tf_op jit(solution)/shard_map/ppermute | solution.py:18
  371.6 0.0 copy-start.4
  371.6 0.0 collective-permute-done.6.refs_7_
  371.6 1.2 copy-done.4
  372.8 0.0 copy-start.5
  372.8 1.2 copy-done.5
  374.0 21.4 %shard_map.46 = bf16[2,128,1536]{2,1,0:T(8,128)(2,1)} custom-call(s32[50]{0:T(128)} %reshape_squeeze.3.flags_ref, bf16[2,128,1536]{2,1,0:T(8,128)(2,1)} %q_ref.1, bf16[2,2,128,1536]{3,2,1,0:T(8,128)(2,1)} %pad_maximum_fusion.refs_0_, bf16[2,2,128,1536]{3,2,1,0:T(8,128)(2,1)} %collective-permute-done.refs_1_, ...), custom_call_target="tpu_custom_call" | custom-call | flops 2617245696 | bytes 14942208 | tf_op jit(solution)/shard_map/pallas_call | solution.py:137
  (1 shorter events, 0.0 us)
Async XLA Ops:
  2.7 39.6 %collective-permute-start.2 = (bf16[2,2,128,1536]{3,2,1,0:T(8,128)(2,1)}, bf16[2,2,128,1536]{3,2,1,0:T(8,128)(2,1)S(1)}, u32[]{:S(2)}, u32[]{:S(2)}) collective-permute-start(bf16[2,2,128,1536]{3,2,1,0:T(8,128)(2,1)} %pad_maximum_fusion.refs_0_), channel_id=1, source_target_pairs={{2,0},{3,1},{4,2},{5,3},{6,4},{7,5},{8,6},{9,7},{10,8},{11,9},{12,... | collective-permute-start | bytes 4718600 | tf_op jit(solution)/shard_map/ppermute | solution.py:18
  8.8 67.9 %collective-permute-start.3 = (bf16[2,2,128,1536]{3,2,1,0:T(8,128)(2,1)}, bf16[2,2,128,1536]{3,2,1,0:T(8,128)(2,1)S(1)}, u32[]{:S(2)}, u32[]{:S(2)}) collective-permute-start(bf16[2,2,128,1536]{3,2,1,0:T(8,128)(2,1)} %pad_maximum_fusion.refs_0_), channel_id=1, source_target_pairs={{0,2},{1,3},{2,4},{3,5},{4,6},{5,7},{6,8},{7,9},{8,10},{9,11},{10,... | collective-permute-start | bytes 4718600 | tf_op jit(solution)/shard_map/ppermute | solution.py:18
  10.7 147.2 %collective-permute-start.4 = (bf16[2,2,128,1536]{3,2,1,0:T(8,128)(2,1)}, bf16[2,2,128,1536]{3,2,1,0:T(8,128)(2,1)}, u32[]{:S(2)}, u32[]{:S(2)}) collective-permute-start(bf16[2,2,128,1536]{3,2,1,0:T(8,128)(2,1)} %pad_maximum_fusion.refs_0_), channel_id=1, source_target_pairs={{0,1},{1,0},{2,3},{3,2},{4,5},{5,4},{6,7},{7,6},{8,9},{9,8},{10,11... | collective-permute-start | bytes 4718600 | tf_op jit(solution)/shard_map/ppermute | solution.py:40
  42.3 34.6 %copy-start.2 = (bf16[2,2,128,1536]{3,2,1,0:T(8,128)(2,1)}, bf16[2,2,128,1536]{3,2,1,0:T(8,128)(2,1)S(1)}, u32[]{:S(2)}) copy-start(bf16[2,2,128,1536]{3,2,1,0:T(8,128)(2,1)S(1)} %collective-permute-done.2.refs_3_) | copy-start | bytes 4718596
  76.7 1.2 copy-start.3
  77.9 80.1 %collective-permute-start.5 = (bf16[2,2,128,1536]{3,2,1,0:T(8,128)(2,1)S(1)}, bf16[2,2,128,1536]{3,2,1,0:T(8,128)(2,1)S(1)}, u32[]{:S(2)}, u32[]{:S(2)}) collective-permute-start(bf16[2,2,128,1536]{3,2,1,0:T(8,128)(2,1)S(1)} %broadcast_select_fusion.2), channel_id=1, source_target_pairs={{0,1},{1,0},{2,3},{3,2},{4,5},{5,4},{6,7},{7,6},{8,9},{9,8},{10,11... | collective-permute-start | bytes 4718600 | tf_op jit(solution)/shard_map/ppermute | solution.py:40
  81.1 109.0 %collective-permute-start = (bf16[2,2,128,1536]{3,2,1,0:T(8,128)(2,1)}, bf16[2,2,128,1536]{3,2,1,0:T(8,128)(2,1)}, u32[]{:S(2)}, u32[]{:S(2)}) collective-permute-start(bf16[2,2,128,1536]{3,2,1,0:T(8,128)(2,1)} %pad_maximum_fusion.refs_0_), channel_id=1, source_target_pairs={{0,32},{32,64},{64,96},{96,128},{128,160},{160,192},{192,224},{224... | collective-permute-start | bytes 4718600 | tf_op jit(solution)/shard_map/ppermute | solution.py:18
  156.0 182.0 %collective-permute-start.1 = (bf16[2,2,128,1536]{3,2,1,0:T(8,128)(2,1)}, bf16[2,2,128,1536]{3,2,1,0:T(8,128)(2,1)}, u32[]{:S(2)}, u32[]{:S(2)}) collective-permute-start(bf16[2,2,128,1536]{3,2,1,0:T(8,128)(2,1)} %pad_maximum_fusion.refs_0_), channel_id=1, source_target_pairs={{32,0},{64,32},{96,64},{128,96},{160,128},{192,160},{224,192},{256... | collective-permute-start | bytes 4718600 | tf_op jit(solution)/shard_map/ppermute | solution.py:18
  159.6 1.1 copy-start
  159.6 1.8 copy-start.1
  162.7 209.0 %collective-permute-start.7 = (bf16[2,2,128,1536]{3,2,1,0:T(8,128)(2,1)}, bf16[2,2,128,1536]{3,2,1,0:T(8,128)(2,1)S(1)}, u32[]{:S(2)}, u32[]{:S(2)}) collective-permute-start(bf16[2,2,128,1536]{3,2,1,0:T(8,128)(2,1)} %pad_maximum_fusion.2), channel_id=1, source_target_pairs={{32,0},{64,32},{96,64},{128,96},{160,128},{192,160},{224,192},{256... | collective-permute-start | bytes 4718600 | tf_op jit(solution)/shard_map/ppermute | solution.py:18
  164.6 10.7 %copy-start.6 = (s32[2,1,5,5]{3,1,2,0:T(1,128)S(1)}, s32[2,1,5,5]{3,1,2,0:T(1,128)}, u32[]{:S(2)}) copy-start(s32[2,1,5,5]{3,1,2,0:T(1,128)} %param.7) | copy-start | bytes 604
  165.9 205.7 %collective-permute-start.6 = (bf16[2,2,128,1536]{3,2,1,0:T(8,128)(2,1)}, bf16[2,2,128,1536]{3,2,1,0:T(8,128)(2,1)S(1)}, u32[]{:S(2)}, u32[]{:S(2)}) collective-permute-start(bf16[2,2,128,1536]{3,2,1,0:T(8,128)(2,1)} %pad_maximum_fusion.1), channel_id=1, source_target_pairs={{0,32},{32,64},{64,96},{96,128},{128,160},{160,192},{192,224},{224... | collective-permute-start | bytes 4718600 | tf_op jit(solution)/shard_map/ppermute | solution.py:18
  371.6 1.2 copy-start.4
  372.8 1.2 copy-start.5

commit v4 on v2

--- a/solution.py
+++ b/solution.py
@@ -35,6 +35,33 @@
     return best
 
 
+X_CHIPS = 4
+
+
+def routed(pairs, block, axis="tm"):
+    return lax.ppermute(block, axis, pairs) if pairs else jnp.zeros_like(block)
+
+
+def tm_shift(block, step):
+    count = lax.axis_size("tm")
+    if step > 0:
+        edge = [t for t in range(count - 1) if t % X_CHIPS == X_CHIPS - 1]
+        direct = [(t, t + 1) for t in range(count - 1) if t not in edge]
+        x_then_z = ([(t, t - X_CHIPS + 1) for t in edge], [(t - X_CHIPS + 1, t + 1) for t in edge])
+        z_then_x = ([(t, t + X_CHIPS) for t in edge], [(t + X_CHIPS, t + 1) for t in edge])
+    else:
+        edge = [t for t in range(1, count) if t % X_CHIPS == 0]
+        direct = [(t, t - 1) for t in range(1, count) if t not in edge]
+        x_then_z = ([(t, t + X_CHIPS - 1) for t in edge], [(t + X_CHIPS - 1, t - 1) for t in edge])
+        z_then_x = ([(t, t - X_CHIPS) for t in edge], [(t - X_CHIPS, t - 1) for t in edge])
+    plain = routed(direct, block)
+    first = routed(x_then_z[1], routed(x_then_z[0], block[:1]))
+    second = routed(z_then_x[1], routed(z_then_x[0], block[1:]))
+    position = lax.axis_index("tm") % X_CHIPS
+    at_edge = position == (0 if step > 0 else X_CHIPS - 1)
+    return jnp.where(at_edge, jnp.concatenate([first, second], axis=0), plain)
+
+
 def swap_cores(block):
     devices = range(lax.axis_size("space"))
     return lax.ppermute(block, "space", [(i, i ^ 1) for i in devices])
@@ -42,8 +69,8 @@
 
 def fetch_sources(stacked):
     frame_count = stacked.shape[1]
-    earlier = shifted(stacked[:, frame_count - TR :], "tm", 1)
-    following = shifted(stacked[:, :TR], "tm", -1)
+    earlier = tm_shift(stacked[:, frame_count - TR :], 1)
+    following = tm_shift(stacked[:, :TR], -1)
     far_next = shifted(stacked, "space", -2)
     far_prev = shifted(stacked, "space", 2)
     core_zero = lax.axis_index("space") % 2 == 0

time: 283 us -> 292 us (1.032)
  the two profiles are of different devices: /device:TPU:30 before, /device:TPU:144 now
where the time goes in v4:
time: 292 us; the launch traced here: 291 us
  starting transfers between devices  145 us (50%)
  waiting for transfers between devices  111 us (38%)
  Pallas kernels  21.4 us (7%)
  other arithmetic  11.6 us (4%)
    ppermute x10, starting transfers between devices, routed(): return lax.ppermute(block, axis, pairs) if pairs else jnp.zeros_like(block)  123 us
    ppermute x10, waiting for transfers between devices, routed(): return lax.ppermute(block, axis, pairs) if pairs else jnp.zeros_like(block)  82.4 us
    ppermute x4, waiting for transfers between devices, shifted(): return lax.ppermute(block, axis, route)  28.4 us
    pallas_call x1, Pallas kernels, attend(): pl.pallas_call(attention_kernel, grid_spec=grid_spec, out_shape=jax.Shape...  21.4 us
    ppermute x4, starting transfers between devices, shifted(): return lax.ppermute(block, axis, route)  16.8 us
  transfers between devices with their start and end apart: 16, of which 6 were waited for; matrix products, arithmetic and copies ran while one was open for 4% of the time, Pallas kernels for 0%

profile of v4, /device:TPU:144, one launch (start us, length us, event | category | flops | bytes accessed | tf_op | source)
XLA Modules:
  0.0 291.3 jit_solution(4629911081612847487)
XLA Ops:
  0.0 4.7 %collective-permute-start.5 = (bf16[1,2,128,1536]{3,2,1,0:T(8,128)(2,1)}, bf16[1,2,128,1536]{3,2,1,0:T(8,128)(2,1)S(1)}, u32[]{:S(2)}, u32[]{:S(2)}) collective-permute-start(bf16[1,2,128,1536]{3,2,1,0:T(8,128)(2,1)} %bitcast.2), channel_id=1, source_target_pairs={{128,224},{256,352},{384,480},{129,225},{257,353},{385,481},{130,2... | collective-permute-start | bytes 2359304 | tf_op jit(solution)/shard_map/ppermute | solution.py:42
  4.7 1.3 collective-permute-start
  6.0 2.1 collective-permute-start.7
  8.1 2.7 pad_maximum_fusion.refs_0_
  10.8 3.8 %collective-permute-start.11 = (bf16[2,2,128,1536]{3,2,1,0:T(8,128)(2,1)}, bf16[2,2,128,1536]{3,2,1,0:T(8,128)(2,1)S(1)}, u32[]{:S(2)}, u32[]{:S(2)}) collective-permute-start(bf16[2,2,128,1536]{3,2,1,0:T(8,128)(2,1)} %pad_maximum_fusion.refs_0_), channel_id=1, source_target_pairs={{0,2},{1,3},{2,4},{3,5},{4,6},{5,7},{6,8},{7,9},{8,10},{9,11},{10,... | collective-permute-start | bytes 4718600 | tf_op jit(solution)/shard_map/ppermute | solution.py:18
  14.6 4.7 %collective-permute-start.10 = (bf16[2,2,128,1536]{3,2,1,0:T(8,128)(2,1)}, bf16[2,2,128,1536]{3,2,1,0:T(8,128)(2,1)S(1)}, u32[]{:S(2)}, u32[]{:S(2)}) collective-permute-start(bf16[2,2,128,1536]{3,2,1,0:T(8,128)(2,1)} %pad_maximum_fusion.refs_0_), channel_id=1, source_target_pairs={{2,0},{3,1},{4,2},{5,3},{6,4},{7,5},{8,6},{9,7},{10,8},{11,9},{12,... | collective-permute-start | bytes 4718600 | tf_op jit(solution)/shard_map/ppermute | solution.py:18
  19.3 2.4 collective-permute-done.5
  21.8 0.7 collective-permute-start.2
  22.5 4.6 %collective-permute-done = bf16[1,2,128,1536]{3,2,1,0:T(8,128)(2,1)S(1)} collective-permute-done((bf16[1,2,128,1536]{3,2,1,0:T(8,128)(2,1)}, bf16[1,2,128,1536]{3,2,1,0:T(8,128)(2,1)S(1)}, u32[]{:S(2)}, u32[]{:S(2)}) %collective-permute-start) | collective-permute-done | bytes 786464 | tf_op jit(solution)/shard_map/ppermute | solution.py:42
  27.0 1.6 collective-permute-start.6
  28.6 24.7 %collective-permute-done.7 = bf16[1,2,128,1536]{3,2,1,0:T(8,128)(2,1)} collective-permute-done((bf16[1,2,128,1536]{3,2,1,0:T(8,128)(2,1)}, bf16[1,2,128,1536]{3,2,1,0:T(8,128)(2,1)}, u32[]{:S(2)}, u32[]{:S(2)}) %collective-permute-start.7) | collective-permute-done | bytes 786464 | tf_op jit(solution)/shard_map/ppermute | solution.py:42
  53.3 1.3 collective-permute-start.9
  54.6 0.0 collective-permute-done.2
  54.6 0.0 copy-done.8
  54.6 0.0 copy-start.9
  54.6 5.7 %collective-permute-start.4 = (bf16[2,2,128,1536]{3,2,1,0:T(8,128)(2,1)}, bf16[2,2,128,1536]{3,2,1,0:T(8,128)(2,1)}, u32[]{:S(2)}, u32[]{:S(2)}) collective-permute-start(bf16[2,2,128,1536]{3,2,1,0:T(8,128)(2,1)} %pad_maximum_fusion.refs_0_), channel_id=1, source_target_pairs={{0,32},{32,64},{64,96},{128,160},{160,192},{192,224},{256,288},{28... | collective-permute-start | bytes 4718600 | tf_op jit(solution)/shard_map/ppermute | solution.py:42
  60.3 0.0 collective-permute-done.6
  60.3 96.5 %collective-permute-start.8 = (bf16[1,2,128,1536]{3,2,1,0:T(8,128)(2,1)}, bf16[1,2,128,1536]{3,2,1,0:T(8,128)(2,1)}, u32[]{:S(2)}, u32[]{:S(2)}) collective-permute-start(bf16[1,2,128,1536]{3,2,1,0:T(8,128)(2,1)} %collective-permute-done.7), channel_id=1, source_target_pairs={{0,96},{128,224},{256,352},{1,97},{129,225},{257,353},{2,98},{130,... | collective-permute-start | bytes 2359304 | tf_op jit(solution)/shard_map/ppermute | solution.py:42
  156.8 0.0 collective-permute-done.11.refs_4_
  156.8 8.4 %collective-permute-start.1 = (bf16[1,2,128,1536]{3,2,1,0:T(8,128)(2,1)}, bf16[1,2,128,1536]{3,2,1,0:T(8,128)(2,1)S(1)}, u32[]{:S(2)}, u32[]{:S(2)}) collective-permute-start(bf16[1,2,128,1536]{3,2,1,0:T(8,128)(2,1)} %copy-done.8), channel_id=1, source_target_pairs={{0,128},{128,256},{256,384},{1,129},{129,257},{257,385},{2,130},{1... | collective-permute-start | bytes 2359304 | tf_op jit(solution)/shard_map/ppermute | solution.py:42
  165.3 0.0 collective-permute-done.10.refs_3_
  165.3 1.3 collective-permute-start.3
  166.6 1.3 broadcast_select_fusion.2
  167.9 3.7 %collective-permute-done.8 = bf16[1,2,128,1536]{3,2,1,0:T(8,128)(2,1)} collective-permute-done((bf16[1,2,128,1536]{3,2,1,0:T(8,128)(2,1)}, bf16[1,2,128,1536]{3,2,1,0:T(8,128)(2,1)}, u32[]{:S(2)}, u32[]{:S(2)}) %collective-permute-start.8) | collective-permute-done | bytes 786464 | tf_op jit(solution)/shard_map/ppermute | solution.py:42
  171.6 1.9 collective-permute-start.12
  173.5 0.0 collective-permute-done.9
  173.5 2.4 collective-permute-start.13
  176.0 2.1 maximum_select_fusion.1.refs_2_
  178.0 0.1 slice.9
  178.1 47.0 %collective-permute-done.1 = bf16[1,2,128,1536]{3,2,1,0:T(8,128)(2,1)S(1)} collective-permute-done((bf16[1,2,128,1536]{3,2,1,0:T(8,128)(2,1)}, bf16[1,2,128,1536]{3,2,1,0:T(8,128)(2,1)S(1)}, u32[]{:S(2)}, u32[]{:S(2)}) %collective-permute-start.1) | collective-permute-done | bytes 786464 | tf_op jit(solution)/shard_map/ppermute | solution.py:42
  225.1 0.0 collective-permute-done.3
  225.1 0.0 collective-permute-done.4
  225.1 0.2 maximum_select_fusion.refs_1_
  225.3 0.1 slice.8
  225.4 0.0 copy-start.7
  225.4 1.4 pad_maximum_fusion.1
  226.8 0.1 copy-done.1
  227.0 1.9 collective-permute-start.15
  228.9 6.3 %collective-permute-start.14 = (bf16[2,2,128,1536]{3,2,1,0:T(8,128)(2,1)}, bf16[2,2,128,1536]{3,2,1,0:T(8,128)(2,1)S(1)}, u32[]{:S(2)}, u32[]{:S(2)}) collective-permute-start(bf16[2,2,128,1536]{3,2,1,0:T(8,128)(2,1)} %pad_maximum_fusion.1), channel_id=1, source_target_pairs={{1,0},{2,1},{3,2},{4,3},{5,4},{6,5},{7,6},{8,7},{9,8},{10,9},{11,1... | collective-permute-start | bytes 4718600 | tf_op jit(solution)/shard_map/ppermute | solution.py:18
  235.3 0.6 reshape_squeeze.3.flags_ref
  235.9 0.0 collective-permute-done.12
  235.9 0.0 collective-permute-done.13
  235.9 3.8 %broadcast_select_fusion = (bf16[2,2,128,1536]{3,2,1,0:T(8,128)(2,1)}, bf16[2,2,128,1536]{3,2,1,0:T(8,128)(2,1)}) fusion(bf16[2,2,128,1536]{3,2,1,0:T(8,128)(2,1)} %collective-permute-done.13, bf16[2,2,128,1536]{3,2,1,0:T(8,128)(2,1)} %collective-permute-done.12, pred[]{:T(512)S(6)} %eq.15), kind=kLoop, calls=%fused_computation.4 | loop fusion | flops 1572864 | bytes 6291457 | tf_op jit(solution)/shard_map/jit(_where)/select_n | solution.py:80
  239.7 28.4 %collective-permute-done.15.refs_8_ = bf16[2,2,128,1536]{3,2,1,0:T(8,128)(2,1)S(1)} collective-permute-done((bf16[2,2,128,1536]{3,2,1,0:T(8,128)(2,1)}, bf16[2,2,128,1536]{3,2,1,0:T(8,128)(2,1)S(1)}, u32[]{:S(2)}, u32[]{:S(2)}) %collective-permute-start.15) | collective-permute-done | bytes 1572896 | tf_op jit(solution)/shard_map/ppermute | solution.py:18
  268.1 0.0 collective-permute-done.14.refs_7_
  268.1 1.2 copy-done.4
  269.3 0.5 copy-done.5
  269.9 21.4 %shard_map.46 = bf16[2,128,1536]{2,1,0:T(8,128)(2,1)} custom-call(s32[50]{0:T(128)} %reshape_squeeze.3.flags_ref, bf16[2,128,1536]{2,1,0:T(8,128)(2,1)} %q_ref.1, bf16[2,2,128,1536]{3,2,1,0:T(8,128)(2,1)} %pad_maximum_fusion.refs_0_, bf16[2,2,128,1536]{3,2,1,0:T(8,128)(2,1)} %copy-done.1, bf16[2,2,128,1536]{3,2,1,0:T(8,128)(2,1)} %copy-done, ...), custom_call_target="tpu_custom_call" | custom-call | flops 2617245696 | bytes 14942208 | tf_op jit(solution)/shard_map/pallas_call | solution.py:157
  (15 shorter events, 0.1 us)
Async XLA Ops:
  0.0 21.8 %collective-permute-start.5 = (bf16[1,2,128,1536]{3,2,1,0:T(8,128)(2,1)}, bf16[1,2,128,1536]{3,2,1,0:T(8,128)(2,1)S(1)}, u32[]{:S(2)}, u32[]{:S(2)}) collective-permute-start(bf16[1,2,128,1536]{3,2,1,0:T(8,128)(2,1)} %bitcast.2), channel_id=1, source_target_pairs={{128,224},{256,352},{384,480},{129,225},{257,353},{385,481},{130,2... | collective-permute-start | bytes 2359304 | tf_op jit(solution)/shard_map/ppermute | solution.py:42
  4.7 22.3 %collective-permute-start = (bf16[1,2,128,1536]{3,2,1,0:T(8,128)(2,1)}, bf16[1,2,128,1536]{3,2,1,0:T(8,128)(2,1)S(1)}, u32[]{:S(2)}, u32[]{:S(2)}) collective-permute-start(bf16[1,2,128,1536]{3,2,1,0:T(8,128)(2,1)} %bitcast.3), channel_id=1, source_target_pairs={{96,0},{224,128},{352,256},{97,1},{225,129},{353,257},{98,2},{226,... | collective-permute-start | bytes 2359304 | tf_op jit(solution)/shard_map/ppermute | solution.py:42
  6.0 15.8 %copy-start.6 = (bf16[2,128,1536]{2,1,0:T(8,128)(2,1)S(1)}, bf16[2,128,1536]{2,1,0:T(8,128)(2,1)}, u32[]{:S(2)}) copy-start(bf16[2,128,1536]{2,1,0:T(8,128)(2,1)} %param.6) | copy-start | bytes 2359300
  6.0 47.3 %collective-permute-start.7 = (bf16[1,2,128,1536]{3,2,1,0:T(8,128)(2,1)}, bf16[1,2,128,1536]{3,2,1,0:T(8,128)(2,1)}, u32[]{:S(2)}, u32[]{:S(2)}) collective-permute-start(bf16[1,2,128,1536]{3,2,1,0:T(8,128)(2,1)} %bitcast.5), channel_id=1, source_target_pairs={{128,0},{256,128},{384,256},{129,1},{257,129},{385,257},{130,2},{2... | collective-permute-start | bytes 2359304 | tf_op jit(solution)/shard_map/ppermute | solution.py:42
  10.8 146.1 %collective-permute-start.11 = (bf16[2,2,128,1536]{3,2,1,0:T(8,128)(2,1)}, bf16[2,2,128,1536]{3,2,1,0:T(8,128)(2,1)S(1)}, u32[]{:S(2)}, u32[]{:S(2)}) collective-permute-start(bf16[2,2,128,1536]{3,2,1,0:T(8,128)(2,1)} %pad_maximum_fusion.refs_0_), channel_id=1, source_target_pairs={{0,2},{1,3},{2,4},{3,5},{4,6},{5,7},{6,8},{7,9},{8,10},{9,11},{10,... | collective-permute-start | bytes 4718600 | tf_op jit(solution)/shard_map/ppermute | solution.py:18
  14.6 150.7 %collective-permute-start.10 = (bf16[2,2,128,1536]{3,2,1,0:T(8,128)(2,1)}, bf16[2,2,128,1536]{3,2,1,0:T(8,128)(2,1)S(1)}, u32[]{:S(2)}, u32[]{:S(2)}) collective-permute-start(bf16[2,2,128,1536]{3,2,1,0:T(8,128)(2,1)} %pad_maximum_fusion.refs_0_), channel_id=1, source_target_pairs={{2,0},{3,1},{4,2},{5,3},{6,4},{7,5},{8,6},{9,7},{10,8},{11,9},{12,... | collective-permute-start | bytes 4718600 | tf_op jit(solution)/shard_map/ppermute | solution.py:18
  21.8 32.8 %collective-permute-start.2 = (bf16[1,2,128,1536]{3,2,1,0:T(8,128)(2,1)S(1)}, bf16[1,2,128,1536]{3,2,1,0:T(8,128)(2,1)S(1)}, u32[]{:S(2)}, u32[]{:S(2)}) collective-permute-start(bf16[1,2,128,1536]{3,2,1,0:T(8,128)(2,1)S(1)} %bitcast.7), channel_id=1, source_target_pairs={{96,224},{224,352},{352,480},{97,225},{225,353},{353,481},{98,226}... | collective-permute-start | bytes 2359304 | tf_op jit(solution)/shard_map/ppermute | solution.py:42
  27.0 27.6 %copy-start.8 = (bf16[1,2,128,1536]{3,2,1,0:T(8,128)(2,1)}, bf16[1,2,128,1536]{3,2,1,0:T(8,128)(2,1)S(1)}, u32[]{:S(2)}) copy-start(bf16[1,2,128,1536]{3,2,1,0:T(8,128)(2,1)S(1)} %collective-permute-done) | copy-start | bytes 2359300
  27.0 33.3 %collective-permute-start.6 = (bf16[1,2,128,1536]{3,2,1,0:T(8,128)(2,1)S(1)}, bf16[1,2,128,1536]{3,2,1,0:T(8,128)(2,1)}, u32[]{:S(2)}, u32[]{:S(2)}) collective-permute-start(bf16[1,2,128,1536]{3,2,1,0:T(8,128)(2,1)S(1)} %collective-permute-done.5), channel_id=1, source_target_pairs={{224,96},{352,224},{480,352},{225,97},{353,225},{481,353},{226,98}... | collective-permute-start | bytes 2359304 | tf_op jit(solution)/shard_map/ppermute | solution.py:42
  53.3 120.2 %collective-permute-start.9 = (bf16[2,2,128,1536]{3,2,1,0:T(8,128)(2,1)}, bf16[2,2,128,1536]{3,2,1,0:T(8,128)(2,1)}, u32[]{:S(2)}, u32[]{:S(2)}) collective-permute-start(bf16[2,2,128,1536]{3,2,1,0:T(8,128)(2,1)} %pad_maximum_fusion.refs_0_), channel_id=1, source_target_pairs={{32,0},{64,32},{96,64},{160,128},{192,160},{224,192},{288,256},{32... | collective-permute-start | bytes 4718600 | tf_op jit(solution)/shard_map/ppermute | solution.py:42
  54.6 5.7 %copy-start.9 = (bf16[1,2,128,1536]{3,2,1,0:T(8,128)(2,1)}, bf16[1,2,128,1536]{3,2,1,0:T(8,128)(2,1)S(1)}, u32[]{:S(2)}) copy-start(bf16[1,2,128,1536]{3,2,1,0:T(8,128)(2,1)S(1)} %collective-permute-done.2) | copy-start | bytes 2359300
  54.6 170.5 %collective-permute-start.4 = (bf16[2,2,128,1536]{3,2,1,0:T(8,128)(2,1)}, bf16[2,2,128,1536]{3,2,1,0:T(8,128)(2,1)}, u32[]{:S(2)}, u32[]{:S(2)}) collective-permute-start(bf16[2,2,128,1536]{3,2,1,0:T(8,128)(2,1)} %pad_maximum_fusion.refs_0_), channel_id=1, source_target_pairs={{0,32},{32,64},{64,96},{128,160},{160,192},{192,224},{256,288},{28... | collective-permute-start | bytes 4718600 | tf_op jit(solution)/shard_map/ppermute | solution.py:42
  60.3 111.3 %collective-permute-start.8 = (bf16[1,2,128,1536]{3,2,1,0:T(8,128)(2,1)}, bf16[1,2,128,1536]{3,2,1,0:T(8,128)(2,1)}, u32[]{:S(2)}, u32[]{:S(2)}) collective-permute-start(bf16[1,2,128,1536]{3,2,1,0:T(8,128)(2,1)} %collective-permute-done.7), channel_id=1, source_target_pairs={{0,96},{128,224},{256,352},{1,97},{129,225},{257,353},{2,98},{130,... | collective-permute-start | bytes 2359304 | tf_op jit(solution)/shard_map/ppermute | solution.py:42
  156.8 11.1 %copy-start.2 = (bf16[2,2,128,1536]{3,2,1,0:T(8,128)(2,1)}, bf16[2,2,128,1536]{3,2,1,0:T(8,128)(2,1)S(1)}, u32[]{:S(2)}) copy-start(bf16[2,2,128,1536]{3,2,1,0:T(8,128)(2,1)S(1)} %collective-permute-done.11.refs_4_) | copy-start | bytes 4718596
  156.8 68.2 %collective-permute-start.1 = (bf16[1,2,128,1536]{3,2,1,0:T(8,128)(2,1)}, bf16[1,2,128,1536]{3,2,1,0:T(8,128)(2,1)S(1)}, u32[]{:S(2)}, u32[]{:S(2)}) collective-permute-start(bf16[1,2,128,1536]{3,2,1,0:T(8,128)(2,1)} %copy-done.8), channel_id=1, source_target_pairs={{0,128},{128,256},{256,384},{1,129},{129,257},{257,385},{2,130},{1... | collective-permute-start | bytes 2359304 | tf_op jit(solution)/shard_map/ppermute | solution.py:42
  165.3 2.7 copy-start.3
  165.3 59.8 %collective-permute-start.3 = (bf16[1,2,128,1536]{3,2,1,0:T(8,128)(2,1)}, bf16[1,2,128,1536]{3,2,1,0:T(8,128)(2,1)S(1)}, u32[]{:S(2)}, u32[]{:S(2)}) collective-permute-start(bf16[1,2,128,1536]{3,2,1,0:T(8,128)(2,1)} %copy-done.9), channel_id=1, source_target_pairs={{224,128},{352,256},{480,384},{225,129},{353,257},{481,385},{226,1... | collective-permute-start | bytes 2359304 | tf_op jit(solution)/shard_map/ppermute | solution.py:42
  171.6 64.2 %collective-permute-start.12 = (bf16[2,2,128,1536]{3,2,1,0:T(8,128)(2,1)}, bf16[2,2,128,1536]{3,2,1,0:T(8,128)(2,1)}, u32[]{:S(2)}, u32[]{:S(2)}) collective-permute-start(bf16[2,2,128,1536]{3,2,1,0:T(8,128)(2,1)} %pad_maximum_fusion.refs_0_), channel_id=1, source_target_pairs={{0,1},{1,0},{2,3},{3,2},{4,5},{5,4},{6,7},{7,6},{8,9},{9,8},{10,11... | collective-permute-start | bytes 4718600 | tf_op jit(solution)/shard_map/ppermute | solution.py:67
  173.5 62.3 %collective-permute-start.13 = (bf16[2,2,128,1536]{3,2,1,0:T(8,128)(2,1)}, bf16[2,2,128,1536]{3,2,1,0:T(8,128)(2,1)}, u32[]{:S(2)}, u32[]{:S(2)}) collective-permute-start(bf16[2,2,128,1536]{3,2,1,0:T(8,128)(2,1)} %broadcast_select_fusion.2), channel_id=1, source_target_pairs={{0,1},{1,0},{2,3},{3,2},{4,5},{5,4},{6,7},{7,6},{8,9},{9,8},{10,11... | collective-permute-start | bytes 4718600 | tf_op jit(solution)/shard_map/ppermute | solution.py:67
  178.0 47.3 %copy-start = (bf16[2,2,128,1536]{3,2,1,0:T(8,128)(2,1)}, bf16[2,2,128,1536]{3,2,1,0:T(8,128)(2,1)S(1)}, u32[]{:S(2)}) copy-start(bf16[2,2,128,1536]{3,2,1,0:T(8,128)(2,1)S(1)} %maximum_select_fusion.1.refs_2_) | copy-start | bytes 4718596
  225.3 1.7 copy-start.1
  225.4 9.8 %copy-start.7 = (s32[2,1,5,5]{3,1,2,0:T(1,128)S(1)}, s32[2,1,5,5]{3,1,2,0:T(1,128)}, u32[]{:S(2)}) copy-start(s32[2,1,5,5]{3,1,2,0:T(1,128)} %param.7) | copy-start | bytes 604
  227.0 41.1 %collective-permute-start.15 = (bf16[2,2,128,1536]{3,2,1,0:T(8,128)(2,1)}, bf16[2,2,128,1536]{3,2,1,0:T(8,128)(2,1)S(1)}, u32[]{:S(2)}, u32[]{:S(2)}) collective-permute-start(bf16[2,2,128,1536]{3,2,1,0:T(8,128)(2,1)} %pad_maximum_fusion.1), channel_id=1, source_target_pairs={{0,1},{1,2},{2,3},{3,4},{4,5},{5,6},{6,7},{7,8},{8,9},{9,10},{10,1... | collective-permute-start | bytes 4718600 | tf_op jit(solution)/shard_map/ppermute | solution.py:18
  228.9 39.2 %collective-permute-start.14 = (bf16[2,2,128,1536]{3,2,1,0:T(8,128)(2,1)}, bf16[2,2,128,1536]{3,2,1,0:T(8,128)(2,1)S(1)}, u32[]{:S(2)}, u32[]{:S(2)}) collective-permute-start(bf16[2,2,128,1536]{3,2,1,0:T(8,128)(2,1)} %pad_maximum_fusion.1), channel_id=1, source_target_pairs={{1,0},{2,1},{3,2},{4,3},{5,4},{6,5},{7,6},{8,7},{9,8},{10,9},{11,1... | collective-permute-start | bytes 4718600 | tf_op jit(solution)/shard_map/ppermute | solution.py:18
  268.1 1.2 copy-start.4
  268.1 1.8 copy-start.5

commit v5 on v2

--- a/solution.py
+++ b/solution.py
@@ -75,37 +75,70 @@
     return (3 if e > 0 else 4), frame
 
 
-def attention_kernel(flags_ref, q_ref, *refs):
-    *sources, o_ref = refs
-    frame_count = q_ref.shape[0]
+LOCAL = (0, 3, 4, 5, 6)
+REMOTE = (1, 2, 7, 8)
+
+
+def scored_pairs(flags_ref, query, sources, frame, kept_sources):
     score_scale = 1.0 / math.sqrt(HD)
-    for frame in range(frame_count):
-        query = q_ref[frame]
-        score_list = []
-        value_list = []
-        for d, e in band_list():
-            which, index = locate(frame, d, e)
-            key_tile = sources[which][0, index]
-            raw = (
-                lax.dot_general(
-                    query, key_tile, (((1,), (1,)), ((), ())), preferred_element_type=jnp.float32
-                )
-                * score_scale
+    score_list = []
+    value_list = []
+    for d, e in band_list():
+        which, index = locate(frame, d, e)
+        if which not in kept_sources:
+            continue
+        source = sources[kept_sources.index(which)]
+        raw = (
+            lax.dot_general(
+                query, source[0, index], (((1,), (1,)), ((), ())), preferred_element_type=jnp.float32
             )
-            flag = flags_ref[frame * 25 + (TR + d) * 5 + (W + e)]
-            score_list.append(jnp.where(flag > 0, raw, -jnp.inf))
-            value_list.append(sources[which][1, index])
-        row_max = jnp.max(score_list[0], axis=1, keepdims=True)
-        for scores in score_list[1:]:
-            row_max = jnp.maximum(row_max, jnp.max(scores, axis=1, keepdims=True))
-        denominator = jnp.zeros_like(row_max)
-        summed = jnp.zeros((query.shape[0], HD), jnp.float32)
-        for scores, value_tile in zip(score_list, value_list):
-            weights = jnp.exp(scores - row_max)
-            denominator = denominator + jnp.sum(weights, axis=1, keepdims=True)
-            summed = summed + jnp.dot(
-                weights.astype(jnp.bfloat16), value_tile, preferred_element_type=jnp.float32
-            )
+            * score_scale
+        )
+        flag = flags_ref[frame * 25 + (TR + d) * 5 + (W + e)]
+        score_list.append(jnp.where(flag > 0, raw, -jnp.inf))
+        value_list.append(source[1, index])
+    row_max = jnp.max(score_list[0], axis=1, keepdims=True)
+    for scores in score_list[1:]:
+        row_max = jnp.maximum(row_max, jnp.max(scores, axis=1, keepdims=True))
+    return score_list, value_list, row_max
+
+
+def weighted_sums(score_list, value_list, row_max):
+    denominator = jnp.zeros_like(row_max)
+    summed = jnp.zeros((row_max.shape[0], HD), jnp.float32)
+    for scores, value_tile in zip(score_list, value_list):
+        weights = jnp.exp(scores - row_max)
+        denominator = denominator + jnp.sum(weights, axis=1, keepdims=True)
+        summed = summed + jnp.dot(
+            weights.astype(jnp.bfloat16), value_tile, preferred_element_type=jnp.float32
+        )
+    return denominator, summed
+
+
+def local_kernel(flags_ref, q_ref, *refs):
+    *sources, max_ref, sum_ref, acc_ref = refs
+    for frame in range(q_ref.shape[0]):
+        score_list, value_list, row_max = scored_pairs(
+            flags_ref, q_ref[frame], sources, frame, LOCAL
+        )
+        denominator, summed = weighted_sums(score_list, value_list, row_max)
+        max_ref[0, frame] = row_max
+        sum_ref[0, frame] = denominator
+        acc_ref[frame] = summed
+
+
+def remote_kernel(flags_ref, q_ref, *refs):
+    *sources, max_ref, sum_ref, acc_ref, o_ref = refs
+    for frame in range(q_ref.shape[0]):
+        score_list, value_list, remote_max = scored_pairs(
+            flags_ref, q_ref[frame], sources, frame, REMOTE
+        )
+        local_max = max_ref[0, frame]
+        row_max = jnp.maximum(local_max, remote_max)
+        rescale = jnp.exp(local_max - row_max)
+        denominator, summed = weighted_sums(score_list, value_list, row_max)
+        denominator = denominator + rescale * sum_ref[0, frame]
+        summed = summed + rescale * acc_ref[frame]
         o_ref[frame] = (summed / denominator).astype(o_ref.dtype)
 
 
@@ -115,24 +148,42 @@
     flags = tile_flags.reshape(-1).astype(jnp.int32)
     source_spec = pl.BlockSpec((2, 2, row_count, HD), lambda h, flags: (0, 0, 0, h))
     tile_spec = pl.BlockSpec((frame_count, row_count, HD), lambda h, flags: (0, 0, h))
-    grid_spec = pltpu.PrefetchScalarGridSpec(
-        num_scalar_prefetch=1,
-        grid=(head_count,),
-        in_specs=[tile_spec] + [source_spec] * len(sources),
-        out_specs=tile_spec,
-    )
-    pairs = len(band_list())
-    cost = pl.CostEstimate(
-        flops=4 * frame_count * head_count * pairs * row_count * row_count * HD,
-        transcendentals=frame_count * head_count * pairs * row_count * row_count,
-        bytes_accessed=(2 + 4 * len(sources)) * frame_count * row_count * feature_width,
-    )
+    stat_spec = pl.BlockSpec((1, frame_count, row_count, 1), lambda h, flags: (h, 0, 0, 0))
+    stat_shape = jax.ShapeDtypeStruct((head_count, frame_count, row_count, 1), jnp.float32)
+    acc_shape = jax.ShapeDtypeStruct(queries.shape, jnp.float32)
+    local_sources = [sources[i] for i in LOCAL]
+    remote_sources = [sources[i] for i in REMOTE]
+
+    def cost(count, extra):
+        return pl.CostEstimate(
+            flops=4 * frame_count * head_count * count * row_count * row_count * HD,
+            transcendentals=frame_count * head_count * count * row_count * row_count,
+            bytes_accessed=(2 + 4 * extra + 4) * frame_count * row_count * feature_width,
+        )
+
+    stats = pl.pallas_call(
+        local_kernel,
+        grid_spec=pltpu.PrefetchScalarGridSpec(
+            num_scalar_prefetch=1,
+            grid=(head_count,),
+            in_specs=[tile_spec] + [source_spec] * len(local_sources),
+            out_specs=[stat_spec, stat_spec, tile_spec],
+        ),
+        out_shape=[stat_shape, stat_shape, acc_shape],
+        cost_estimate=cost(16, len(local_sources)),
+    )(flags, queries, *local_sources)
     return pl.pallas_call(
-        attention_kernel,
-        grid_spec=grid_spec,
+        remote_kernel,
+        grid_spec=pltpu.PrefetchScalarGridSpec(
+            num_scalar_prefetch=1,
+            grid=(head_count,),
+            in_specs=[tile_spec] + [source_spec] * len(remote_sources)
+            + [stat_spec, stat_spec, tile_spec],
+            out_specs=tile_spec,
+        ),
         out_shape=jax.ShapeDtypeStruct(queries.shape, queries.dtype),
-        cost_estimate=cost,
-    )(flags, queries, *sources)
+        cost_estimate=cost(10, len(remote_sources)),
+    )(flags, queries, *remote_sources, *stats)
 
 
 def on_device(queries, keys, values, tile_mask):

time: 283 us -> 276 us (0.975)
  the two profiles are of different devices: /device:TPU:30 before, /device:TPU:118 now
where the time goes in v5:
time: 276 us; the launch traced here: 275 us
  waiting for transfers between devices  200 us (72%)
  Pallas kernels  33.8 us (12%)
  starting transfers between devices  27.1 us (10%)
  other arithmetic  10.5 us (4%)
  local copies, waits for them, and re-layouts  3.42 us (1%)
    ppermute x6, waiting for transfers between devices, shifted(): return lax.ppermute(block, axis, route)  200 us
    ppermute x6, starting transfers between devices, shifted(): return lax.ppermute(block, axis, route)  23.2 us
    pallas_call x1, Pallas kernels, attend(): pl.pallas_call(remote_kernel, grid_spec=pltpu.PrefetchScalarGridSpec(num_...  17.1 us
    pallas_call x1, Pallas kernels, attend(): pl.pallas_call(local_kernel, grid_spec=pltpu.PrefetchScalarGridSpec(num_s...  16.7 us
  transfers between devices with their start and end apart: 8, of which 3 were waited for; matrix products, arithmetic and copies ran while one was open for 3% of the time, Pallas kernels for 6%

profile of v5, /device:TPU:118, one launch (start us, length us, event | category | flops | bytes accessed | tf_op | source)
XLA Modules:
  0.0 275.1 jit_solution(8535172342815131162)
XLA Ops:
  0.0 2.7 pad_maximum_fusion.refs_0_
  2.7 1.9 collective-permute-start.5
  4.6 3.9 %collective-permute-start.4 = (bf16[2,2,128,1536]{3,2,1,0:T(8,128)(2,1)}, bf16[2,2,128,1536]{3,2,1,0:T(8,128)(2,1)}, u32[]{:S(2)}, u32[]{:S(2)}) collective-permute-start(bf16[2,2,128,1536]{3,2,1,0:T(8,128)(2,1)} %pad_maximum_fusion.refs_0_), channel_id=1, source_target_pairs={{2,0},{3,1},{4,2},{5,3},{6,4},{7,5},{8,6},{9,7},{10,8},{11,9},{12,... | collective-permute-start | bytes 4718600 | tf_op jit(solution)/shard_map/ppermute | solution.py:18
  8.5 2.7 collective-permute-start.1
  11.3 9.1 %collective-permute-start = (bf16[2,2,128,1536]{3,2,1,0:T(8,128)(2,1)}, bf16[2,2,128,1536]{3,2,1,0:T(8,128)(2,1)S(1)}, u32[]{:S(2)}, u32[]{:S(2)}) collective-permute-start(bf16[2,2,128,1536]{3,2,1,0:T(8,128)(2,1)} %pad_maximum_fusion.refs_0_), channel_id=1, source_target_pairs={{0,32},{32,64},{64,96},{96,128},{128,160},{160,192},{192,224},{224... | collective-permute-start | bytes 4718600 | tf_op jit(solution)/shard_map/ppermute | solution.py:18
  20.4 1.9 collective-permute-start.6
  22.3 120.9 %collective-permute-done.5.refs_2_ = bf16[2,2,128,1536]{3,2,1,0:T(8,128)(2,1)} collective-permute-done((bf16[2,2,128,1536]{3,2,1,0:T(8,128)(2,1)}, bf16[2,2,128,1536]{3,2,1,0:T(8,128)(2,1)}, u32[]{:S(2)}, u32[]{:S(2)}) %collective-permute-start.5) | collective-permute-done | bytes 1572896 | tf_op jit(solution)/shard_map/ppermute | solution.py:18
  143.2 0.0 collective-permute-done.4.refs_1_
  143.2 2.7 broadcast_select_fusion.2
  146.0 1.9 collective-permute-start.7
  147.9 67.1 %collective-permute-done.1.refs_1_ = bf16[2,2,128,1536]{3,2,1,0:T(8,128)(2,1)S(1)} collective-permute-done((bf16[2,2,128,1536]{3,2,1,0:T(8,128)(2,1)}, bf16[2,2,128,1536]{3,2,1,0:T(8,128)(2,1)S(1)}, u32[]{:S(2)}, u32[]{:S(2)}) %collective-permute-start.1) | collective-permute-done | bytes 1572896 | tf_op jit(solution)/shard_map/ppermute | solution.py:18
  215.0 0.0 copy-start
  215.0 0.1 slice.9
  215.1 0.0 collective-permute-done.refs_0_
  215.1 0.0 copy-start.1
  215.1 0.1 slice.8
  215.2 1.0 copy-done
  216.2 0.0 copy-start.4
  216.2 1.4 pad_maximum_fusion.1
  217.6 0.0 copy-done.1
  217.6 1.9 collective-permute-start.3
  219.5 3.6 %collective-permute-start.2 = (bf16[2,2,128,1536]{3,2,1,0:T(8,128)(2,1)}, bf16[2,2,128,1536]{3,2,1,0:T(8,128)(2,1)S(1)}, u32[]{:S(2)}, u32[]{:S(2)}) collective-permute-start(bf16[2,2,128,1536]{3,2,1,0:T(8,128)(2,1)} %pad_maximum_fusion.1), channel_id=1, source_target_pairs={{1,0},{2,1},{3,2},{4,3},{5,4},{6,5},{7,6},{8,7},{9,8},{10,9},{11,1... | collective-permute-start | bytes 4718600 | tf_op jit(solution)/shard_map/ppermute | solution.py:18
  223.1 0.0 copy-done.4
  223.2 0.6 reshape_squeeze.3.flags_ref
  223.8 0.0 collective-permute-done.6
  223.8 0.0 collective-permute-done.7
  223.8 3.7 %broadcast_select_fusion = (bf16[2,2,128,1536]{3,2,1,0:T(8,128)(2,1)}, bf16[2,2,128,1536]{3,2,1,0:T(8,128)(2,1)}) fusion(bf16[2,2,128,1536]{3,2,1,0:T(8,128)(2,1)} %collective-permute-done.7, bf16[2,2,128,1536]{3,2,1,0:T(8,128)(2,1)} %collective-permute-done.6, pred[]{:T(512)S(6)} %eq.5), kind=kLoop, calls=%fused_computation.2 | loop fusion | flops 1572864 | bytes 6291457 | tf_op jit(solution)/shard_map/jit(_where)/select_n | solution.py:53
  227.5 16.7 %shard_map.46 = (f32[12,2,128,1]{3,2,1,0:T(8,128)}, f32[12,2,128,1]{3,2,1,0:T(8,128)}, f32[2,128,1536]{2,1,0:T(8,128)}) custom-call(s32[50]{0:T(128)} %reshape_squeeze.3.flags_ref, bf16[2,128,1536]{2,1,0:T(8,128)(2,1)} %q_ref.3, bf16[2,2,128,1536]{3,2,1,0:T(8,128)(2,1)} %pad_maximum_fusion.refs_0_, bf16[2,2,128,1536]{3,2,1,0:T(8,128)(2,1)} %collective-permute-done.4.refs_1_, ...), custom_call_target="tpu_custom_call" | custom-call | flops 3221225472 | bytes 10223616 | tf_op jit(solution)/shard_map/pallas_call | solution.py:164
  244.2 12.1 %collective-permute-done.3.refs_3_ = bf16[2,2,128,1536]{3,2,1,0:T(8,128)(2,1)S(1)} collective-permute-done((bf16[2,2,128,1536]{3,2,1,0:T(8,128)(2,1)}, bf16[2,2,128,1536]{3,2,1,0:T(8,128)(2,1)S(1)}, u32[]{:S(2)}, u32[]{:S(2)}) %collective-permute-start.3) | collective-permute-done | bytes 1572896 | tf_op jit(solution)/shard_map/ppermute | solution.py:18
  256.4 0.0 copy-start.2
  256.4 0.0 collective-permute-done.2.refs_2_
  256.4 0.0 copy-start.3
  256.4 1.1 copy-done.2
  257.5 0.5 copy-done.3
  258.0 17.1 %shard_map.47 = bf16[2,128,1536]{2,1,0:T(8,128)(2,1)} custom-call(s32[50]{0:T(128)} %reshape_squeeze.3.flags_ref, bf16[2,128,1536]{2,1,0:T(8,128)(2,1)} %q_ref.3, bf16[2,2,128,1536]{3,2,1,0:T(8,128)(2,1)} %copy-done.1, bf16[2,2,128,1536]{3,2,1,0:T(8,128)(2,1)} %copy-done, bf16[2,2,128,1536]{3,2,1,0:T(8,128)(2,1)} %copy-done.3, ...), custom_call_target="tpu_custom_call" | custom-call | flops 2013265920 | bytes 8650752 | tf_op jit(solution)/shard_map/pallas_call | solution.py:175
  (1 shorter events, 0.0 us)
Async XLA Ops:
  2.7 140.6 %collective-permute-start.5 = (bf16[2,2,128,1536]{3,2,1,0:T(8,128)(2,1)}, bf16[2,2,128,1536]{3,2,1,0:T(8,128)(2,1)}, u32[]{:S(2)}, u32[]{:S(2)}) collective-permute-start(bf16[2,2,128,1536]{3,2,1,0:T(8,128)(2,1)} %pad_maximum_fusion.refs_0_), channel_id=1, source_target_pairs={{0,2},{1,3},{2,4},{3,5},{4,6},{5,7},{6,8},{7,9},{8,10},{9,11},{10,... | collective-permute-start | bytes 4718600 | tf_op jit(solution)/shard_map/ppermute | solution.py:18
  4.6 138.7 %collective-permute-start.4 = (bf16[2,2,128,1536]{3,2,1,0:T(8,128)(2,1)}, bf16[2,2,128,1536]{3,2,1,0:T(8,128)(2,1)}, u32[]{:S(2)}, u32[]{:S(2)}) collective-permute-start(bf16[2,2,128,1536]{3,2,1,0:T(8,128)(2,1)} %pad_maximum_fusion.refs_0_), channel_id=1, source_target_pairs={{2,0},{3,1},{4,2},{5,3},{6,4},{7,5},{8,6},{9,7},{10,8},{11,9},{12,... | collective-permute-start | bytes 4718600 | tf_op jit(solution)/shard_map/ppermute | solution.py:18
  8.5 206.5 %collective-permute-start.1 = (bf16[2,2,128,1536]{3,2,1,0:T(8,128)(2,1)}, bf16[2,2,128,1536]{3,2,1,0:T(8,128)(2,1)S(1)}, u32[]{:S(2)}, u32[]{:S(2)}) collective-permute-start(bf16[2,2,128,1536]{3,2,1,0:T(8,128)(2,1)} %pad_maximum_fusion.refs_0_), channel_id=1, source_target_pairs={{32,0},{64,32},{96,64},{128,96},{160,128},{192,160},{224,192},{256... | collective-permute-start | bytes 4718600 | tf_op jit(solution)/shard_map/ppermute | solution.py:18
  11.3 203.8 %collective-permute-start = (bf16[2,2,128,1536]{3,2,1,0:T(8,128)(2,1)}, bf16[2,2,128,1536]{3,2,1,0:T(8,128)(2,1)S(1)}, u32[]{:S(2)}, u32[]{:S(2)}) collective-permute-start(bf16[2,2,128,1536]{3,2,1,0:T(8,128)(2,1)} %pad_maximum_fusion.refs_0_), channel_id=1, source_target_pairs={{0,32},{32,64},{64,96},{96,128},{128,160},{160,192},{192,224},{224... | collective-permute-start | bytes 4718600 | tf_op jit(solution)/shard_map/ppermute | solution.py:18
  20.4 203.4 %collective-permute-start.6 = (bf16[2,2,128,1536]{3,2,1,0:T(8,128)(2,1)}, bf16[2,2,128,1536]{3,2,1,0:T(8,128)(2,1)}, u32[]{:S(2)}, u32[]{:S(2)}) collective-permute-start(bf16[2,2,128,1536]{3,2,1,0:T(8,128)(2,1)} %pad_maximum_fusion.refs_0_), channel_id=1, source_target_pairs={{0,1},{1,0},{2,3},{3,2},{4,5},{5,4},{6,7},{7,6},{8,9},{9,8},{10,11... | collective-permute-start | bytes 4718600 | tf_op jit(solution)/shard_map/ppermute | solution.py:40
  146.0 77.8 %collective-permute-start.7 = (bf16[2,2,128,1536]{3,2,1,0:T(8,128)(2,1)}, bf16[2,2,128,1536]{3,2,1,0:T(8,128)(2,1)}, u32[]{:S(2)}, u32[]{:S(2)}) collective-permute-start(bf16[2,2,128,1536]{3,2,1,0:T(8,128)(2,1)} %broadcast_select_fusion.2), channel_id=1, source_target_pairs={{0,1},{1,0},{2,3},{3,2},{4,5},{5,4},{6,7},{7,6},{8,9},{9,8},{10,11... | collective-permute-start | bytes 4718600 | tf_op jit(solution)/shard_map/ppermute | solution.py:40
  215.0 1.1 copy-start
  215.1 2.5 copy-start.1
  216.2 7.0 %copy-start.4 = (s32[2,1,5,5]{3,1,2,0:T(1,128)S(1)}, s32[2,1,5,5]{3,1,2,0:T(1,128)}, u32[]{:S(2)}) copy-start(s32[2,1,5,5]{3,1,2,0:T(1,128)} %param.7) | copy-start | bytes 604
  217.6 38.8 %collective-permute-start.3 = (bf16[2,2,128,1536]{3,2,1,0:T(8,128)(2,1)}, bf16[2,2,128,1536]{3,2,1,0:T(8,128)(2,1)S(1)}, u32[]{:S(2)}, u32[]{:S(2)}) collective-permute-start(bf16[2,2,128,1536]{3,2,1,0:T(8,128)(2,1)} %pad_maximum_fusion.1), channel_id=1, source_target_pairs={{0,1},{1,2},{2,3},{3,4},{4,5},{5,6},{6,7},{7,8},{8,9},{9,10},{10,1... | collective-permute-start | bytes 4718600 | tf_op jit(solution)/shard_map/ppermute | solution.py:18
  219.5 36.9 %collective-permute-start.2 = (bf16[2,2,128,1536]{3,2,1,0:T(8,128)(2,1)}, bf16[2,2,128,1536]{3,2,1,0:T(8,128)(2,1)S(1)}, u32[]{:S(2)}, u32[]{:S(2)}) collective-permute-start(bf16[2,2,128,1536]{3,2,1,0:T(8,128)(2,1)} %pad_maximum_fusion.1), channel_id=1, source_target_pairs={{1,0},{2,1},{3,2},{4,3},{5,4},{6,5},{7,6},{8,7},{9,8},{10,9},{11,1... | collective-permute-start | bytes 4718600 | tf_op jit(solution)/shard_map/ppermute | solution.py:18
  256.4 1.1 copy-start.2
  256.4 1.7 copy-start.3

commit v6 on v5

--- a/solution.py
+++ b/solution.py
@@ -76,10 +76,11 @@
 
 
 LOCAL = (0, 3, 4, 5, 6)
+HEAD_GROUP = 4
 REMOTE = (1, 2, 7, 8)
 
 
-def scored_pairs(flags_ref, query, sources, frame, kept_sources):
+def scored_pairs(flags_ref, query, sources, frame, kept_sources, lanes):
     score_scale = 1.0 / math.sqrt(HD)
     score_list = []
     value_list = []
@@ -90,13 +91,14 @@
         source = sources[kept_sources.index(which)]
         raw = (
             lax.dot_general(
-                query, source[0, index], (((1,), (1,)), ((), ())), preferred_element_type=jnp.float32
+                query, source[0, index, :, lanes], (((1,), (1,)), ((), ())),
+                preferred_element_type=jnp.float32,
             )
             * score_scale
         )
         flag = flags_ref[frame * 25 + (TR + d) * 5 + (W + e)]
         score_list.append(jnp.where(flag > 0, raw, -jnp.inf))
-        value_list.append(source[1, index])
+        value_list.append(source[1, index, :, lanes])
     row_max = jnp.max(score_list[0], axis=1, keepdims=True)
     for scores in score_list[1:]:
         row_max = jnp.maximum(row_max, jnp.max(scores, axis=1, keepdims=True))
@@ -117,38 +119,44 @@
 
 def local_kernel(flags_ref, q_ref, *refs):
     *sources, max_ref, sum_ref, acc_ref = refs
-    for frame in range(q_ref.shape[0]):
-        score_list, value_list, row_max = scored_pairs(
-            flags_ref, q_ref[frame], sources, frame, LOCAL
-        )
-        denominator, summed = weighted_sums(score_list, value_list, row_max)
-        max_ref[0, frame] = row_max
-        sum_ref[0, frame] = denominator
-        acc_ref[frame] = summed
+    for head in range(max_ref.shape[0]):
+        lanes = slice(head * HD, (head + 1) * HD)
+        for frame in range(q_ref.shape[0]):
+            score_list, value_list, row_max = scored_pairs(
+                flags_ref, q_ref[frame, :, lanes], sources, frame, LOCAL, lanes
+            )
+            denominator, summed = weighted_sums(score_list, value_list, row_max)
+            max_ref[head, frame] = row_max
+            sum_ref[head, frame] = denominator
+            acc_ref[frame, :, lanes] = summed
 
 
 def remote_kernel(flags_ref, q_ref, *refs):
     *sources, max_ref, sum_ref, acc_ref, o_ref = refs
-    for frame in range(q_ref.shape[0]):
-        score_list, value_list, remote_max = scored_pairs(
-            flags_ref, q_ref[frame], sources, frame, REMOTE
-        )
-        local_max = max_ref[0, frame]
-        row_max = jnp.maximum(local_max, remote_max)
-        rescale = jnp.exp(local_max - row_max)
-        denominator, summed = weighted_sums(score_list, value_list, row_max)
-        denominator = denominator + rescale * sum_ref[0, frame]
-        summed = summed + rescale * acc_ref[frame]
-        o_ref[frame] = (summed / denominator).astype(o_ref.dtype)
+    for head in range(max_ref.shape[0]):
+        lanes = slice(head * HD, (head + 1) * HD)
+        for frame in range(q_ref.shape[0]):
+            score_list, value_list, remote_max = scored_pairs(
+                flags_ref, q_ref[frame, :, lanes], sources, frame, REMOTE, lanes
+            )
+            local_max = max_ref[head, frame]
+            row_max = jnp.maximum(local_max, remote_max)
+            rescale = jnp.exp(local_max - row_max)
+            denominator, summed = weighted_sums(score_list, value_list, row_max)
+            denominator = denominator + rescale * sum_ref[head, frame]
+            summed = summed + rescale * acc_ref[frame, :, lanes]
+            o_ref[frame, :, lanes] = (summed / denominator).astype(o_ref.dtype)
 
 
 def attend(queries, sources, tile_flags):
     frame_count, row_count, feature_width = queries.shape
     head_count = feature_width // HD
+    group = HEAD_GROUP
+    steps = head_count // group
     flags = tile_flags.reshape(-1).astype(jnp.int32)
-    source_spec = pl.BlockSpec((2, 2, row_count, HD), lambda h, flags: (0, 0, 0, h))
-    tile_spec = pl.BlockSpec((frame_count, row_count, HD), lambda h, flags: (0, 0, h))
-    stat_spec = pl.BlockSpec((1, frame_count, row_count, 1), lambda h, flags: (h, 0, 0, 0))
+    source_spec = pl.BlockSpec((2, 2, row_count, group * HD), lambda h, flags: (0, 0, 0, h))
+    tile_spec = pl.BlockSpec((frame_count, row_count, group * HD), lambda h, flags: (0, 0, h))
+    stat_spec = pl.BlockSpec((group, frame_count, row_count, 1), lambda h, flags: (h, 0, 0, 0))
     stat_shape = jax.ShapeDtypeStruct((head_count, frame_count, row_count, 1), jnp.float32)
     acc_shape = jax.ShapeDtypeStruct(queries.shape, jnp.float32)
     local_sources = [sources[i] for i in LOCAL]
@@ -165,7 +173,7 @@
         local_kernel,
         grid_spec=pltpu.PrefetchScalarGridSpec(
             num_scalar_prefetch=1,
-            grid=(head_count,),
+            grid=(steps,),
             in_specs=[tile_spec] + [source_spec] * len(local_sources),
             out_specs=[stat_spec, stat_spec, tile_spec],
         ),
@@ -176,7 +184,7 @@
         remote_kernel,
         grid_spec=pltpu.PrefetchScalarGridSpec(
             num_scalar_prefetch=1,
-            grid=(head_count,),
+            grid=(steps,),
             in_specs=[tile_spec] + [source_spec] * len(remote_sources)
             + [stat_spec, stat_spec, tile_spec],
             out_specs=tile_spec,

time: 276 us -> 273 us (0.989)
  Pallas kernels: 33.8 us -> 29.2 us
  waiting for transfers between devices: 200 us -> 203 us
  transfers between devices with their start and end apart: 8 -> 8, of which waited for: 3 -> 3; matrix products, arithmetic and copies ran while one was open for 3% -> 3% of each run, Pallas kernels for 6% -> 5%
where the time goes in v6:
time: 273 us
  waiting for transfers between devices  203 us (74%)
  Pallas kernels  29.2 us (11%)
  starting transfers between devices  27.1 us (10%)
  other arithmetic  10.5 us (4%)
  local copies, waits for them, and re-layouts  3.42 us (1%)
    ppermute x6, waiting for transfers between devices, shifted(): return lax.ppermute(block, axis, route)  203 us
    ppermute x6, starting transfers between devices, shifted(): return lax.ppermute(block, axis, route)  23.2 us
    pallas_call x1, Pallas kernels, attend(): pl.pallas_call(remote_kernel, grid_spec=pltpu.PrefetchScalarGridSpec(num_...  14.9 us
    pallas_call x1, Pallas kernels, attend(): pl.pallas_call(local_kernel, grid_spec=pltpu.PrefetchScalarGridSpec(num_s...  14.4 us
  transfers between devices with their start and end apart: 8, of which 3 were waited for; matrix products, arithmetic and copies ran while one was open for 3% of the time, Pallas kernels for 5%

profile of v6, /device:TPU:118, one launch (start us, length us, event | category | flops | bytes accessed | tf_op | source)
XLA Modules:
  0.0 272.9 jit_solution(13154630941236775005)
XLA Ops:
  0.0 2.7 pad_maximum_fusion.refs_0_
  2.7 1.9 collective-permute-start.5
  4.6 3.9 %collective-permute-start.4 = (bf16[2,2,128,1536]{3,2,1,0:T(8,128)(2,1)}, bf16[2,2,128,1536]{3,2,1,0:T(8,128)(2,1)}, u32[]{:S(2)}, u32[]{:S(2)}) collective-permute-start(bf16[2,2,128,1536]{3,2,1,0:T(8,128)(2,1)} %pad_maximum_fusion.refs_0_), channel_id=1, source_target_pairs={{2,0},{3,1},{4,2},{5,3},{6,4},{7,5},{8,6},{9,7},{10,8},{11,9},{12,... | collective-permute-start | bytes 4718600 | tf_op jit(solution)/shard_map/ppermute | solution.py:18
  8.5 2.7 %collective-permute-start.1 = (bf16[2,2,128,1536]{3,2,1,0:T(8,128)(2,1)}, bf16[2,2,128,1536]{3,2,1,0:T(8,128)(2,1)S(1)}, u32[]{:S(2)}, u32[]{:S(2)}) collective-permute-start(bf16[2,2,128,1536]{3,2,1,0:T(8,128)(2,1)} %pad_maximum_fusion.refs_0_), channel_id=1, source_target_pairs={{32,0},{64,32},{96,64},{128,96},{160,128},{192,160},{224,192},{256... | collective-permute-start | bytes 4718600 | tf_op jit(solution)/shard_map/ppermute | solution.py:18
  11.3 9.1 %collective-permute-start = (bf16[2,2,128,1536]{3,2,1,0:T(8,128)(2,1)}, bf16[2,2,128,1536]{3,2,1,0:T(8,128)(2,1)S(1)}, u32[]{:S(2)}, u32[]{:S(2)}) collective-permute-start(bf16[2,2,128,1536]{3,2,1,0:T(8,128)(2,1)} %pad_maximum_fusion.refs_0_), channel_id=1, source_target_pairs={{0,32},{32,64},{64,96},{96,128},{128,160},{160,192},{192,224},{224... | collective-permute-start | bytes 4718600 | tf_op jit(solution)/shard_map/ppermute | solution.py:18
  20.4 1.9 collective-permute-start.6
  22.3 120.9 %collective-permute-done.5.refs_2_ = bf16[2,2,128,1536]{3,2,1,0:T(8,128)(2,1)} collective-permute-done((bf16[2,2,128,1536]{3,2,1,0:T(8,128)(2,1)}, bf16[2,2,128,1536]{3,2,1,0:T(8,128)(2,1)}, u32[]{:S(2)}, u32[]{:S(2)}) %collective-permute-start.5) | collective-permute-done | bytes 1572896 | tf_op jit(solution)/shard_map/ppermute | solution.py:18
  143.2 0.0 collective-permute-done.4.refs_1_
  143.2 2.7 %broadcast_select_fusion.2 = bf16[2,2,128,1536]{3,2,1,0:T(8,128)(2,1)} fusion(bf16[2,2,128,1536]{3,2,1,0:T(8,128)(2,1)} %collective-permute-done.4.refs_1_, bf16[2,2,128,1536]{3,2,1,0:T(8,128)(2,1)} %collective-permute-done.5.refs_2_, pred[]{:T(512)S(6)} %eq.5), kind=kLoop, calls=%fused_computation.4 | loop fusion | flops 786432 | bytes 4718593 | tf_op jit(solution)/shard_map/jit(_where)/select_n | solution.py:51
  146.0 1.9 collective-permute-start.7
  147.9 67.1 %collective-permute-done.1.refs_1_ = bf16[2,2,128,1536]{3,2,1,0:T(8,128)(2,1)S(1)} collective-permute-done((bf16[2,2,128,1536]{3,2,1,0:T(8,128)(2,1)}, bf16[2,2,128,1536]{3,2,1,0:T(8,128)(2,1)S(1)}, u32[]{:S(2)}, u32[]{:S(2)}) %collective-permute-start.1) | collective-permute-done | bytes 1572896 | tf_op jit(solution)/shard_map/ppermute | solution.py:18
  215.0 0.0 copy-start
  215.0 0.1 slice.9
  215.1 0.0 collective-permute-done.refs_0_
  215.1 0.0 copy-start.1
  215.1 0.1 slice.8
  215.2 1.0 copy-done
  216.2 0.0 copy-start.4
  216.2 1.4 pad_maximum_fusion.1
  217.6 0.0 copy-done.1
  217.6 1.9 collective-permute-start.3
  219.5 3.6 %collective-permute-start.2 = (bf16[2,2,128,1536]{3,2,1,0:T(8,128)(2,1)}, bf16[2,2,128,1536]{3,2,1,0:T(8,128)(2,1)S(1)}, u32[]{:S(2)}, u32[]{:S(2)}) collective-permute-start(bf16[2,2,128,1536]{3,2,1,0:T(8,128)(2,1)} %pad_maximum_fusion.1), channel_id=1, source_target_pairs={{1,0},{2,1},{3,2},{4,3},{5,4},{6,5},{7,6},{8,7},{9,8},{10,9},{11,1... | collective-permute-start | bytes 4718600 | tf_op jit(solution)/shard_map/ppermute | solution.py:18
  223.1 0.0 copy-done.4
  223.2 0.6 reshape_squeeze.3.flags_ref
  223.8 0.0 collective-permute-done.6
  223.8 0.0 collective-permute-done.7
  223.8 3.7 %broadcast_select_fusion = (bf16[2,2,128,1536]{3,2,1,0:T(8,128)(2,1)}, bf16[2,2,128,1536]{3,2,1,0:T(8,128)(2,1)}) fusion(bf16[2,2,128,1536]{3,2,1,0:T(8,128)(2,1)} %collective-permute-done.7, bf16[2,2,128,1536]{3,2,1,0:T(8,128)(2,1)} %collective-permute-done.6, pred[]{:T(512)S(6)} %eq.5), kind=kLoop, calls=%fused_computation.2 | loop fusion | flops 1572864 | bytes 6291457 | tf_op jit(solution)/shard_map/jit(_where)/select_n | solution.py:53
  227.5 14.4 %shard_map.46 = (f32[12,2,128,1]{3,2,1,0:T(8,128)}, f32[12,2,128,1]{3,2,1,0:T(8,128)}, f32[2,128,1536]{2,1,0:T(8,128)}) custom-call(s32[50]{0:T(128)} %reshape_squeeze.3.flags_ref, bf16[2,128,1536]{2,1,0:T(8,128)(2,1)} %q_ref.3, bf16[2,2,128,1536]{3,2,1,0:T(8,128)(2,1)} %pad_maximum_fusion.refs_0_, bf16[2,2,128,1536]{3,2,1,0:T(8,128)(2,1)} %collective-permute-done.4.refs_1_, ...), custom_call_target="tpu_custom_call" | custom-call | flops 3221225472 | bytes 10223616 | tf_op jit(solution)/shard_map/pallas_call | solution.py:172
  241.9 14.5 %collective-permute-done.3.refs_3_ = bf16[2,2,128,1536]{3,2,1,0:T(8,128)(2,1)S(1)} collective-permute-done((bf16[2,2,128,1536]{3,2,1,0:T(8,128)(2,1)}, bf16[2,2,128,1536]{3,2,1,0:T(8,128)(2,1)S(1)}, u32[]{:S(2)}, u32[]{:S(2)}) %collective-permute-start.3) | collective-permute-done | bytes 1572896 | tf_op jit(solution)/shard_map/ppermute | solution.py:18
  256.4 0.0 copy-start.2
  256.4 0.0 collective-permute-done.2.refs_2_
  256.4 0.0 copy-start.3
  256.4 1.1 copy-done.2
  257.5 0.5 copy-done.3
  258.0 14.9 %shard_map.47 = bf16[2,128,1536]{2,1,0:T(8,128)(2,1)} custom-call(s32[50]{0:T(128)} %reshape_squeeze.3.flags_ref, bf16[2,128,1536]{2,1,0:T(8,128)(2,1)} %q_ref.3, bf16[2,2,128,1536]{3,2,1,0:T(8,128)(2,1)} %copy-done.1, bf16[2,2,128,1536]{3,2,1,0:T(8,128)(2,1)} %copy-done, bf16[2,2,128,1536]{3,2,1,0:T(8,128)(2,1)} %copy-done.3, ...), custom_call_target="tpu_custom_call" | custom-call | flops 2013265920 | bytes 8650752 | tf_op jit(solution)/shard_map/pallas_call | solution.py:183
  (1 shorter events, 0.0 us)
Async XLA Ops:
  2.7 140.6 %collective-permute-start.5 = (bf16[2,2,128,1536]{3,2,1,0:T(8,128)(2,1)}, bf16[2,2,128,1536]{3,2,1,0:T(8,128)(2,1)}, u32[]{:S(2)}, u32[]{:S(2)}) collective-permute-start(bf16[2,2,128,1536]{3,2,1,0:T(8,128)(2,1)} %pad_maximum_fusion.refs_0_), channel_id=1, source_target_pairs={{0,2},{1,3},{2,4},{3,5},{4,6},{5,7},{6,8},{7,9},{8,10},{9,11},{10,... | collective-permute-start | bytes 4718600 | tf_op jit(solution)/shard_map/ppermute | solution.py:18
  4.6 138.7 %collective-permute-start.4 = (bf16[2,2,128,1536]{3,2,1,0:T(8,128)(2,1)}, bf16[2,2,128,1536]{3,2,1,0:T(8,128)(2,1)}, u32[]{:S(2)}, u32[]{:S(2)}) collective-permute-start(bf16[2,2,128,1536]{3,2,1,0:T(8,128)(2,1)} %pad_maximum_fusion.refs_0_), channel_id=1, source_target_pairs={{2,0},{3,1},{4,2},{5,3},{6,4},{7,5},{8,6},{9,7},{10,8},{11,9},{12,... | collective-permute-start | bytes 4718600 | tf_op jit(solution)/shard_map/ppermute | solution.py:18
  8.5 206.5 %collective-permute-start.1 = (bf16[2,2,128,1536]{3,2,1,0:T(8,128)(2,1)}, bf16[2,2,128,1536]{3,2,1,0:T(8,128)(2,1)S(1)}, u32[]{:S(2)}, u32[]{:S(2)}) collective-permute-start(bf16[2,2,128,1536]{3,2,1,0:T(8,128)(2,1)} %pad_maximum_fusion.refs_0_), channel_id=1, source_target_pairs={{32,0},{64,32},{96,64},{128,96},{160,128},{192,160},{224,192},{256... | collective-permute-start | bytes 4718600 | tf_op jit(solution)/shard_map/ppermute | solution.py:18
  11.3 203.8 %collective-permute-start = (bf16[2,2,128,1536]{3,2,1,0:T(8,128)(2,1)}, bf16[2,2,128,1536]{3,2,1,0:T(8,128)(2,1)S(1)}, u32[]{:S(2)}, u32[]{:S(2)}) collective-permute-start(bf16[2,2,128,1536]{3,2,1,0:T(8,128)(2,1)} %pad_maximum_fusion.refs_0_), channel_id=1, source_target_pairs={{0,32},{32,64},{64,96},{96,128},{128,160},{160,192},{192,224},{224... | collective-permute-start | bytes 4718600 | tf_op jit(solution)/shard_map/ppermute | solution.py:18
  20.4 203.4 %collective-permute-start.6 = (bf16[2,2,128,1536]{3,2,1,0:T(8,128)(2,1)}, bf16[2,2,128,1536]{3,2,1,0:T(8,128)(2,1)}, u32[]{:S(2)}, u32[]{:S(2)}) collective-permute-start(bf16[2,2,128,1536]{3,2,1,0:T(8,128)(2,1)} %pad_maximum_fusion.refs_0_), channel_id=1, source_target_pairs={{0,1},{1,0},{2,3},{3,2},{4,5},{5,4},{6,7},{7,6},{8,9},{9,8},{10,11... | collective-permute-start | bytes 4718600 | tf_op jit(solution)/shard_map/ppermute | solution.py:40
  146.0 77.8 %collective-permute-start.7 = (bf16[2,2,128,1536]{3,2,1,0:T(8,128)(2,1)}, bf16[2,2,128,1536]{3,2,1,0:T(8,128)(2,1)}, u32[]{:S(2)}, u32[]{:S(2)}) collective-permute-start(bf16[2,2,128,1536]{3,2,1,0:T(8,128)(2,1)} %broadcast_select_fusion.2), channel_id=1, source_target_pairs={{0,1},{1,0},{2,3},{3,2},{4,5},{5,4},{6,7},{7,6},{8,9},{9,8},{10,11... | collective-permute-start | bytes 4718600 | tf_op jit(solution)/shard_map/ppermute | solution.py:40
  215.0 1.1 copy-start
  215.1 2.5 copy-start.1
  216.2 7.0 %copy-start.4 = (s32[2,1,5,5]{3,1,2,0:T(1,128)S(1)}, s32[2,1,5,5]{3,1,2,0:T(1,128)}, u32[]{:S(2)}) copy-start(s32[2,1,5,5]{3,1,2,0:T(1,128)} %param.7) | copy-start | bytes 604
  217.6 38.8 %collective-permute-start.3 = (bf16[2,2,128,1536]{3,2,1,0:T(8,128)(2,1)}, bf16[2,2,128,1536]{3,2,1,0:T(8,128)(2,1)S(1)}, u32[]{:S(2)}, u32[]{:S(2)}) collective-permute-start(bf16[2,2,128,1536]{3,2,1,0:T(8,128)(2,1)} %pad_maximum_fusion.1), channel_id=1, source_target_pairs={{0,1},{1,2},{2,3},{3,4},{4,5},{5,6},{6,7},{7,8},{8,9},{9,10},{10,1... | collective-permute-start | bytes 4718600 | tf_op jit(solution)/shard_map/ppermute | solution.py:18
  219.5 36.9 %collective-permute-start.2 = (bf16[2,2,128,1536]{3,2,1,0:T(8,128)(2,1)}, bf16[2,2,128,1536]{3,2,1,0:T(8,128)(2,1)S(1)}, u32[]{:S(2)}, u32[]{:S(2)}) collective-permute-start(bf16[2,2,128,1536]{3,2,1,0:T(8,128)(2,1)} %pad_maximum_fusion.1), channel_id=1, source_target_pairs={{1,0},{2,1},{3,2},{4,3},{5,4},{6,5},{7,6},{8,7},{9,8},{10,9},{11,1... | collective-permute-start | bytes 4718600 | tf_op jit(solution)/shard_map/ppermute | solution.py:18
  256.4 1.1 copy-start.2
  256.4 1.7 copy-start.3

commit v7 on v6

--- a/solution.py
+++ b/solution.py
@@ -99,22 +99,22 @@
         flag = flags_ref[frame * 25 + (TR + d) * 5 + (W + e)]
         score_list.append(jnp.where(flag > 0, raw, -jnp.inf))
         value_list.append(source[1, index, :, lanes])
-    row_max = jnp.max(score_list[0], axis=1, keepdims=True)
+    tile_max = score_list[0]
     for scores in score_list[1:]:
-        row_max = jnp.maximum(row_max, jnp.max(scores, axis=1, keepdims=True))
-    return score_list, value_list, row_max
+        tile_max = jnp.maximum(tile_max, scores)
+    return score_list, value_list, jnp.max(tile_max, axis=1, keepdims=True)
 
 
 def weighted_sums(score_list, value_list, row_max):
-    denominator = jnp.zeros_like(row_max)
+    tile_sum = jnp.zeros_like(score_list[0])
     summed = jnp.zeros((row_max.shape[0], HD), jnp.float32)
     for scores, value_tile in zip(score_list, value_list):
         weights = jnp.exp(scores - row_max)
-        denominator = denominator + jnp.sum(weights, axis=1, keepdims=True)
+        tile_sum = tile_sum + weights
         summed = summed + jnp.dot(
             weights.astype(jnp.bfloat16), value_tile, preferred_element_type=jnp.float32
         )
-    return denominator, summed
+    return jnp.sum(tile_sum, axis=1, keepdims=True), summed
 
 
 def local_kernel(flags_ref, q_ref, *refs):

time: 273 us -> 273 us (level)
  no operation moved by 1% of the time
where the time goes in v7:
time: 273 us
  waiting for transfers between devices  203 us (74%)
  Pallas kernels  29.2 us (11%)
  starting transfers between devices  27.1 us (10%)
  other arithmetic  10.5 us (4%)
  local copies, waits for them, and re-layouts  3.42 us (1%)
    ppermute x6, waiting for transfers between devices, shifted(): return lax.ppermute(block, axis, route)  203 us
    ppermute x6, starting transfers between devices, shifted(): return lax.ppermute(block, axis, route)  23.2 us
    pallas_call x1, Pallas kernels, attend(): pl.pallas_call(remote_kernel, grid_spec=pltpu.PrefetchScalarGridSpec(num_...  14.9 us
    pallas_call x1, Pallas kernels, attend(): pl.pallas_call(local_kernel, grid_spec=pltpu.PrefetchScalarGridSpec(num_s...  14.3 us
  transfers between devices with their start and end apart: 8, of which 3 were waited for; matrix products, arithmetic and copies ran while one was open for 3% of the time, Pallas kernels for 5%

profile of v7, /device:TPU:118, one launch (start us, length us, event | category | flops | bytes accessed | tf_op | source)
XLA Modules:
  0.0 272.9 jit_solution(2363795736039389682)
XLA Ops:
  0.0 2.7 pad_maximum_fusion.refs_0_
  2.7 1.9 collective-permute-start.5
  4.6 3.9 %collective-permute-start.4 = (bf16[2,2,128,1536]{3,2,1,0:T(8,128)(2,1)}, bf16[2,2,128,1536]{3,2,1,0:T(8,128)(2,1)}, u32[]{:S(2)}, u32[]{:S(2)}) collective-permute-start(bf16[2,2,128,1536]{3,2,1,0:T(8,128)(2,1)} %pad_maximum_fusion.refs_0_), channel_id=1, source_target_pairs={{2,0},{3,1},{4,2},{5,3},{6,4},{7,5},{8,6},{9,7},{10,8},{11,9},{12,... | collective-permute-start | bytes 4718600 | tf_op jit(solution)/shard_map/ppermute | solution.py:18
  8.5 2.7 %collective-permute-start.1 = (bf16[2,2,128,1536]{3,2,1,0:T(8,128)(2,1)}, bf16[2,2,128,1536]{3,2,1,0:T(8,128)(2,1)S(1)}, u32[]{:S(2)}, u32[]{:S(2)}) collective-permute-start(bf16[2,2,128,1536]{3,2,1,0:T(8,128)(2,1)} %pad_maximum_fusion.refs_0_), channel_id=1, source_target_pairs={{32,0},{64,32},{96,64},{128,96},{160,128},{192,160},{224,192},{256... | collective-permute-start | bytes 4718600 | tf_op jit(solution)/shard_map/ppermute | solution.py:18
  11.3 9.1 %collective-permute-start = (bf16[2,2,128,1536]{3,2,1,0:T(8,128)(2,1)}, bf16[2,2,128,1536]{3,2,1,0:T(8,128)(2,1)S(1)}, u32[]{:S(2)}, u32[]{:S(2)}) collective-permute-start(bf16[2,2,128,1536]{3,2,1,0:T(8,128)(2,1)} %pad_maximum_fusion.refs_0_), channel_id=1, source_target_pairs={{0,32},{32,64},{64,96},{96,128},{128,160},{160,192},{192,224},{224... | collective-permute-start | bytes 4718600 | tf_op jit(solution)/shard_map/ppermute | solution.py:18
  20.4 1.9 collective-permute-start.6
  22.3 120.9 %collective-permute-done.5.refs_2_ = bf16[2,2,128,1536]{3,2,1,0:T(8,128)(2,1)} collective-permute-done((bf16[2,2,128,1536]{3,2,1,0:T(8,128)(2,1)}, bf16[2,2,128,1536]{3,2,1,0:T(8,128)(2,1)}, u32[]{:S(2)}, u32[]{:S(2)}) %collective-permute-start.5) | collective-permute-done | bytes 1572896 | tf_op jit(solution)/shard_map/ppermute | solution.py:18
  143.2 0.0 collective-permute-done.4.refs_1_
  143.2 2.7 %broadcast_select_fusion.2 = bf16[2,2,128,1536]{3,2,1,0:T(8,128)(2,1)} fusion(bf16[2,2,128,1536]{3,2,1,0:T(8,128)(2,1)} %collective-permute-done.4.refs_1_, bf16[2,2,128,1536]{3,2,1,0:T(8,128)(2,1)} %collective-permute-done.5.refs_2_, pred[]{:T(512)S(6)} %eq.5), kind=kLoop, calls=%fused_computation.4 | loop fusion | flops 786432 | bytes 4718593 | tf_op jit(solution)/shard_map/jit(_where)/select_n | solution.py:51
  146.0 1.9 collective-permute-start.7
  147.9 67.1 %collective-permute-done.1.refs_1_ = bf16[2,2,128,1536]{3,2,1,0:T(8,128)(2,1)S(1)} collective-permute-done((bf16[2,2,128,1536]{3,2,1,0:T(8,128)(2,1)}, bf16[2,2,128,1536]{3,2,1,0:T(8,128)(2,1)S(1)}, u32[]{:S(2)}, u32[]{:S(2)}) %collective-permute-start.1) | collective-permute-done | bytes 1572896 | tf_op jit(solution)/shard_map/ppermute | solution.py:18
  215.0 0.0 copy-start
  215.0 0.1 slice.9
  215.1 0.0 collective-permute-done.refs_0_
  215.1 0.0 copy-start.1
  215.1 0.1 slice.8
  215.2 1.0 copy-done
  216.2 0.0 copy-start.4
  216.2 1.4 pad_maximum_fusion.1
  217.6 0.0 copy-done.1
  217.6 1.9 collective-permute-start.3
  219.5 3.6 %collective-permute-start.2 = (bf16[2,2,128,1536]{3,2,1,0:T(8,128)(2,1)}, bf16[2,2,128,1536]{3,2,1,0:T(8,128)(2,1)S(1)}, u32[]{:S(2)}, u32[]{:S(2)}) collective-permute-start(bf16[2,2,128,1536]{3,2,1,0:T(8,128)(2,1)} %pad_maximum_fusion.1), channel_id=1, source_target_pairs={{1,0},{2,1},{3,2},{4,3},{5,4},{6,5},{7,6},{8,7},{9,8},{10,9},{11,1... | collective-permute-start | bytes 4718600 | tf_op jit(solution)/shard_map/ppermute | solution.py:18
  223.1 0.0 copy-done.4
  223.2 0.6 reshape_squeeze.3.flags_ref
  223.8 0.0 collective-permute-done.6
  223.8 0.0 collective-permute-done.7
  223.8 3.7 %broadcast_select_fusion = (bf16[2,2,128,1536]{3,2,1,0:T(8,128)(2,1)}, bf16[2,2,128,1536]{3,2,1,0:T(8,128)(2,1)}) fusion(bf16[2,2,128,1536]{3,2,1,0:T(8,128)(2,1)} %collective-permute-done.7, bf16[2,2,128,1536]{3,2,1,0:T(8,128)(2,1)} %collective-permute-done.6, pred[]{:T(512)S(6)} %eq.5), kind=kLoop, calls=%fused_computation.2 | loop fusion | flops 1572864 | bytes 6291457 | tf_op jit(solution)/shard_map/jit(_where)/select_n | solution.py:53
  227.5 14.3 %shard_map.46 = (f32[12,2,128,1]{3,2,1,0:T(8,128)}, f32[12,2,128,1]{3,2,1,0:T(8,128)}, f32[2,128,1536]{2,1,0:T(8,128)}) custom-call(s32[50]{0:T(128)} %reshape_squeeze.3.flags_ref, bf16[2,128,1536]{2,1,0:T(8,128)(2,1)} %q_ref.3, bf16[2,2,128,1536]{3,2,1,0:T(8,128)(2,1)} %pad_maximum_fusion.refs_0_, bf16[2,2,128,1536]{3,2,1,0:T(8,128)(2,1)} %collective-permute-done.4.refs_1_, ...), custom_call_target="tpu_custom_call" | custom-call | flops 3221225472 | bytes 10223616 | tf_op jit(solution)/shard_map/pallas_call | solution.py:172
  241.8 14.5 %collective-permute-done.3.refs_3_ = bf16[2,2,128,1536]{3,2,1,0:T(8,128)(2,1)S(1)} collective-permute-done((bf16[2,2,128,1536]{3,2,1,0:T(8,128)(2,1)}, bf16[2,2,128,1536]{3,2,1,0:T(8,128)(2,1)S(1)}, u32[]{:S(2)}, u32[]{:S(2)}) %collective-permute-start.3) | collective-permute-done | bytes 1572896 | tf_op jit(solution)/shard_map/ppermute | solution.py:18
  256.4 0.0 copy-start.2
  256.4 0.0 collective-permute-done.2.refs_2_
  256.4 0.0 copy-start.3
  256.4 1.1 copy-done.2
  257.5 0.5 copy-done.3
  258.0 14.9 %shard_map.47 = bf16[2,128,1536]{2,1,0:T(8,128)(2,1)} custom-call(s32[50]{0:T(128)} %reshape_squeeze.3.flags_ref, bf16[2,128,1536]{2,1,0:T(8,128)(2,1)} %q_ref.3, bf16[2,2,128,1536]{3,2,1,0:T(8,128)(2,1)} %copy-done.1, bf16[2,2,128,1536]{3,2,1,0:T(8,128)(2,1)} %copy-done, bf16[2,2,128,1536]{3,2,1,0:T(8,128)(2,1)} %copy-done.3, ...), custom_call_target="tpu_custom_call" | custom-call | flops 2013265920 | bytes 8650752 | tf_op jit(solution)/shard_map/pallas_call | solution.py:183
  (1 shorter events, 0.0 us)
Async XLA Ops:
  2.7 140.6 %collective-permute-start.5 = (bf16[2,2,128,1536]{3,2,1,0:T(8,128)(2,1)}, bf16[2,2,128,1536]{3,2,1,0:T(8,128)(2,1)}, u32[]{:S(2)}, u32[]{:S(2)}) collective-permute-start(bf16[2,2,128,1536]{3,2,1,0:T(8,128)(2,1)} %pad_maximum_fusion.refs_0_), channel_id=1, source_target_pairs={{0,2},{1,3},{2,4},{3,5},{4,6},{5,7},{6,8},{7,9},{8,10},{9,11},{10,... | collective-permute-start | bytes 4718600 | tf_op jit(solution)/shard_map/ppermute | solution.py:18
  4.6 138.7 %collective-permute-start.4 = (bf16[2,2,128,1536]{3,2,1,0:T(8,128)(2,1)}, bf16[2,2,128,1536]{3,2,1,0:T(8,128)(2,1)}, u32[]{:S(2)}, u32[]{:S(2)}) collective-permute-start(bf16[2,2,128,1536]{3,2,1,0:T(8,128)(2,1)} %pad_maximum_fusion.refs_0_), channel_id=1, source_target_pairs={{2,0},{3,1},{4,2},{5,3},{6,4},{7,5},{8,6},{9,7},{10,8},{11,9},{12,... | collective-permute-start | bytes 4718600 | tf_op jit(solution)/shard_map/ppermute | solution.py:18
  8.5 206.5 %collective-permute-start.1 = (bf16[2,2,128,1536]{3,2,1,0:T(8,128)(2,1)}, bf16[2,2,128,1536]{3,2,1,0:T(8,128)(2,1)S(1)}, u32[]{:S(2)}, u32[]{:S(2)}) collective-permute-start(bf16[2,2,128,1536]{3,2,1,0:T(8,128)(2,1)} %pad_maximum_fusion.refs_0_), channel_id=1, source_target_pairs={{32,0},{64,32},{96,64},{128,96},{160,128},{192,160},{224,192},{256... | collective-permute-start | bytes 4718600 | tf_op jit(solution)/shard_map/ppermute | solution.py:18
  11.3 203.8 %collective-permute-start = (bf16[2,2,128,1536]{3,2,1,0:T(8,128)(2,1)}, bf16[2,2,128,1536]{3,2,1,0:T(8,128)(2,1)S(1)}, u32[]{:S(2)}, u32[]{:S(2)}) collective-permute-start(bf16[2,2,128,1536]{3,2,1,0:T(8,128)(2,1)} %pad_maximum_fusion.refs_0_), channel_id=1, source_target_pairs={{0,32},{32,64},{64,96},{96,128},{128,160},{160,192},{192,224},{224... | collective-permute-start | bytes 4718600 | tf_op jit(solution)/shard_map/ppermute | solution.py:18
  20.4 203.4 %collective-permute-start.6 = (bf16[2,2,128,1536]{3,2,1,0:T(8,128)(2,1)}, bf16[2,2,128,1536]{3,2,1,0:T(8,128)(2,1)}, u32[]{:S(2)}, u32[]{:S(2)}) collective-permute-start(bf16[2,2,128,1536]{3,2,1,0:T(8,128)(2,1)} %pad_maximum_fusion.refs_0_), channel_id=1, source_target_pairs={{0,1},{1,0},{2,3},{3,2},{4,5},{5,4},{6,7},{7,6},{8,9},{9,8},{10,11... | collective-permute-start | bytes 4718600 | tf_op jit(solution)/shard_map/ppermute | solution.py:40
  146.0 77.8 %collective-permute-start.7 = (bf16[2,2,128,1536]{3,2,1,0:T(8,128)(2,1)}, bf16[2,2,128,1536]{3,2,1,0:T(8,128)(2,1)}, u32[]{:S(2)}, u32[]{:S(2)}) collective-permute-start(bf16[2,2,128,1536]{3,2,1,0:T(8,128)(2,1)} %broadcast_select_fusion.2), channel_id=1, source_target_pairs={{0,1},{1,0},{2,3},{3,2},{4,5},{5,4},{6,7},{7,6},{8,9},{9,8},{10,11... | collective-permute-start | bytes 4718600 | tf_op jit(solution)/shard_map/ppermute | solution.py:40
  215.0 1.1 copy-start
  215.1 2.5 copy-start.1
  216.2 7.0 %copy-start.4 = (s32[2,1,5,5]{3,1,2,0:T(1,128)S(1)}, s32[2,1,5,5]{3,1,2,0:T(1,128)}, u32[]{:S(2)}) copy-start(s32[2,1,5,5]{3,1,2,0:T(1,128)} %param.7) | copy-start | bytes 604
  217.6 38.8 %collective-permute-start.3 = (bf16[2,2,128,1536]{3,2,1,0:T(8,128)(2,1)}, bf16[2,2,128,1536]{3,2,1,0:T(8,128)(2,1)S(1)}, u32[]{:S(2)}, u32[]{:S(2)}) collective-permute-start(bf16[2,2,128,1536]{3,2,1,0:T(8,128)(2,1)} %pad_maximum_fusion.1), channel_id=1, source_target_pairs={{0,1},{1,2},{2,3},{3,4},{4,5},{5,6},{6,7},{7,8},{8,9},{9,10},{10,1... | collective-permute-start | bytes 4718600 | tf_op jit(solution)/shard_map/ppermute | solution.py:18
  219.5 36.9 %collective-permute-start.2 = (bf16[2,2,128,1536]{3,2,1,0:T(8,128)(2,1)}, bf16[2,2,128,1536]{3,2,1,0:T(8,128)(2,1)S(1)}, u32[]{:S(2)}, u32[]{:S(2)}) collective-permute-start(bf16[2,2,128,1536]{3,2,1,0:T(8,128)(2,1)} %pad_maximum_fusion.1), channel_id=1, source_target_pairs={{1,0},{2,1},{3,2},{4,3},{5,4},{6,5},{7,6},{8,7},{9,8},{10,9},{11,1... | collective-permute-start | bytes 4718600 | tf_op jit(solution)/shard_map/ppermute | solution.py:18
  256.4 1.1 copy-start.2
  256.4 1.7 copy-start.3

commit v8 on v7

--- a/solution.py
+++ b/solution.py
@@ -119,8 +119,10 @@
 
 def local_kernel(flags_ref, q_ref, *refs):
     *sources, max_ref, sum_ref, acc_ref = refs
-    for head in range(max_ref.shape[0]):
-        lanes = slice(head * HD, (head + 1) * HD)
+
+    @pl.loop(0, max_ref.shape[0])
+    def _(head):
+        lanes = pl.ds(pl.multiple_of(head * HD, HD), HD)
         for frame in range(q_ref.shape[0]):
             score_list, value_list, row_max = scored_pairs(
                 flags_ref, q_ref[frame, :, lanes], sources, frame, LOCAL, lanes
@@ -133,8 +135,10 @@
 
 def remote_kernel(flags_ref, q_ref, *refs):
     *sources, max_ref, sum_ref, acc_ref, o_ref = refs
-    for head in range(max_ref.shape[0]):
-        lanes = slice(head * HD, (head + 1) * HD)
+
+    @pl.loop(0, max_ref.shape[0])
+    def _(head):
+        lanes = pl.ds(pl.multiple_of(head * HD, HD), HD)
         for frame in range(q_ref.shape[0]):
             score_list, value_list, remote_max = scored_pairs(
                 flags_ref, q_ref[frame, :, lanes], sources, frame, REMOTE, lanes
@@ -151,16 +155,14 @@
 def attend(queries, sources, tile_flags):
     frame_count, row_count, feature_width = queries.shape
     head_count = feature_width // HD
-    group = HEAD_GROUP
-    steps = head_count // group
     flags = tile_flags.reshape(-1).astype(jnp.int32)
-    source_spec = pl.BlockSpec((2, 2, row_count, group * HD), lambda h, flags: (0, 0, 0, h))
-    tile_spec = pl.BlockSpec((frame_count, row_count, group * HD), lambda h, flags: (0, 0, h))
-    stat_spec = pl.BlockSpec((group, frame_count, row_count, 1), lambda h, flags: (h, 0, 0, 0))
     stat_shape = jax.ShapeDtypeStruct((head_count, frame_count, row_count, 1), jnp.float32)
     acc_shape = jax.ShapeDtypeStruct(queries.shape, jnp.float32)
     local_sources = [sources[i] for i in LOCAL]
     remote_sources = [sources[i] for i in REMOTE]
+    smem = pl.BlockSpec(memory_space=pltpu.SMEM)
+    vmem = pl.BlockSpec(memory_space=pltpu.VMEM)
+    params = pltpu.CompilerParams(vmem_limit_bytes=48 * 1024 * 1024)
 
     def cost(count, extra):
         return pl.CostEstimate(
@@ -171,25 +173,18 @@
 
     stats = pl.pallas_call(
         local_kernel,
-        grid_spec=pltpu.PrefetchScalarGridSpec(
-            num_scalar_prefetch=1,
-            grid=(steps,),
-            in_specs=[tile_spec] + [source_spec] * len(local_sources),
-            out_specs=[stat_spec, stat_spec, tile_spec],
-        ),
+        in_specs=[smem, vmem] + [vmem] * len(local_sources),
+        out_specs=[vmem, vmem, vmem],
         out_shape=[stat_shape, stat_shape, acc_shape],
+        compiler_params=params,
         cost_estimate=cost(16, len(local_sources)),
     )(flags, queries, *local_sources)
     return pl.pallas_call(
         remote_kernel,
-        grid_spec=pltpu.PrefetchScalarGridSpec(
-            num_scalar_prefetch=1,
-            grid=(steps,),
-            in_specs=[tile_spec] + [source_spec] * len(remote_sources)
-            + [stat_spec, stat_spec, tile_spec],
-            out_specs=tile_spec,
-        ),
+        in_specs=[smem, vmem] + [vmem] * (len(remote_sources) + 3),
+        out_specs=vmem,
         out_shape=jax.ShapeDtypeStruct(queries.shape, queries.dtype),
+        compiler_params=params,
         cost_estimate=cost(10, len(remote_sources)),
     )(flags, queries, *remote_sources, *stats)
 

time: 273 us -> 273 us (level)
  waiting for transfers between devices: 203 us -> 197 us
  Pallas kernels: 29.2 us -> 34.5 us
    ppermute x6, waiting for transfers between devices: 203 us -> 197 us  [shifted(): return lax.ppermute(block, axis, route)]
    pallas_call x2, Pallas kernels: 29.2 us -> 34.5 us  [the longest x1 17.5 us: attend(): pl.pallas_call(remote_kernel, in_specs=[smem, vmem] + [vmem] * (len(remot...]
  transfers between devices with their start and end apart: 8 -> 8, of which waited for: 3 -> 3; matrix products, arithmetic and copies ran while one was open for 3% -> 3% of each run, Pallas kernels for 5% -> 6%
where the time goes in v8:
time: 273 us
  waiting for transfers between devices  197 us (72%)
  Pallas kernels  34.5 us (13%)
  starting transfers between devices  27.1 us (10%)
  other arithmetic  10.6 us (4%)
  local copies, waits for them, and re-layouts  3.74 us (1%)
    ppermute x6, waiting for transfers between devices, shifted(): return lax.ppermute(block, axis, route)  197 us
    ppermute x6, starting transfers between devices, shifted(): return lax.ppermute(block, axis, route)  23.2 us
    pallas_call x1, Pallas kernels, attend(): pl.pallas_call(remote_kernel, in_specs=[smem, vmem] + [vmem] * (len(remot...  17.5 us
    pallas_call x1, Pallas kernels, attend(): pl.pallas_call(local_kernel, in_specs=[smem, vmem] + [vmem] * len(local_s...  17 us
  transfers between devices with their start and end apart: 8, of which 3 were waited for; matrix products, arithmetic and copies ran while one was open for 3% of the time, Pallas kernels for 6%

profile of v8, /device:TPU:118, one launch (start us, length us, event | category | flops | bytes accessed | tf_op | source)
XLA Modules:
  0.0 272.9 jit_solution(12784491919115709869)
XLA Ops:
  0.0 2.7 pad_maximum_fusion.refs_0_
  2.7 1.9 collective-permute-start.5
  4.6 3.9 %collective-permute-start.4 = (bf16[2,2,128,1536]{3,2,1,0:T(8,128)(2,1)}, bf16[2,2,128,1536]{3,2,1,0:T(8,128)(2,1)}, u32[]{:S(2)}, u32[]{:S(2)}) collective-permute-start(bf16[2,2,128,1536]{3,2,1,0:T(8,128)(2,1)} %pad_maximum_fusion.refs_0_), channel_id=1, source_target_pairs={{2,0},{3,1},{4,2},{5,3},{6,4},{7,5},{8,6},{9,7},{10,8},{11,9},{12,... | collective-permute-start | bytes 4718600 | tf_op jit(solution)/shard_map/ppermute | solution.py:18
  8.5 2.7 %collective-permute-start.1 = (bf16[2,2,128,1536]{3,2,1,0:T(8,128)(2,1)}, bf16[2,2,128,1536]{3,2,1,0:T(8,128)(2,1)S(1)}, u32[]{:S(2)}, u32[]{:S(2)}) collective-permute-start(bf16[2,2,128,1536]{3,2,1,0:T(8,128)(2,1)} %pad_maximum_fusion.refs_0_), channel_id=1, source_target_pairs={{32,0},{64,32},{96,64},{128,96},{160,128},{192,160},{224,192},{256... | collective-permute-start | bytes 4718600 | tf_op jit(solution)/shard_map/ppermute | solution.py:18
  11.3 9.1 %collective-permute-start = (bf16[2,2,128,1536]{3,2,1,0:T(8,128)(2,1)}, bf16[2,2,128,1536]{3,2,1,0:T(8,128)(2,1)S(1)}, u32[]{:S(2)}, u32[]{:S(2)}) collective-permute-start(bf16[2,2,128,1536]{3,2,1,0:T(8,128)(2,1)} %pad_maximum_fusion.refs_0_), channel_id=1, source_target_pairs={{0,32},{32,64},{64,96},{96,128},{128,160},{160,192},{192,224},{224... | collective-permute-start | bytes 4718600 | tf_op jit(solution)/shard_map/ppermute | solution.py:18
  20.4 1.9 collective-permute-start.6
  22.3 120.9 %collective-permute-done.5.refs_2_ = bf16[2,2,128,1536]{3,2,1,0:T(8,128)(2,1)} collective-permute-done((bf16[2,2,128,1536]{3,2,1,0:T(8,128)(2,1)}, bf16[2,2,128,1536]{3,2,1,0:T(8,128)(2,1)}, u32[]{:S(2)}, u32[]{:S(2)}) %collective-permute-start.5) | collective-permute-done | bytes 1572896 | tf_op jit(solution)/shard_map/ppermute | solution.py:18
  143.3 0.0 collective-permute-done.4.refs_1_
  143.3 2.7 %broadcast_select_fusion.2 = bf16[2,2,128,1536]{3,2,1,0:T(8,128)(2,1)} fusion(bf16[2,2,128,1536]{3,2,1,0:T(8,128)(2,1)} %collective-permute-done.4.refs_1_, bf16[2,2,128,1536]{3,2,1,0:T(8,128)(2,1)} %collective-permute-done.5.refs_2_, pred[]{:T(512)S(6)} %eq.5), kind=kLoop, calls=%fused_computation.4 | loop fusion | flops 786432 | bytes 4718593 | tf_op jit(solution)/shard_map/jit(_where)/select_n | solution.py:51
  146.0 1.9 collective-permute-start.7
  147.9 67.1 %collective-permute-done.1.refs_1_ = bf16[2,2,128,1536]{3,2,1,0:T(8,128)(2,1)S(1)} collective-permute-done((bf16[2,2,128,1536]{3,2,1,0:T(8,128)(2,1)}, bf16[2,2,128,1536]{3,2,1,0:T(8,128)(2,1)S(1)}, u32[]{:S(2)}, u32[]{:S(2)}) %collective-permute-start.1) | collective-permute-done | bytes 1572896 | tf_op jit(solution)/shard_map/ppermute | solution.py:18
  215.1 0.1 slice.9
  215.1 0.0 collective-permute-done.refs_0_
  215.1 0.1 slice.8
  215.2 0.0 copy-start.4
  215.2 1.3 pad_maximum_fusion.1
  216.5 1.9 collective-permute-start.3
  218.4 3.6 %collective-permute-start.2 = (bf16[2,2,128,1536]{3,2,1,0:T(8,128)(2,1)}, bf16[2,2,128,1536]{3,2,1,0:T(8,128)(2,1)}, u32[]{:S(2)}, u32[]{:S(2)}) collective-permute-start(bf16[2,2,128,1536]{3,2,1,0:T(8,128)(2,1)} %pad_maximum_fusion.1), channel_id=1, source_target_pairs={{1,0},{2,1},{3,2},{4,3},{5,4},{6,5},{7,6},{8,7},{9,8},{10,9},{11,1... | collective-permute-start | bytes 4718600 | tf_op jit(solution)/shard_map/ppermute | solution.py:18
  222.1 0.0 copy-done.4
  222.1 0.1 reshape_squeeze.3.flags_ref
  222.2 0.0 copy-start.3
  222.2 0.0 collective-permute-done.6
  222.2 0.0 collective-permute-done.7
  222.2 3.8 %broadcast_select_fusion = (bf16[2,2,128,1536]{3,2,1,0:T(8,128)(2,1)}, bf16[2,2,128,1536]{3,2,1,0:T(8,128)(2,1)}) fusion(bf16[2,2,128,1536]{3,2,1,0:T(8,128)(2,1)} %collective-permute-done.7, bf16[2,2,128,1536]{3,2,1,0:T(8,128)(2,1)} %collective-permute-done.6, pred[]{:T(512)S(6)} %eq.5), kind=kLoop, calls=%fused_computation.2 | loop fusion | flops 1572864 | bytes 6291457 | tf_op jit(solution)/shard_map/jit(_where)/select_n | solution.py:53
  226.0 0.0 copy-done.3
  226.0 17.0 %shard_map.46 = (f32[12,2,128,1]{3,2,1,0:T(8,128)S(1)}, f32[12,2,128,1]{3,2,1,0:T(8,128)S(1)}, f32[2,128,1536]{2,1,0:T(8,128)S(1)}) custom-call(s32[50]{0:T(128)S(1)} %reshape_squeeze.3.flags_ref, bf16[2,128,1536]{2,1,0:T(8,128)(2,1)S(1)} %copy-done.3, bf16[2,2,128,1536]{3,2,1,0:T(8,128)(2,1)} %pad_maximum_fusion.refs_0_, ...), custom_call_target="tpu_custom_call" | custom-call | flops 3221225472 | bytes 10223616 | tf_op jit(solution)/shard_map/pallas_call | solution.py:174
  243.0 0.0 copy-start
  243.0 1.2 copy-done
  244.2 0.0 copy-start.1
  244.2 1.1 copy-done.1
  245.3 0.0 copy-start.2
  245.3 1.2 copy-done.2
  246.5 8.9 %collective-permute-done.3.refs_3_ = bf16[2,2,128,1536]{3,2,1,0:T(8,128)(2,1)} collective-permute-done((bf16[2,2,128,1536]{3,2,1,0:T(8,128)(2,1)}, bf16[2,2,128,1536]{3,2,1,0:T(8,128)(2,1)}, u32[]{:S(2)}, u32[]{:S(2)}) %collective-permute-start.3) | collective-permute-done | bytes 1572896 | tf_op jit(solution)/shard_map/ppermute | solution.py:18
  255.4 0.0 collective-permute-done.2.refs_2_
  255.4 17.5 %shard_map.47 = bf16[2,128,1536]{2,1,0:T(8,128)(2,1)} custom-call(s32[50]{0:T(128)S(1)} %reshape_squeeze.3.flags_ref, bf16[2,128,1536]{2,1,0:T(8,128)(2,1)S(1)} %copy-done.3, bf16[2,2,128,1536]{3,2,1,0:T(8,128)(2,1)S(1)} %collective-permute-done.refs_0_, bf16[2,2,128,1536]{3,2,1,0:T(8,128)(2,1)S(1)} %collective-permute-done.1.refs_1_, ...), custom_call_target="tpu_custom_call" | custom-call | flops 2013265920 | bytes 8650752 | tf_op jit(solution)/shard_map/pallas_call | solution.py:182
  (1 shorter events, 0.0 us)
Async XLA Ops:
  2.7 140.6 %collective-permute-start.5 = (bf16[2,2,128,1536]{3,2,1,0:T(8,128)(2,1)}, bf16[2,2,128,1536]{3,2,1,0:T(8,128)(2,1)}, u32[]{:S(2)}, u32[]{:S(2)}) collective-permute-start(bf16[2,2,128,1536]{3,2,1,0:T(8,128)(2,1)} %pad_maximum_fusion.refs_0_), channel_id=1, source_target_pairs={{0,2},{1,3},{2,4},{3,5},{4,6},{5,7},{6,8},{7,9},{8,10},{9,11},{10,... | collective-permute-start | bytes 4718600 | tf_op jit(solution)/shard_map/ppermute | solution.py:18
  4.6 138.7 %collective-permute-start.4 = (bf16[2,2,128,1536]{3,2,1,0:T(8,128)(2,1)}, bf16[2,2,128,1536]{3,2,1,0:T(8,128)(2,1)}, u32[]{:S(2)}, u32[]{:S(2)}) collective-permute-start(bf16[2,2,128,1536]{3,2,1,0:T(8,128)(2,1)} %pad_maximum_fusion.refs_0_), channel_id=1, source_target_pairs={{2,0},{3,1},{4,2},{5,3},{6,4},{7,5},{8,6},{9,7},{10,8},{11,9},{12,... | collective-permute-start | bytes 4718600 | tf_op jit(solution)/shard_map/ppermute | solution.py:18
  8.5 206.5 %collective-permute-start.1 = (bf16[2,2,128,1536]{3,2,1,0:T(8,128)(2,1)}, bf16[2,2,128,1536]{3,2,1,0:T(8,128)(2,1)S(1)}, u32[]{:S(2)}, u32[]{:S(2)}) collective-permute-start(bf16[2,2,128,1536]{3,2,1,0:T(8,128)(2,1)} %pad_maximum_fusion.refs_0_), channel_id=1, source_target_pairs={{32,0},{64,32},{96,64},{128,96},{160,128},{192,160},{224,192},{256... | collective-permute-start | bytes 4718600 | tf_op jit(solution)/shard_map/ppermute | solution.py:18
  11.3 203.8 %collective-permute-start = (bf16[2,2,128,1536]{3,2,1,0:T(8,128)(2,1)}, bf16[2,2,128,1536]{3,2,1,0:T(8,128)(2,1)S(1)}, u32[]{:S(2)}, u32[]{:S(2)}) collective-permute-start(bf16[2,2,128,1536]{3,2,1,0:T(8,128)(2,1)} %pad_maximum_fusion.refs_0_), channel_id=1, source_target_pairs={{0,32},{32,64},{64,96},{96,128},{128,160},{160,192},{192,224},{224... | collective-permute-start | bytes 4718600 | tf_op jit(solution)/shard_map/ppermute | solution.py:18
  20.4 201.8 %collective-permute-start.6 = (bf16[2,2,128,1536]{3,2,1,0:T(8,128)(2,1)}, bf16[2,2,128,1536]{3,2,1,0:T(8,128)(2,1)}, u32[]{:S(2)}, u32[]{:S(2)}) collective-permute-start(bf16[2,2,128,1536]{3,2,1,0:T(8,128)(2,1)} %pad_maximum_fusion.refs_0_), channel_id=1, source_target_pairs={{0,1},{1,0},{2,3},{3,2},{4,5},{5,4},{6,7},{7,6},{8,9},{9,8},{10,11... | collective-permute-start | bytes 4718600 | tf_op jit(solution)/shard_map/ppermute | solution.py:40
  146.0 76.2 %collective-permute-start.7 = (bf16[2,2,128,1536]{3,2,1,0:T(8,128)(2,1)}, bf16[2,2,128,1536]{3,2,1,0:T(8,128)(2,1)}, u32[]{:S(2)}, u32[]{:S(2)}) collective-permute-start(bf16[2,2,128,1536]{3,2,1,0:T(8,128)(2,1)} %broadcast_select_fusion.2), channel_id=1, source_target_pairs={{0,1},{1,0},{2,3},{3,2},{4,5},{5,4},{6,7},{7,6},{8,9},{9,8},{10,11... | collective-permute-start | bytes 4718600 | tf_op jit(solution)/shard_map/ppermute | solution.py:40
  215.2 6.9 %copy-start.4 = (s32[2,1,5,5]{3,1,2,0:T(1,128)S(1)}, s32[2,1,5,5]{3,1,2,0:T(1,128)}, u32[]{:S(2)}) copy-start(s32[2,1,5,5]{3,1,2,0:T(1,128)} %param.7) | copy-start | bytes 604
  216.5 38.9 %collective-permute-start.3 = (bf16[2,2,128,1536]{3,2,1,0:T(8,128)(2,1)}, bf16[2,2,128,1536]{3,2,1,0:T(8,128)(2,1)}, u32[]{:S(2)}, u32[]{:S(2)}) collective-permute-start(bf16[2,2,128,1536]{3,2,1,0:T(8,128)(2,1)} %pad_maximum_fusion.1), channel_id=1, source_target_pairs={{0,1},{1,2},{2,3},{3,4},{4,5},{5,6},{6,7},{7,8},{8,9},{9,10},{10,1... | collective-permute-start | bytes 4718600 | tf_op jit(solution)/shard_map/ppermute | solution.py:18
  218.4 37.0 %collective-permute-start.2 = (bf16[2,2,128,1536]{3,2,1,0:T(8,128)(2,1)}, bf16[2,2,128,1536]{3,2,1,0:T(8,128)(2,1)}, u32[]{:S(2)}, u32[]{:S(2)}) collective-permute-start(bf16[2,2,128,1536]{3,2,1,0:T(8,128)(2,1)} %pad_maximum_fusion.1), channel_id=1, source_target_pairs={{1,0},{2,1},{3,2},{4,3},{5,4},{6,5},{7,6},{8,7},{9,8},{10,9},{11,1... | collective-permute-start | bytes 4718600 | tf_op jit(solution)/shard_map/ppermute | solution.py:18
  222.2 3.8 %copy-start.3 = (bf16[2,128,1536]{2,1,0:T(8,128)(2,1)S(1)}, bf16[2,128,1536]{2,1,0:T(8,128)(2,1)}, u32[]{:S(2)}) copy-start(bf16[2,128,1536]{2,1,0:T(8,128)(2,1)} %q_ref.3) | copy-start | bytes 2359300
  243.0 1.2 copy-start
  244.2 1.1 copy-start.1
  245.3 1.2 copy-start.2

commit v9 on v7

--- a/solution.py
+++ b/solution.py
@@ -51,10 +51,13 @@
     partner_far = swap_cores(jnp.where(core_zero, far_next, far_prev))
     near_next = jnp.where(core_zero, partner_own, partner_far)
     near_prev = jnp.where(core_zero, partner_far, partner_own)
-    band = jnp.concatenate([earlier[:, TR - 1 :], following[:, :1]], axis=1)
-    diag_next = shifted(band, "space", -1)
-    diag_prev = shifted(band, "space", 1)
-    return (stacked, earlier, following, far_next, far_prev, near_next, near_prev, diag_next, diag_prev)
+    early_band = earlier[:, TR - 1 :]
+    late_band = following[:, :1]
+    return (
+        stacked, earlier, following, far_next, far_prev, near_next, near_prev,
+        shifted(early_band, "space", -1), shifted(early_band, "space", 1),
+        shifted(late_band, "space", -1), shifted(late_band, "space", 1),
+    )
 
 
 def locate(frame, d, e):
@@ -66,18 +69,18 @@
             return 0, offset
         return 2, offset - 2
     if abs(e) == 1:
-        near, diag = (5, 7) if e > 0 else (6, 8)
+        side = 0 if e > 0 else 1
         if offset < 0:
-            return diag, 0
+            return 7 + side, 0
         if offset < 2:
-            return near, offset
-        return diag, 1
+            return 5 + side, offset
+        return 9 + side, 0
     return (3 if e > 0 else 4), frame
 
 
 LOCAL = (0, 3, 4, 5, 6)
 HEAD_GROUP = 4
-REMOTE = (1, 2, 7, 8)
+REMOTE = (1, 2, 7, 8, 9, 10)
 
 
 def scored_pairs(flags_ref, query, sources, frame, kept_sources, lanes):
@@ -154,7 +157,9 @@
     group = HEAD_GROUP
     steps = head_count // group
     flags = tile_flags.reshape(-1).astype(jnp.int32)
-    source_spec = pl.BlockSpec((2, 2, row_count, group * HD), lambda h, flags: (0, 0, 0, h))
+    def source_spec(source):
+        return pl.BlockSpec((2, source.shape[1], row_count, group * HD), lambda h, flags: (0, 0, 0, h))
+
     tile_spec = pl.BlockSpec((frame_count, row_count, group * HD), lambda h, flags: (0, 0, h))
     stat_spec = pl.BlockSpec((group, frame_count, row_count, 1), lambda h, flags: (h, 0, 0, 0))
     stat_shape = jax.ShapeDtypeStruct((head_count, frame_count, row_count, 1), jnp.float32)
@@ -174,7 +179,7 @@
         grid_spec=pltpu.PrefetchScalarGridSpec(
             num_scalar_prefetch=1,
             grid=(steps,),
-            in_specs=[tile_spec] + [source_spec] * len(local_sources),
+            in_specs=[tile_spec] + [source_spec(s) for s in local_sources],
             out_specs=[stat_spec, stat_spec, tile_spec],
         ),
         out_shape=[stat_shape, stat_shape, acc_shape],
@@ -185,7 +190,7 @@
         grid_spec=pltpu.PrefetchScalarGridSpec(
             num_scalar_prefetch=1,
             grid=(steps,),
-            in_specs=[tile_spec] + [source_spec] * len(remote_sources)
+            in_specs=[tile_spec] + [source_spec(s) for s in remote_sources]
             + [stat_spec, stat_spec, tile_spec],
             out_specs=tile_spec,
         ),

time: 273 us -> 271 us (level)
  waiting for transfers between devices: 203 us -> 196 us
  starting transfers between devices: 27.1 us -> 32.6 us
    ppermute x6 -> x8, waiting for transfers between devices: 203 us -> 196 us  [shifted(): return lax.ppermute(block, axis, route)]
    ppermute x6 -> x8, starting transfers between devices: 23.2 us -> 28.8 us  [shifted(): return lax.ppermute(block, axis, route)]
  transfers between devices with their start and end apart: 8 -> 10, of which waited for: 3 -> 4; matrix products, arithmetic and copies ran while one was open for 3% -> 3% of each run, Pallas kernels for 5% -> 5%
where the time goes in v9:
time: 271 us
  waiting for transfers between devices  196 us (72%)
  starting transfers between devices  32.6 us (12%)
  Pallas kernels  29.2 us (11%)
  other arithmetic  9.16 us (3%)
  local copies, waits for them, and re-layouts  3.57 us (1%)
    ppermute x8, waiting for transfers between devices, shifted(): return lax.ppermute(block, axis, route)  196 us
    ppermute x8, starting transfers between devices, shifted(): return lax.ppermute(block, axis, route)  28.8 us
    pallas_call x1, Pallas kernels, attend(): pl.pallas_call(remote_kernel, grid_spec=pltpu.PrefetchScalarGridSpec(num_...  14.9 us
    pallas_call x1, Pallas kernels, attend(): pl.pallas_call(local_kernel, grid_spec=pltpu.PrefetchScalarGridSpec(num_s...  14.3 us
  transfers between devices with their start and end apart: 10, of which 4 were waited for; matrix products, arithmetic and copies ran while one was open for 3% of the time, Pallas kernels for 5%

profile of v9, /device:TPU:118, one launch (start us, length us, event | category | flops | bytes accessed | tf_op | source)
XLA Modules:
  0.0 270.8 jit_solution(17127660005607531781)
XLA Ops:
  0.0 2.7 pad_maximum_fusion.refs_0_
  2.7 1.9 collective-permute-start.7
  4.6 3.9 %collective-permute-start.6 = (bf16[2,2,128,1536]{3,2,1,0:T(8,128)(2,1)}, bf16[2,2,128,1536]{3,2,1,0:T(8,128)(2,1)}, u32[]{:S(2)}, u32[]{:S(2)}) collective-permute-start(bf16[2,2,128,1536]{3,2,1,0:T(8,128)(2,1)} %pad_maximum_fusion.refs_0_), channel_id=1, source_target_pairs={{2,0},{3,1},{4,2},{5,3},{6,4},{7,5},{8,6},{9,7},{10,8},{11,9},{12,... | collective-permute-start | bytes 4718600 | tf_op jit(solution)/shard_map/ppermute | solution.py:18
  8.5 1.9 collective-permute-start.8
  10.4 2.7 %collective-permute-start.1 = (bf16[2,2,128,1536]{3,2,1,0:T(8,128)(2,1)}, bf16[2,2,128,1536]{3,2,1,0:T(8,128)(2,1)S(1)}, u32[]{:S(2)}, u32[]{:S(2)}) collective-permute-start(bf16[2,2,128,1536]{3,2,1,0:T(8,128)(2,1)} %pad_maximum_fusion.refs_0_), channel_id=1, source_target_pairs={{32,0},{64,32},{96,64},{128,96},{160,128},{192,160},{224,192},{256... | collective-permute-start | bytes 4718600 | tf_op jit(solution)/shard_map/ppermute | solution.py:18
  13.2 9.1 %collective-permute-start = (bf16[2,2,128,1536]{3,2,1,0:T(8,128)(2,1)}, bf16[2,2,128,1536]{3,2,1,0:T(8,128)(2,1)S(1)}, u32[]{:S(2)}, u32[]{:S(2)}) collective-permute-start(bf16[2,2,128,1536]{3,2,1,0:T(8,128)(2,1)} %pad_maximum_fusion.refs_0_), channel_id=1, source_target_pairs={{0,32},{32,64},{64,96},{96,128},{128,160},{160,192},{192,224},{224... | collective-permute-start | bytes 4718600 | tf_op jit(solution)/shard_map/ppermute | solution.py:18
  22.3 0.0 copy-start.3
  22.3 120.9 %collective-permute-done.7.refs_2_ = bf16[2,2,128,1536]{3,2,1,0:T(8,128)(2,1)} collective-permute-done((bf16[2,2,128,1536]{3,2,1,0:T(8,128)(2,1)}, bf16[2,2,128,1536]{3,2,1,0:T(8,128)(2,1)}, u32[]{:S(2)}, u32[]{:S(2)}) %collective-permute-start.7) | collective-permute-done | bytes 1572896 | tf_op jit(solution)/shard_map/ppermute | solution.py:18
  143.2 0.0 collective-permute-done.6.refs_1_
  143.2 2.7 %broadcast_select_fusion.2 = bf16[2,2,128,1536]{3,2,1,0:T(8,128)(2,1)} fusion(bf16[2,2,128,1536]{3,2,1,0:T(8,128)(2,1)} %collective-permute-done.6.refs_1_, bf16[2,2,128,1536]{3,2,1,0:T(8,128)(2,1)} %collective-permute-done.7.refs_2_, pred[]{:T(512)S(6)} %eq.5), kind=kLoop, calls=%fused_computation.3 | loop fusion | flops 786432 | bytes 4718593 | tf_op jit(solution)/shard_map/jit(_where)/select_n | solution.py:51
  146.0 1.9 collective-permute-start.9
  147.9 0.0 copy-done.3
  147.9 0.7 reshape_squeeze.3.flags_ref
  148.6 66.5 %collective-permute-done.1.refs_1_ = bf16[2,2,128,1536]{3,2,1,0:T(8,128)(2,1)S(1)} collective-permute-done((bf16[2,2,128,1536]{3,2,1,0:T(8,128)(2,1)}, bf16[2,2,128,1536]{3,2,1,0:T(8,128)(2,1)S(1)}, u32[]{:S(2)}, u32[]{:S(2)}) %collective-permute-start.1) | collective-permute-done | bytes 1572896 | tf_op jit(solution)/shard_map/ppermute | solution.py:18
  215.1 0.0 copy-start
  215.1 1.0 slice.9
  216.1 1.9 collective-permute-start.5
  218.0 3.6 %collective-permute-start.4 = (bf16[2,1,128,1536]{3,2,1,0:T(8,128)(2,1)}, bf16[2,1,128,1536]{3,2,1,0:T(8,128)(2,1)}, u32[]{:S(2)}, u32[]{:S(2)}) collective-permute-start(bf16[2,1,128,1536]{3,2,1,0:T(8,128)(2,1)} %slice.9), channel_id=1, source_target_pairs={{1,0},{2,1},{3,2},{4,3},{5,4},{6,5},{7,6},{8,7},{9,8},{10,9},{11,1... | collective-permute-start | bytes 2359304 | tf_op jit(solution)/shard_map/ppermute | solution.py:18
  221.7 0.0 collective-permute-done.refs_0_
  221.7 0.0 copy-start.1
  221.7 1.0 slice.8
  222.7 0.0 copy-done
  222.7 1.9 collective-permute-start.3
  224.6 0.0 collective-permute-done.8
  224.6 3.6 %collective-permute-start.2 = (bf16[2,1,128,1536]{3,2,1,0:T(8,128)(2,1)}, bf16[2,1,128,1536]{3,2,1,0:T(8,128)(2,1)S(1)}, u32[]{:S(2)}, u32[]{:S(2)}) collective-permute-start(bf16[2,1,128,1536]{3,2,1,0:T(8,128)(2,1)} %slice.8), channel_id=1, source_target_pairs={{1,0},{2,1},{3,2},{4,3},{5,4},{6,5},{7,6},{8,7},{9,8},{10,9},{11,1... | collective-permute-start | bytes 2359304 | tf_op jit(solution)/shard_map/ppermute | solution.py:18
  228.3 0.0 collective-permute-done.9
  228.3 3.7 %broadcast_select_fusion = (bf16[2,2,128,1536]{3,2,1,0:T(8,128)(2,1)}, bf16[2,2,128,1536]{3,2,1,0:T(8,128)(2,1)}) fusion(bf16[2,2,128,1536]{3,2,1,0:T(8,128)(2,1)} %collective-permute-done.9, bf16[2,2,128,1536]{3,2,1,0:T(8,128)(2,1)} %collective-permute-done.8, pred[]{:T(512)S(6)} %eq.5), kind=kLoop, calls=%fused_computation.1 | loop fusion | flops 1572864 | bytes 6291457 | tf_op jit(solution)/shard_map/jit(_where)/select_n | solution.py:53
  232.0 0.0 copy-done.1
  232.0 14.3 %shard_map.46 = (f32[12,2,128,1]{3,2,1,0:T(8,128)}, f32[12,2,128,1]{3,2,1,0:T(8,128)}, f32[2,128,1536]{2,1,0:T(8,128)}) custom-call(s32[50]{0:T(128)} %reshape_squeeze.3.flags_ref, bf16[2,128,1536]{2,1,0:T(8,128)(2,1)} %q_ref.3, bf16[2,2,128,1536]{3,2,1,0:T(8,128)(2,1)} %pad_maximum_fusion.refs_0_, bf16[2,2,128,1536]{3,2,1,0:T(8,128)(2,1)} %collective-permute-done.6.refs_1_, ...), custom_call_target="tpu_custom_call" | custom-call | flops 3221225472 | bytes 10223616 | tf_op jit(solution)/shard_map/pallas_call | solution.py:177
  246.3 0.2 collective-permute-done.5.refs_5_
  246.6 0.0 collective-permute-done.4.refs_4_
  246.6 8.4 %collective-permute-done.3.refs_3_ = bf16[2,1,128,1536]{3,2,1,0:T(8,128)(2,1)} collective-permute-done((bf16[2,1,128,1536]{3,2,1,0:T(8,128)(2,1)}, bf16[2,1,128,1536]{3,2,1,0:T(8,128)(2,1)}, u32[]{:S(2)}, u32[]{:S(2)}) %collective-permute-start.3) | collective-permute-done | bytes 786464 | tf_op jit(solution)/shard_map/ppermute | solution.py:18
  255.0 0.0 collective-permute-done.2.refs_2_
  255.0 0.0 copy-start.2
  255.0 0.9 copy-done.2
  255.9 14.9 %shard_map.47 = bf16[2,128,1536]{2,1,0:T(8,128)(2,1)} custom-call(s32[50]{0:T(128)} %reshape_squeeze.3.flags_ref, bf16[2,128,1536]{2,1,0:T(8,128)(2,1)} %q_ref.3, bf16[2,2,128,1536]{3,2,1,0:T(8,128)(2,1)} %copy-done.1, bf16[2,2,128,1536]{3,2,1,0:T(8,128)(2,1)} %copy-done, bf16[2,1,128,1536]{3,2,1,0:T(8,128)(2,1)} %copy-done.2, ...), custom_call_target="tpu_custom_call" | custom-call | flops 2013265920 | bytes 11796480 | tf_op jit(solution)/shard_map/pallas_call | solution.py:188
  (1 shorter events, 0.0 us)
Async XLA Ops:
  2.7 140.6 %collective-permute-start.7 = (bf16[2,2,128,1536]{3,2,1,0:T(8,128)(2,1)}, bf16[2,2,128,1536]{3,2,1,0:T(8,128)(2,1)}, u32[]{:S(2)}, u32[]{:S(2)}) collective-permute-start(bf16[2,2,128,1536]{3,2,1,0:T(8,128)(2,1)} %pad_maximum_fusion.refs_0_), channel_id=1, source_target_pairs={{0,2},{1,3},{2,4},{3,5},{4,6},{5,7},{6,8},{7,9},{8,10},{9,11},{10,... | collective-permute-start | bytes 4718600 | tf_op jit(solution)/shard_map/ppermute | solution.py:18
  4.6 138.7 %collective-permute-start.6 = (bf16[2,2,128,1536]{3,2,1,0:T(8,128)(2,1)}, bf16[2,2,128,1536]{3,2,1,0:T(8,128)(2,1)}, u32[]{:S(2)}, u32[]{:S(2)}) collective-permute-start(bf16[2,2,128,1536]{3,2,1,0:T(8,128)(2,1)} %pad_maximum_fusion.refs_0_), channel_id=1, source_target_pairs={{2,0},{3,1},{4,2},{5,3},{6,4},{7,5},{8,6},{9,7},{10,8},{11,9},{12,... | collective-permute-start | bytes 4718600 | tf_op jit(solution)/shard_map/ppermute | solution.py:18
  8.5 216.1 %collective-permute-start.8 = (bf16[2,2,128,1536]{3,2,1,0:T(8,128)(2,1)}, bf16[2,2,128,1536]{3,2,1,0:T(8,128)(2,1)}, u32[]{:S(2)}, u32[]{:S(2)}) collective-permute-start(bf16[2,2,128,1536]{3,2,1,0:T(8,128)(2,1)} %pad_maximum_fusion.refs_0_), channel_id=1, source_target_pairs={{0,1},{1,0},{2,3},{3,2},{4,5},{5,4},{6,7},{7,6},{8,9},{9,8},{10,11... | collective-permute-start | bytes 4718600 | tf_op jit(solution)/shard_map/ppermute | solution.py:40
  10.4 204.6 %collective-permute-start.1 = (bf16[2,2,128,1536]{3,2,1,0:T(8,128)(2,1)}, bf16[2,2,128,1536]{3,2,1,0:T(8,128)(2,1)S(1)}, u32[]{:S(2)}, u32[]{:S(2)}) collective-permute-start(bf16[2,2,128,1536]{3,2,1,0:T(8,128)(2,1)} %pad_maximum_fusion.refs_0_), channel_id=1, source_target_pairs={{32,0},{64,32},{96,64},{128,96},{160,128},{192,160},{224,192},{256... | collective-permute-start | bytes 4718600 | tf_op jit(solution)/shard_map/ppermute | solution.py:18
  13.2 208.5 %collective-permute-start = (bf16[2,2,128,1536]{3,2,1,0:T(8,128)(2,1)}, bf16[2,2,128,1536]{3,2,1,0:T(8,128)(2,1)S(1)}, u32[]{:S(2)}, u32[]{:S(2)}) collective-permute-start(bf16[2,2,128,1536]{3,2,1,0:T(8,128)(2,1)} %pad_maximum_fusion.refs_0_), channel_id=1, source_target_pairs={{0,32},{32,64},{64,96},{96,128},{128,160},{160,192},{192,224},{224... | collective-permute-start | bytes 4718600 | tf_op jit(solution)/shard_map/ppermute | solution.py:18
  22.3 125.6 %copy-start.3 = (s32[2,1,5,5]{3,1,2,0:T(1,128)S(1)}, s32[2,1,5,5]{3,1,2,0:T(1,128)}, u32[]{:S(2)}) copy-start(s32[2,1,5,5]{3,1,2,0:T(1,128)} %param.7) | copy-start | bytes 604
  146.0 82.3 %collective-permute-start.9 = (bf16[2,2,128,1536]{3,2,1,0:T(8,128)(2,1)}, bf16[2,2,128,1536]{3,2,1,0:T(8,128)(2,1)}, u32[]{:S(2)}, u32[]{:S(2)}) collective-permute-start(bf16[2,2,128,1536]{3,2,1,0:T(8,128)(2,1)} %broadcast_select_fusion.2), channel_id=1, source_target_pairs={{0,1},{1,0},{2,3},{3,2},{4,5},{5,4},{6,7},{7,6},{8,9},{9,8},{10,11... | collective-permute-start | bytes 4718600 | tf_op jit(solution)/shard_map/ppermute | solution.py:40
  215.1 7.6 %copy-start = (bf16[2,2,128,1536]{3,2,1,0:T(8,128)(2,1)}, bf16[2,2,128,1536]{3,2,1,0:T(8,128)(2,1)S(1)}, u32[]{:S(2)}) copy-start(bf16[2,2,128,1536]{3,2,1,0:T(8,128)(2,1)S(1)} %collective-permute-done.1.refs_1_) | copy-start | bytes 4718596
  216.1 30.5 %collective-permute-start.5 = (bf16[2,1,128,1536]{3,2,1,0:T(8,128)(2,1)}, bf16[2,1,128,1536]{3,2,1,0:T(8,128)(2,1)}, u32[]{:S(2)}, u32[]{:S(2)}) collective-permute-start(bf16[2,1,128,1536]{3,2,1,0:T(8,128)(2,1)} %slice.9), channel_id=1, source_target_pairs={{0,1},{1,2},{2,3},{3,4},{4,5},{5,6},{6,7},{7,8},{8,9},{9,10},{10,1... | collective-permute-start | bytes 2359304 | tf_op jit(solution)/shard_map/ppermute | solution.py:18
  218.0 28.6 %collective-permute-start.4 = (bf16[2,1,128,1536]{3,2,1,0:T(8,128)(2,1)}, bf16[2,1,128,1536]{3,2,1,0:T(8,128)(2,1)}, u32[]{:S(2)}, u32[]{:S(2)}) collective-permute-start(bf16[2,1,128,1536]{3,2,1,0:T(8,128)(2,1)} %slice.9), channel_id=1, source_target_pairs={{1,0},{2,1},{3,2},{4,3},{5,4},{6,5},{7,6},{8,7},{9,8},{10,9},{11,1... | collective-permute-start | bytes 2359304 | tf_op jit(solution)/shard_map/ppermute | solution.py:18
  221.7 10.4 %copy-start.1 = (bf16[2,2,128,1536]{3,2,1,0:T(8,128)(2,1)}, bf16[2,2,128,1536]{3,2,1,0:T(8,128)(2,1)S(1)}, u32[]{:S(2)}) copy-start(bf16[2,2,128,1536]{3,2,1,0:T(8,128)(2,1)S(1)} %collective-permute-done.refs_0_) | copy-start | bytes 4718596
  222.7 32.3 %collective-permute-start.3 = (bf16[2,1,128,1536]{3,2,1,0:T(8,128)(2,1)}, bf16[2,1,128,1536]{3,2,1,0:T(8,128)(2,1)}, u32[]{:S(2)}, u32[]{:S(2)}) collective-permute-start(bf16[2,1,128,1536]{3,2,1,0:T(8,128)(2,1)} %slice.8), channel_id=1, source_target_pairs={{0,1},{1,2},{2,3},{3,4},{4,5},{5,6},{6,7},{7,8},{8,9},{9,10},{10,1... | collective-permute-start | bytes 2359304 | tf_op jit(solution)/shard_map/ppermute | solution.py:18
  224.6 30.3 %collective-permute-start.2 = (bf16[2,1,128,1536]{3,2,1,0:T(8,128)(2,1)}, bf16[2,1,128,1536]{3,2,1,0:T(8,128)(2,1)S(1)}, u32[]{:S(2)}, u32[]{:S(2)}) collective-permute-start(bf16[2,1,128,1536]{3,2,1,0:T(8,128)(2,1)} %slice.8), channel_id=1, source_target_pairs={{1,0},{2,1},{3,2},{4,3},{5,4},{6,5},{7,6},{8,7},{9,8},{10,9},{11,1... | collective-permute-start | bytes 2359304 | tf_op jit(solution)/shard_map/ppermute | solution.py:18
  255.0 0.9 copy-start.2

commit v10 on v9

--- a/solution.py
+++ b/solution.py
@@ -35,6 +35,40 @@
     return best
 
 
+X_CHIPS = 4
+
+
+def routed(pairs, block):
+    return lax.ppermute(block, "tm", pairs) if pairs else jnp.zeros_like(block)
+
+
+def relayed(block, hops):
+    for pairs in hops:
+        block = routed(pairs, block)
+    return block
+
+
+def tm_shift(block, step):
+    count = lax.axis_size("tm")
+    x = X_CHIPS
+    if step > 0:
+        edge = [t for t in range(count - 1) if t % x == x - 1]
+        direct = [(t, t + 1) for t in range(count - 1) if t not in edge]
+        via_two = [[(t, t - 1) for t in edge], [(t - 1, t + 3) for t in edge], [(t + 3, t + 1) for t in edge]]
+        via_one = [[(t, t - 2) for t in edge], [(t - 2, t + 2) for t in edge], [(t + 2, t + 1) for t in edge]]
+    else:
+        edge = [t for t in range(1, count) if t % x == 0]
+        direct = [(t, t - 1) for t in range(1, count) if t not in edge]
+        via_one = [[(t, t + 1) for t in edge], [(t + 1, t - 3) for t in edge], [(t - 3, t - 1) for t in edge]]
+        via_two = [[(t, t + 2) for t in edge], [(t + 2, t - 2) for t in edge], [(t - 2, t - 1) for t in edge]]
+    plain = routed(direct, block)
+    keys_part = relayed(block[:1], via_one)
+    values_part = relayed(block[1:], via_two)
+    position = lax.axis_index("tm") % x
+    at_edge = position == (0 if step > 0 else x - 1)
+    return jnp.where(at_edge, jnp.concatenate([keys_part, values_part], axis=0), plain)
+
+
 def swap_cores(block):
     devices = range(lax.axis_size("space"))
     return lax.ppermute(block, "space", [(i, i ^ 1) for i in devices])
@@ -42,8 +76,8 @@
 
 def fetch_sources(stacked):
     frame_count = stacked.shape[1]
-    earlier = shifted(stacked[:, frame_count - TR :], "tm", 1)
-    following = shifted(stacked[:, :TR], "tm", -1)
+    earlier = tm_shift(stacked[:, frame_count - TR :], 1)
+    following = tm_shift(stacked[:, :TR], -1)
     far_next = shifted(stacked, "space", -2)
     far_prev = shifted(stacked, "space", 2)
     core_zero = lax.axis_index("space") % 2 == 0

time: 271 us -> 240 us (0.89)
  the two profiles are of different devices: /device:TPU:118 before, /device:TPU:417 now
where the time goes in v10:
time: 240 us; the launch traced here: 239 us
  waiting for transfers between devices  113 us (47%)
  starting transfers between devices  82.1 us (34%)
  Pallas kernels  29.2 us (12%)
  other arithmetic  10 us (4%)
  local copies, waits for them, and re-layouts  4.4 us (2%)
    ppermute x14, waiting for transfers between devices, routed(): return lax.ppermute(block, 'tm', pairs) if pairs else jnp.zeros_like(block)  107 us
    ppermute x14, starting transfers between devices, routed(): return lax.ppermute(block, 'tm', pairs) if pairs else jnp.zeros_like(block)  52.4 us
    ppermute x6, starting transfers between devices, shifted(): return lax.ppermute(block, axis, route)  21.5 us
    pallas_call x1, Pallas kernels, attend(): pl.pallas_call(remote_kernel, grid_spec=pltpu.PrefetchScalarGridSpec(num_...  14.9 us
    pallas_call x1, Pallas kernels, attend(): pl.pallas_call(local_kernel, grid_spec=pltpu.PrefetchScalarGridSpec(num_s...  14.3 us
    ppermute x2, starting transfers between devices, swap_cores(): return lax.ppermute(block, 'space', [(i, i ^ 1) for i in devices])  8.18 us
    ppermute x6, waiting for transfers between devices, shifted(): return lax.ppermute(block, axis, route)  5.9 us
  transfers between devices with their start and end apart: 22, of which 8 were waited for; matrix products, arithmetic and copies ran while one was open for 5% of the time, Pallas kernels for 6%

profile of v10, /device:TPU:417, one launch (start us, length us, event | category | flops | bytes accessed | tf_op | source)
XLA Modules:
  0.0 239.1 jit_solution(13047564518277971756)
XLA Ops:
  0.0 5.5 %collective-permute-start.10 = (bf16[1,2,128,1536]{3,2,1,0:T(8,128)(2,1)}, bf16[1,2,128,1536]{3,2,1,0:T(8,128)(2,1)}, u32[]{:S(2)}, u32[]{:S(2)}) collective-permute-start(bf16[1,2,128,1536]{3,2,1,0:T(8,128)(2,1)} %bitcast.5), channel_id=1, source_target_pairs={{128,192},{256,320},{384,448},{129,193},{257,321},{385,449},{130,1... | collective-permute-start | bytes 2359304 | tf_op jit(solution)/shard_map/ppermute | solution.py:42
  5.6 2.4 collective-permute-start.7
  7.9 2.7 %pad_maximum_fusion.refs_0_ = bf16[2,2,128,1536]{3,2,1,0:T(8,128)(2,1)} fusion(bf16[1,2,128,1536]{3,2,1,0:T(8,128)(2,1)} %bitcast.6, bf16[1,2,128,1536]{3,2,1,0:T(8,128)(2,1)} %bitcast.3), kind=kLoop, calls=%fused_computation.1 | loop fusion | flops 786432 | bytes 3145728 | tf_op jit(solution)/shard_map/stack | solution.py:237
  10.6 2.6 %collective-permute-start.18 = (bf16[2,2,128,1536]{3,2,1,0:T(8,128)(2,1)}, bf16[2,2,128,1536]{3,2,1,0:T(8,128)(2,1)S(1)}, u32[]{:S(2)}, u32[]{:S(2)}) collective-permute-start(bf16[2,2,128,1536]{3,2,1,0:T(8,128)(2,1)} %pad_maximum_fusion.refs_0_), channel_id=1, source_target_pairs={{2,0},{3,1},{4,2},{5,3},{6,4},{7,5},{8,6},{9,7},{10,8},{11,9},{12,... | collective-permute-start | bytes 4718600 | tf_op jit(solution)/shard_map/ppermute | solution.py:18
  13.2 2.6 %collective-permute-start.19 = (bf16[2,2,128,1536]{3,2,1,0:T(8,128)(2,1)}, bf16[2,2,128,1536]{3,2,1,0:T(8,128)(2,1)S(1)}, u32[]{:S(2)}, u32[]{:S(2)}) collective-permute-start(bf16[2,2,128,1536]{3,2,1,0:T(8,128)(2,1)} %pad_maximum_fusion.refs_0_), channel_id=1, source_target_pairs={{0,2},{1,3},{2,4},{3,5},{4,6},{5,7},{6,8},{7,9},{8,10},{9,11},{10,... | collective-permute-start | bytes 4718600 | tf_op jit(solution)/shard_map/ppermute | solution.py:18
  15.9 1.3 collective-permute-start.13
  17.2 4.0 %collective-permute-done.10 = bf16[1,2,128,1536]{3,2,1,0:T(8,128)(2,1)} collective-permute-done((bf16[1,2,128,1536]{3,2,1,0:T(8,128)(2,1)}, bf16[1,2,128,1536]{3,2,1,0:T(8,128)(2,1)}, u32[]{:S(2)}, u32[]{:S(2)}) %collective-permute-start.10) | collective-permute-done | bytes 786464 | tf_op jit(solution)/shard_map/ppermute | solution.py:42
  21.2 1.6 collective-permute-start
  22.7 15.3 %collective-permute-done.7 = bf16[1,2,128,1536]{3,2,1,0:T(8,128)(2,1)} collective-permute-done((bf16[1,2,128,1536]{3,2,1,0:T(8,128)(2,1)}, bf16[1,2,128,1536]{3,2,1,0:T(8,128)(2,1)}, u32[]{:S(2)}, u32[]{:S(2)}) %collective-permute-start.7) | collective-permute-done | bytes 786464 | tf_op jit(solution)/shard_map/ppermute | solution.py:42
  38.0 1.6 collective-permute-start.3
  39.6 0.0 collective-permute-done
  39.6 1.6 collective-permute-start.11
  41.1 1.5 collective-permute-start.8
  42.7 5.1 %collective-permute-done.18.refs_1_ = bf16[2,2,128,1536]{3,2,1,0:T(8,128)(2,1)S(1)} collective-permute-done((bf16[2,2,128,1536]{3,2,1,0:T(8,128)(2,1)}, bf16[2,2,128,1536]{3,2,1,0:T(8,128)(2,1)S(1)}, u32[]{:S(2)}, u32[]{:S(2)}) %collective-permute-start.18) | collective-permute-done | bytes 1572896 | tf_op jit(solution)/shard_map/ppermute | solution.py:18
  47.8 1.6 collective-permute-start.1
  49.4 0.8 collective-permute-done.19.refs_2_
  50.2 1.5 collective-permute-start.4
  51.7 0.8 collective-permute-done.13
  52.5 28.1 %collective-permute-start.6 = (bf16[2,2,128,1536]{3,2,1,0:T(8,128)(2,1)}, bf16[2,2,128,1536]{3,2,1,0:T(8,128)(2,1)}, u32[]{:S(2)}, u32[]{:S(2)}) collective-permute-start(bf16[2,2,128,1536]{3,2,1,0:T(8,128)(2,1)} %pad_maximum_fusion.refs_0_), channel_id=1, source_target_pairs={{0,32},{32,64},{64,96},{128,160},{160,192},{192,224},{256,288},{28... | collective-permute-start | bytes 4718600 | tf_op jit(solution)/shard_map/ppermute | solution.py:42
  80.6 0.0 collective-permute-done.11
  80.6 1.6 collective-permute-start.12
  82.2 0.0 collective-permute-done.8
  82.2 1.6 collective-permute-start.9
  83.8 1.3 broadcast_select_fusion.2
  85.1 0.0 collective-permute-done.1
  85.1 6.3 %collective-permute-start.20 = (bf16[2,2,128,1536]{3,2,1,0:T(8,128)(2,1)}, bf16[2,2,128,1536]{3,2,1,0:T(8,128)(2,1)}, u32[]{:S(2)}, u32[]{:S(2)}) collective-permute-start(bf16[2,2,128,1536]{3,2,1,0:T(8,128)(2,1)} %pad_maximum_fusion.refs_0_), channel_id=1, source_target_pairs={{0,1},{1,0},{2,3},{3,2},{4,5},{5,4},{6,7},{7,6},{8,9},{9,8},{10,11... | collective-permute-start | bytes 4718600 | tf_op jit(solution)/shard_map/ppermute | solution.py:74
  91.4 1.9 collective-permute-start.21
  93.3 1.3 collective-permute-start.2
  94.6 1.3 collective-permute-start.5
  96.0 0.7 reshape_squeeze.3.flags_ref
  96.7 2.0 maximum_select_fusion.1.refs_1_
  98.7 1.0 slice.9
  99.8 9.7 %collective-permute-done.6 = bf16[2,2,128,1536]{3,2,1,0:T(8,128)(2,1)} collective-permute-done((bf16[2,2,128,1536]{3,2,1,0:T(8,128)(2,1)}, bf16[2,2,128,1536]{3,2,1,0:T(8,128)(2,1)}, u32[]{:S(2)}, u32[]{:S(2)}) %collective-permute-start.6) | collective-permute-done | bytes 1572896 | tf_op jit(solution)/shard_map/ppermute | solution.py:42
  109.5 6.8 %collective-permute-start.16 = (bf16[2,1,128,1536]{3,2,1,0:T(8,128)(2,1)}, bf16[2,1,128,1536]{3,2,1,0:T(8,128)(2,1)S(1)}, u32[]{:S(2)}, u32[]{:S(2)}) collective-permute-start(bf16[2,1,128,1536]{3,2,1,0:T(8,128)(2,1)} %slice.9), channel_id=1, source_target_pairs={{1,0},{2,1},{3,2},{4,3},{5,4},{6,5},{7,6},{8,7},{9,8},{10,9},{11,1... | collective-permute-start | bytes 2359304 | tf_op jit(solution)/shard_map/ppermute | solution.py:18
  116.3 39.1 %collective-permute-done.2 = bf16[1,2,128,1536]{3,2,1,0:T(8,128)(2,1)S(1)} collective-permute-done((bf16[1,2,128,1536]{3,2,1,0:T(8,128)(2,1)}, bf16[1,2,128,1536]{3,2,1,0:T(8,128)(2,1)S(1)}, u32[]{:S(2)}, u32[]{:S(2)}) %collective-permute-start.2) | collective-permute-done | bytes 786464 | tf_op jit(solution)/shard_map/ppermute | solution.py:42
  155.4 3.9 %collective-permute-start.17 = (bf16[2,1,128,1536]{3,2,1,0:T(8,128)(2,1)}, bf16[2,1,128,1536]{3,2,1,0:T(8,128)(2,1)S(1)}, u32[]{:S(2)}, u32[]{:S(2)}) collective-permute-start(bf16[2,1,128,1536]{3,2,1,0:T(8,128)(2,1)} %slice.9), channel_id=1, source_target_pairs={{0,1},{1,2},{2,3},{3,4},{4,5},{5,6},{6,7},{7,8},{8,9},{9,10},{10,1... | collective-permute-start | bytes 2359304 | tf_op jit(solution)/shard_map/ppermute | solution.py:18
  159.3 38.3 %collective-permute-done.5 = bf16[1,2,128,1536]{3,2,1,0:T(8,128)(2,1)S(1)} collective-permute-done((bf16[1,2,128,1536]{3,2,1,0:T(8,128)(2,1)}, bf16[1,2,128,1536]{3,2,1,0:T(8,128)(2,1)S(1)}, u32[]{:S(2)}, u32[]{:S(2)}) %collective-permute-start.5) | collective-permute-done | bytes 786464 | tf_op jit(solution)/shard_map/ppermute | solution.py:42
  197.6 0.2 maximum_select_fusion.refs_0_
  197.8 1.0 slice.8
  198.8 2.5 %collective-permute-start.14 = (bf16[2,1,128,1536]{3,2,1,0:T(8,128)(2,1)}, bf16[2,1,128,1536]{3,2,1,0:T(8,128)(2,1)S(1)}, u32[]{:S(2)}, u32[]{:S(2)}) collective-permute-start(bf16[2,1,128,1536]{3,2,1,0:T(8,128)(2,1)} %slice.8), channel_id=1, source_target_pairs={{1,0},{2,1},{3,2},{4,3},{5,4},{6,5},{7,6},{8,7},{9,8},{10,9},{11,1... | collective-permute-start | bytes 2359304 | tf_op jit(solution)/shard_map/ppermute | solution.py:18
  201.4 3.1 %collective-permute-start.15 = (bf16[2,1,128,1536]{3,2,1,0:T(8,128)(2,1)}, bf16[2,1,128,1536]{3,2,1,0:T(8,128)(2,1)S(1)}, u32[]{:S(2)}, u32[]{:S(2)}) collective-permute-start(bf16[2,1,128,1536]{3,2,1,0:T(8,128)(2,1)} %slice.8), channel_id=1, source_target_pairs={{0,1},{1,2},{2,3},{3,4},{4,5},{5,6},{6,7},{7,8},{8,9},{9,10},{10,1... | collective-permute-start | bytes 2359304 | tf_op jit(solution)/shard_map/ppermute | solution.py:18
  204.4 3.7 %broadcast_select_fusion = (bf16[2,2,128,1536]{3,2,1,0:T(8,128)(2,1)}, bf16[2,2,128,1536]{3,2,1,0:T(8,128)(2,1)}) fusion(bf16[2,2,128,1536]{3,2,1,0:T(8,128)(2,1)} %collective-permute-done.21, bf16[2,2,128,1536]{3,2,1,0:T(8,128)(2,1)} %collective-permute-done.20, pred[]{:T(512)S(6)} %eq.15), kind=kLoop, calls=%fused_computation.3 | loop fusion | flops 1572864 | bytes 6291457 | tf_op jit(solution)/shard_map/jit(_where)/select_n | solution.py:87
  208.2 14.3 %shard_map.46 = (f32[12,2,128,1]{3,2,1,0:T(8,128)}, f32[12,2,128,1]{3,2,1,0:T(8,128)}, f32[2,128,1536]{2,1,0:T(8,128)}) custom-call(s32[50]{0:T(128)} %reshape_squeeze.3.flags_ref, bf16[2,128,1536]{2,1,0:T(8,128)(2,1)} %q_ref.3, bf16[2,2,128,1536]{3,2,1,0:T(8,128)(2,1)} %pad_maximum_fusion.refs_0_, bf16[2,2,128,1536]{3,2,1,0:T(8,128)(2,1)} %copy-done.2, ...), custom_call_target="tpu_custom_call" | custom-call | flops 3221225472 | bytes 10223616 | tf_op jit(solution)/shard_map/pallas_call | solution.py:211
  222.5 0.9 copy-done.4
  223.4 0.3 copy-done.5
  223.7 0.3 copy-done.6
  224.0 0.2 copy-done.7
  224.2 14.9 %shard_map.47 = bf16[2,128,1536]{2,1,0:T(8,128)(2,1)} custom-call(s32[50]{0:T(128)} %reshape_squeeze.3.flags_ref, bf16[2,128,1536]{2,1,0:T(8,128)(2,1)} %q_ref.3, bf16[2,2,128,1536]{3,2,1,0:T(8,128)(2,1)} %copy-done.1, bf16[2,2,128,1536]{3,2,1,0:T(8,128)(2,1)} %copy-done, bf16[2,1,128,1536]{3,2,1,0:T(8,128)(2,1)} %copy-done.6, ...), custom_call_target="tpu_custom_call" | custom-call | flops 2013265920 | bytes 11796480 | tf_op jit(solution)/shard_map/pallas_call | solution.py:222
  (29 shorter events, 0.1 us)
Async XLA Ops:
  0.0 21.2 %collective-permute-start.10 = (bf16[1,2,128,1536]{3,2,1,0:T(8,128)(2,1)}, bf16[1,2,128,1536]{3,2,1,0:T(8,128)(2,1)}, u32[]{:S(2)}, u32[]{:S(2)}) collective-permute-start(bf16[1,2,128,1536]{3,2,1,0:T(8,128)(2,1)} %bitcast.5), channel_id=1, source_target_pairs={{128,192},{256,320},{384,448},{129,193},{257,321},{385,449},{130,1... | collective-permute-start | bytes 2359304 | tf_op jit(solution)/shard_map/ppermute | solution.py:42
  5.5 15.6 %copy-start.8 = (bf16[2,128,1536]{2,1,0:T(8,128)(2,1)S(1)}, bf16[2,128,1536]{2,1,0:T(8,128)(2,1)}, u32[]{:S(2)}) copy-start(bf16[2,128,1536]{2,1,0:T(8,128)(2,1)} %param.5) | copy-start | bytes 2359300
  5.5 32.5 %copy-start.9 = (bf16[2,128,1536]{2,1,0:T(8,128)(2,1)S(1)}, bf16[2,128,1536]{2,1,0:T(8,128)(2,1)}, u32[]{:S(2)}) copy-start(bf16[2,128,1536]{2,1,0:T(8,128)(2,1)} %param.6) | copy-start | bytes 2359300
  5.6 32.5 %collective-permute-start.7 = (bf16[1,2,128,1536]{3,2,1,0:T(8,128)(2,1)}, bf16[1,2,128,1536]{3,2,1,0:T(8,128)(2,1)}, u32[]{:S(2)}, u32[]{:S(2)}) collective-permute-start(bf16[1,2,128,1536]{3,2,1,0:T(8,128)(2,1)} %bitcast.2), channel_id=1, source_target_pairs={{128,160},{256,288},{384,416},{129,161},{257,289},{385,417},{130,1... | collective-permute-start | bytes 2359304 | tf_op jit(solution)/shard_map/ppermute | solution.py:42
  10.6 37.2 %collective-permute-start.18 = (bf16[2,2,128,1536]{3,2,1,0:T(8,128)(2,1)}, bf16[2,2,128,1536]{3,2,1,0:T(8,128)(2,1)S(1)}, u32[]{:S(2)}, u32[]{:S(2)}) collective-permute-start(bf16[2,2,128,1536]{3,2,1,0:T(8,128)(2,1)} %pad_maximum_fusion.refs_0_), channel_id=1, source_target_pairs={{2,0},{3,1},{4,2},{5,3},{6,4},{7,5},{8,6},{9,7},{10,8},{11,9},{12,... | collective-permute-start | bytes 4718600 | tf_op jit(solution)/shard_map/ppermute | solution.py:18
  13.2 36.9 %collective-permute-start.19 = (bf16[2,2,128,1536]{3,2,1,0:T(8,128)(2,1)}, bf16[2,2,128,1536]{3,2,1,0:T(8,128)(2,1)S(1)}, u32[]{:S(2)}, u32[]{:S(2)}) collective-permute-start(bf16[2,2,128,1536]{3,2,1,0:T(8,128)(2,1)} %pad_maximum_fusion.refs_0_), channel_id=1, source_target_pairs={{0,2},{1,3},{2,4},{3,5},{4,6},{5,7},{6,8},{7,9},{8,10},{9,11},{10,... | collective-permute-start | bytes 4718600 | tf_op jit(solution)/shard_map/ppermute | solution.py:18
  15.9 36.6 %collective-permute-start.13 = (bf16[2,2,128,1536]{3,2,1,0:T(8,128)(2,1)}, bf16[2,2,128,1536]{3,2,1,0:T(8,128)(2,1)}, u32[]{:S(2)}, u32[]{:S(2)}) collective-permute-start(bf16[2,2,128,1536]{3,2,1,0:T(8,128)(2,1)} %pad_maximum_fusion.refs_0_), channel_id=1, source_target_pairs={{32,0},{64,32},{96,64},{160,128},{192,160},{224,192},{288,256},{32... | collective-permute-start | bytes 4718600 | tf_op jit(solution)/shard_map/ppermute | solution.py:42
  21.2 18.4 %collective-permute-start = (bf16[1,2,128,1536]{3,2,1,0:T(8,128)(2,1)S(1)}, bf16[1,2,128,1536]{3,2,1,0:T(8,128)(2,1)}, u32[]{:S(2)}, u32[]{:S(2)}) collective-permute-start(bf16[1,2,128,1536]{3,2,1,0:T(8,128)(2,1)S(1)} %bitcast.4), channel_id=1, source_target_pairs={{96,32},{224,160},{352,288},{97,33},{225,161},{353,289},{98,34},{2... | collective-permute-start | bytes 2359304 | tf_op jit(solution)/shard_map/ppermute | solution.py:42
  38.0 3.1 %collective-permute-start.3 = (bf16[1,2,128,1536]{3,2,1,0:T(8,128)(2,1)S(1)}, bf16[1,2,128,1536]{3,2,1,0:T(8,128)(2,1)}, u32[]{:S(2)}, u32[]{:S(2)}) collective-permute-start(bf16[1,2,128,1536]{3,2,1,0:T(8,128)(2,1)S(1)} %bitcast.7), channel_id=1, source_target_pairs={{96,64},{224,192},{352,320},{97,65},{225,193},{353,321},{98,66},{2... | collective-permute-start | bytes 2359304 | tf_op jit(solution)/shard_map/ppermute | solution.py:42
  39.6 41.1 %collective-permute-start.11 = (bf16[1,2,128,1536]{3,2,1,0:T(8,128)(2,1)}, bf16[1,2,128,1536]{3,2,1,0:T(8,128)(2,1)}, u32[]{:S(2)}, u32[]{:S(2)}) collective-permute-start(bf16[1,2,128,1536]{3,2,1,0:T(8,128)(2,1)} %collective-permute-done.10), channel_id=1, source_target_pairs={{192,64},{320,192},{448,320},{193,65},{321,193},{449,321},{194,66}... | collective-permute-start | bytes 2359304 | tf_op jit(solution)/shard_map/ppermute | solution.py:42
  41.1 41.1 %collective-permute-start.8 = (bf16[1,2,128,1536]{3,2,1,0:T(8,128)(2,1)}, bf16[1,2,128,1536]{3,2,1,0:T(8,128)(2,1)}, u32[]{:S(2)}, u32[]{:S(2)}) collective-permute-start(bf16[1,2,128,1536]{3,2,1,0:T(8,128)(2,1)} %collective-permute-done.7), channel_id=1, source_target_pairs={{160,32},{288,160},{416,288},{161,33},{289,161},{417,289},{162,34}... | collective-permute-start | bytes 2359304 | tf_op jit(solution)/shard_map/ppermute | solution.py:42
  47.8 37.3 %copy-start.2 = (bf16[2,2,128,1536]{3,2,1,0:T(8,128)(2,1)}, bf16[2,2,128,1536]{3,2,1,0:T(8,128)(2,1)S(1)}, u32[]{:S(2)}) copy-start(bf16[2,2,128,1536]{3,2,1,0:T(8,128)(2,1)S(1)} %collective-permute-done.18.refs_1_) | copy-start | bytes 4718596
  47.8 37.3 %collective-permute-start.1 = (bf16[1,2,128,1536]{3,2,1,0:T(8,128)(2,1)}, bf16[1,2,128,1536]{3,2,1,0:T(8,128)(2,1)}, u32[]{:S(2)}, u32[]{:S(2)}) collective-permute-start(bf16[1,2,128,1536]{3,2,1,0:T(8,128)(2,1)} %collective-permute-done), channel_id=1, source_target_pairs={{32,160},{160,288},{288,416},{33,161},{161,289},{289,417},{34,162}... | collective-permute-start | bytes 2359304 | tf_op jit(solution)/shard_map/ppermute | solution.py:42
  50.2 34.9 %copy-start.3 = (bf16[2,2,128,1536]{3,2,1,0:T(8,128)(2,1)}, bf16[2,2,128,1536]{3,2,1,0:T(8,128)(2,1)S(1)}, u32[]{:S(2)}) copy-start(bf16[2,2,128,1536]{3,2,1,0:T(8,128)(2,1)S(1)} %collective-permute-done.19.refs_2_) | copy-start | bytes 4718596
  50.2 41.2 %collective-permute-start.4 = (bf16[1,2,128,1536]{3,2,1,0:T(8,128)(2,1)}, bf16[1,2,128,1536]{3,2,1,0:T(8,128)(2,1)}, u32[]{:S(2)}, u32[]{:S(2)}) collective-permute-start(bf16[1,2,128,1536]{3,2,1,0:T(8,128)(2,1)} %collective-permute-done.3), channel_id=1, source_target_pairs={{64,192},{192,320},{320,448},{65,193},{193,321},{321,449},{66,194}... | collective-permute-start | bytes 2359304 | tf_op jit(solution)/shard_map/ppermute | solution.py:42
  51.7 44.2 %copy-start.10 = (s32[2,1,5,5]{3,1,2,0:T(1,128)S(1)}, s32[2,1,5,5]{3,1,2,0:T(1,128)}, u32[]{:S(2)}) copy-start(s32[2,1,5,5]{3,1,2,0:T(1,128)} %param.7) | copy-start | bytes 604
  52.5 56.9 %collective-permute-start.6 = (bf16[2,2,128,1536]{3,2,1,0:T(8,128)(2,1)}, bf16[2,2,128,1536]{3,2,1,0:T(8,128)(2,1)}, u32[]{:S(2)}, u32[]{:S(2)}) collective-permute-start(bf16[2,2,128,1536]{3,2,1,0:T(8,128)(2,1)} %pad_maximum_fusion.refs_0_), channel_id=1, source_target_pairs={{0,32},{32,64},{64,96},{128,160},{160,192},{192,224},{256,288},{28... | collective-permute-start | bytes 4718600 | tf_op jit(solution)/shard_map/ppermute | solution.py:42
  80.6 12.7 %collective-permute-start.12 = (bf16[1,2,128,1536]{3,2,1,0:T(8,128)(2,1)}, bf16[1,2,128,1536]{3,2,1,0:T(8,128)(2,1)}, u32[]{:S(2)}, u32[]{:S(2)}) collective-permute-start(bf16[1,2,128,1536]{3,2,1,0:T(8,128)(2,1)} %collective-permute-done.11), channel_id=1, source_target_pairs={{64,96},{192,224},{320,352},{65,97},{193,225},{321,353},{66,98},{1... | collective-permute-start | bytes 2359304 | tf_op jit(solution)/shard_map/ppermute | solution.py:42
  82.2 12.4 %collective-permute-start.9 = (bf16[1,2,128,1536]{3,2,1,0:T(8,128)(2,1)}, bf16[1,2,128,1536]{3,2,1,0:T(8,128)(2,1)}, u32[]{:S(2)}, u32[]{:S(2)}) collective-permute-start(bf16[1,2,128,1536]{3,2,1,0:T(8,128)(2,1)} %collective-permute-done.8), channel_id=1, source_target_pairs={{32,96},{160,224},{288,352},{33,97},{161,225},{289,353},{34,98},{1... | collective-permute-start | bytes 2359304 | tf_op jit(solution)/shard_map/ppermute | solution.py:42
  85.1 116.2 %collective-permute-start.20 = (bf16[2,2,128,1536]{3,2,1,0:T(8,128)(2,1)}, bf16[2,2,128,1536]{3,2,1,0:T(8,128)(2,1)}, u32[]{:S(2)}, u32[]{:S(2)}) collective-permute-start(bf16[2,2,128,1536]{3,2,1,0:T(8,128)(2,1)} %pad_maximum_fusion.refs_0_), channel_id=1, source_target_pairs={{0,1},{1,0},{2,3},{3,2},{4,5},{5,4},{6,7},{7,6},{8,9},{9,8},{10,11... | collective-permute-start | bytes 4718600 | tf_op jit(solution)/shard_map/ppermute | solution.py:74
  91.4 113.0 %collective-permute-start.21 = (bf16[2,2,128,1536]{3,2,1,0:T(8,128)(2,1)}, bf16[2,2,128,1536]{3,2,1,0:T(8,128)(2,1)}, u32[]{:S(2)}, u32[]{:S(2)}) collective-permute-start(bf16[2,2,128,1536]{3,2,1,0:T(8,128)(2,1)} %broadcast_select_fusion.2), channel_id=1, source_target_pairs={{0,1},{1,0},{2,3},{3,2},{4,5},{5,4},{6,7},{7,6},{8,9},{9,8},{10,11... | collective-permute-start | bytes 4718600 | tf_op jit(solution)/shard_map/ppermute | solution.py:74
  93.3 62.1 %collective-permute-start.2 = (bf16[1,2,128,1536]{3,2,1,0:T(8,128)(2,1)}, bf16[1,2,128,1536]{3,2,1,0:T(8,128)(2,1)S(1)}, u32[]{:S(2)}, u32[]{:S(2)}) collective-permute-start(bf16[1,2,128,1536]{3,2,1,0:T(8,128)(2,1)} %collective-permute-done.1), channel_id=1, source_target_pairs={{160,128},{288,256},{416,384},{161,129},{289,257},{417,385},{162,1... | collective-permute-start | bytes 2359304 | tf_op jit(solution)/shard_map/ppermute | solution.py:42
  94.6 103.0 %collective-permute-start.5 = (bf16[1,2,128,1536]{3,2,1,0:T(8,128)(2,1)}, bf16[1,2,128,1536]{3,2,1,0:T(8,128)(2,1)S(1)}, u32[]{:S(2)}, u32[]{:S(2)}) collective-permute-start(bf16[1,2,128,1536]{3,2,1,0:T(8,128)(2,1)} %collective-permute-done.4), channel_id=1, source_target_pairs={{192,128},{320,256},{448,384},{193,129},{321,257},{449,385},{194,1... | collective-permute-start | bytes 2359304 | tf_op jit(solution)/shard_map/ppermute | solution.py:42
  98.7 99.1 %copy-start = (bf16[2,2,128,1536]{3,2,1,0:T(8,128)(2,1)}, bf16[2,2,128,1536]{3,2,1,0:T(8,128)(2,1)S(1)}, u32[]{:S(2)}) copy-start(bf16[2,2,128,1536]{3,2,1,0:T(8,128)(2,1)S(1)} %maximum_select_fusion.1.refs_1_) | copy-start | bytes 4718596
  109.5 113.0 %collective-permute-start.16 = (bf16[2,1,128,1536]{3,2,1,0:T(8,128)(2,1)}, bf16[2,1,128,1536]{3,2,1,0:T(8,128)(2,1)S(1)}, u32[]{:S(2)}, u32[]{:S(2)}) collective-permute-start(bf16[2,1,128,1536]{3,2,1,0:T(8,128)(2,1)} %slice.9), channel_id=1, source_target_pairs={{1,0},{2,1},{3,2},{4,3},{5,4},{6,5},{7,6},{8,7},{9,8},{10,9},{11,1... | collective-permute-start | bytes 2359304 | tf_op jit(solution)/shard_map/ppermute | solution.py:18
  155.4 67.1 %collective-permute-start.17 = (bf16[2,1,128,1536]{3,2,1,0:T(8,128)(2,1)}, bf16[2,1,128,1536]{3,2,1,0:T(8,128)(2,1)S(1)}, u32[]{:S(2)}, u32[]{:S(2)}) collective-permute-start(bf16[2,1,128,1536]{3,2,1,0:T(8,128)(2,1)} %slice.9), channel_id=1, source_target_pairs={{0,1},{1,2},{2,3},{3,4},{4,5},{5,6},{6,7},{7,8},{8,9},{9,10},{10,1... | collective-permute-start | bytes 2359304 | tf_op jit(solution)/shard_map/ppermute | solution.py:18
  197.8 10.3 %copy-start.1 = (bf16[2,2,128,1536]{3,2,1,0:T(8,128)(2,1)}, bf16[2,2,128,1536]{3,2,1,0:T(8,128)(2,1)S(1)}, u32[]{:S(2)}) copy-start(bf16[2,2,128,1536]{3,2,1,0:T(8,128)(2,1)S(1)} %maximum_select_fusion.refs_0_) | copy-start | bytes 4718596
  198.8 23.7 %collective-permute-start.14 = (bf16[2,1,128,1536]{3,2,1,0:T(8,128)(2,1)}, bf16[2,1,128,1536]{3,2,1,0:T(8,128)(2,1)S(1)}, u32[]{:S(2)}, u32[]{:S(2)}) collective-permute-start(bf16[2,1,128,1536]{3,2,1,0:T(8,128)(2,1)} %slice.8), channel_id=1, source_target_pairs={{1,0},{2,1},{3,2},{4,3},{5,4},{6,5},{7,6},{8,7},{9,8},{10,9},{11,1... | collective-permute-start | bytes 2359304 | tf_op jit(solution)/shard_map/ppermute | solution.py:18
  201.4 21.2 %collective-permute-start.15 = (bf16[2,1,128,1536]{3,2,1,0:T(8,128)(2,1)}, bf16[2,1,128,1536]{3,2,1,0:T(8,128)(2,1)S(1)}, u32[]{:S(2)}, u32[]{:S(2)}) collective-permute-start(bf16[2,1,128,1536]{3,2,1,0:T(8,128)(2,1)} %slice.8), channel_id=1, source_target_pairs={{0,1},{1,2},{2,3},{3,4},{4,5},{5,6},{6,7},{7,8},{8,9},{9,10},{10,1... | collective-permute-start | bytes 2359304 | tf_op jit(solution)/shard_map/ppermute | solution.py:18
  222.5 0.9 copy-start.4
  222.5 1.2 copy-start.5
  222.5 1.5 copy-start.6
  222.5 1.7 copy-start.7

commit v11 on v10

--- a/solution.py
+++ b/solution.py
@@ -6,6 +6,7 @@
 from jax.experimental import pallas as pl
 from jax.experimental.pallas import tpu as pltpu
 from jax.sharding import PartitionSpec as P
+
 
 HD = 128
 TR = 2
@@ -25,14 +26,6 @@
         for e in range(-spread, spread + 1):
             pairs.append((d, e))
     return pairs
-
-
-def frame_reach(e):
-    best = 0
-    for d in range(TR + 1):
-        if W >> d >= abs(e):
-            best = d
-    return best
 
 
 X_CHIPS = 4
@@ -191,6 +184,7 @@
     group = HEAD_GROUP
     steps = head_count // group
     flags = tile_flags.reshape(-1).astype(jnp.int32)
+
     def source_spec(source):
         return pl.BlockSpec((2, source.shape[1], row_count, group * HD), lambda h, flags: (0, 0, 0, h))
 
@@ -208,7 +202,7 @@
             bytes_accessed=(2 + 4 * extra + 4) * frame_count * row_count * feature_width,
         )
 
-    stats = pl.pallas_call(
+    local_call = pl.pallas_call(
         local_kernel,
         grid_spec=pltpu.PrefetchScalarGridSpec(
             num_scalar_prefetch=1,
@@ -218,7 +212,8 @@
         ),
         out_shape=[stat_shape, stat_shape, acc_shape],
         cost_estimate=cost(16, len(local_sources)),
-    )(flags, queries, *local_sources)
+    )
+    stats = local_call(flags, queries, *local_sources)
     return pl.pallas_call(
         remote_kernel,
         grid_spec=pltpu.PrefetchScalarGridSpec(

time: 240 us -> 240 us (level)
  no operation moved by 1% of the time
where the time goes in v11:
time: 240 us; the launch traced here: 239 us
  waiting for transfers between devices  113 us (47%)
  starting transfers between devices  82.1 us (34%)
  Pallas kernels  29.2 us (12%)
  other arithmetic  10 us (4%)
  local copies, waits for them, and re-layouts  4.4 us (2%)
    ppermute x14, waiting for transfers between devices, routed(): return lax.ppermute(block, 'tm', pairs) if pairs else jnp.zeros_like(block)  107 us
    ppermute x14, starting transfers between devices, routed(): return lax.ppermute(block, 'tm', pairs) if pairs else jnp.zeros_like(block)  52.4 us
    ppermute x6, starting transfers between devices, shifted(): return lax.ppermute(block, axis, route)  21.5 us
    pallas_call x1, Pallas kernels, attend(): pl.pallas_call(remote_kernel, grid_spec=pltpu.PrefetchScalarGridSpec(num_...  14.9 us
    pallas_call x1, Pallas kernels, attend(): stats = local_call(flags, queries, *local_sources)  14.3 us
    ppermute x2, starting transfers between devices, swap_cores(): return lax.ppermute(block, 'space', [(i, i ^ 1) for i in devices])  8.18 us
    ppermute x6, waiting for transfers between devices, shifted(): return lax.ppermute(block, axis, route)  5.9 us
  transfers between devices with their start and end apart: 22, of which 8 were waited for; matrix products, arithmetic and copies ran while one was open for 5% of the time, Pallas kernels for 6%

profile of v11, /device:TPU:417, one launch (start us, length us, event | category | flops | bytes accessed | tf_op | source)
XLA Modules:
  0.0 239.1 jit_solution(13047564518277971756)
XLA Ops:
  0.0 5.5 %collective-permute-start.10 = (bf16[1,2,128,1536]{3,2,1,0:T(8,128)(2,1)}, bf16[1,2,128,1536]{3,2,1,0:T(8,128)(2,1)}, u32[]{:S(2)}, u32[]{:S(2)}) collective-permute-start(bf16[1,2,128,1536]{3,2,1,0:T(8,128)(2,1)} %bitcast.5), channel_id=1, source_target_pairs={{128,192},{256,320},{384,448},{129,193},{257,321},{385,449},{130,1... | collective-permute-start | bytes 2359304 | tf_op jit(solution)/shard_map/ppermute | solution.py:35
  5.6 2.4 collective-permute-start.7
  7.9 2.7 %pad_maximum_fusion.refs_0_ = bf16[2,2,128,1536]{3,2,1,0:T(8,128)(2,1)} fusion(bf16[1,2,128,1536]{3,2,1,0:T(8,128)(2,1)} %bitcast.6, bf16[1,2,128,1536]{3,2,1,0:T(8,128)(2,1)} %bitcast.3), kind=kLoop, calls=%fused_computation.1 | loop fusion | flops 786432 | bytes 3145728 | tf_op jit(solution)/shard_map/stack | solution.py:232
  10.6 2.6 %collective-permute-start.18 = (bf16[2,2,128,1536]{3,2,1,0:T(8,128)(2,1)}, bf16[2,2,128,1536]{3,2,1,0:T(8,128)(2,1)S(1)}, u32[]{:S(2)}, u32[]{:S(2)}) collective-permute-start(bf16[2,2,128,1536]{3,2,1,0:T(8,128)(2,1)} %pad_maximum_fusion.refs_0_), channel_id=1, source_target_pairs={{2,0},{3,1},{4,2},{5,3},{6,4},{7,5},{8,6},{9,7},{10,8},{11,9},{12,... | collective-permute-start | bytes 4718600 | tf_op jit(solution)/shard_map/ppermute | solution.py:19
  13.2 2.6 %collective-permute-start.19 = (bf16[2,2,128,1536]{3,2,1,0:T(8,128)(2,1)}, bf16[2,2,128,1536]{3,2,1,0:T(8,128)(2,1)S(1)}, u32[]{:S(2)}, u32[]{:S(2)}) collective-permute-start(bf16[2,2,128,1536]{3,2,1,0:T(8,128)(2,1)} %pad_maximum_fusion.refs_0_), channel_id=1, source_target_pairs={{0,2},{1,3},{2,4},{3,5},{4,6},{5,7},{6,8},{7,9},{8,10},{9,11},{10,... | collective-permute-start | bytes 4718600 | tf_op jit(solution)/shard_map/ppermute | solution.py:19
  15.9 1.3 collective-permute-start.13
  17.2 4.0 %collective-permute-done.10 = bf16[1,2,128,1536]{3,2,1,0:T(8,128)(2,1)} collective-permute-done((bf16[1,2,128,1536]{3,2,1,0:T(8,128)(2,1)}, bf16[1,2,128,1536]{3,2,1,0:T(8,128)(2,1)}, u32[]{:S(2)}, u32[]{:S(2)}) %collective-permute-start.10) | collective-permute-done | bytes 786464 | tf_op jit(solution)/shard_map/ppermute | solution.py:35
  21.2 1.6 collective-permute-start
  22.7 15.3 %collective-permute-done.7 = bf16[1,2,128,1536]{3,2,1,0:T(8,128)(2,1)} collective-permute-done((bf16[1,2,128,1536]{3,2,1,0:T(8,128)(2,1)}, bf16[1,2,128,1536]{3,2,1,0:T(8,128)(2,1)}, u32[]{:S(2)}, u32[]{:S(2)}) %collective-permute-start.7) | collective-permute-done | bytes 786464 | tf_op jit(solution)/shard_map/ppermute | solution.py:35
  38.0 1.6 collective-permute-start.3
  39.6 0.0 collective-permute-done
  39.6 1.6 collective-permute-start.11
  41.1 1.5 collective-permute-start.8
  42.7 5.1 %collective-permute-done.18.refs_1_ = bf16[2,2,128,1536]{3,2,1,0:T(8,128)(2,1)S(1)} collective-permute-done((bf16[2,2,128,1536]{3,2,1,0:T(8,128)(2,1)}, bf16[2,2,128,1536]{3,2,1,0:T(8,128)(2,1)S(1)}, u32[]{:S(2)}, u32[]{:S(2)}) %collective-permute-start.18) | collective-permute-done | bytes 1572896 | tf_op jit(solution)/shard_map/ppermute | solution.py:19
  47.8 1.6 collective-permute-start.1
  49.4 0.8 collective-permute-done.19.refs_2_
  50.2 1.5 collective-permute-start.4
  51.7 0.8 collective-permute-done.13
  52.5 28.1 %collective-permute-start.6 = (bf16[2,2,128,1536]{3,2,1,0:T(8,128)(2,1)}, bf16[2,2,128,1536]{3,2,1,0:T(8,128)(2,1)}, u32[]{:S(2)}, u32[]{:S(2)}) collective-permute-start(bf16[2,2,128,1536]{3,2,1,0:T(8,128)(2,1)} %pad_maximum_fusion.refs_0_), channel_id=1, source_target_pairs={{0,32},{32,64},{64,96},{128,160},{160,192},{192,224},{256,288},{28... | collective-permute-start | bytes 4718600 | tf_op jit(solution)/shard_map/ppermute | solution.py:35
  80.6 0.0 collective-permute-done.11
  80.6 1.6 collective-permute-start.12
  82.2 0.0 collective-permute-done.8
  82.2 1.6 collective-permute-start.9
  83.8 1.3 broadcast_select_fusion.2
  85.1 0.0 collective-permute-done.1
  85.1 6.3 %collective-permute-start.20 = (bf16[2,2,128,1536]{3,2,1,0:T(8,128)(2,1)}, bf16[2,2,128,1536]{3,2,1,0:T(8,128)(2,1)}, u32[]{:S(2)}, u32[]{:S(2)}) collective-permute-start(bf16[2,2,128,1536]{3,2,1,0:T(8,128)(2,1)} %pad_maximum_fusion.refs_0_), channel_id=1, source_target_pairs={{0,1},{1,0},{2,3},{3,2},{4,5},{5,4},{6,7},{7,6},{8,9},{9,8},{10,11... | collective-permute-start | bytes 4718600 | tf_op jit(solution)/shard_map/ppermute | solution.py:67
  91.4 1.9 collective-permute-start.21
  93.3 1.3 collective-permute-start.2
  94.6 1.3 collective-permute-start.5
  96.0 0.7 reshape_squeeze.3.flags_ref
  96.7 2.0 maximum_select_fusion.1.refs_1_
  98.7 1.0 slice.9
  99.8 9.7 %collective-permute-done.6 = bf16[2,2,128,1536]{3,2,1,0:T(8,128)(2,1)} collective-permute-done((bf16[2,2,128,1536]{3,2,1,0:T(8,128)(2,1)}, bf16[2,2,128,1536]{3,2,1,0:T(8,128)(2,1)}, u32[]{:S(2)}, u32[]{:S(2)}) %collective-permute-start.6) | collective-permute-done | bytes 1572896 | tf_op jit(solution)/shard_map/ppermute | solution.py:35
  109.5 6.8 %collective-permute-start.16 = (bf16[2,1,128,1536]{3,2,1,0:T(8,128)(2,1)}, bf16[2,1,128,1536]{3,2,1,0:T(8,128)(2,1)S(1)}, u32[]{:S(2)}, u32[]{:S(2)}) collective-permute-start(bf16[2,1,128,1536]{3,2,1,0:T(8,128)(2,1)} %slice.9), channel_id=1, source_target_pairs={{1,0},{2,1},{3,2},{4,3},{5,4},{6,5},{7,6},{8,7},{9,8},{10,9},{11,1... | collective-permute-start | bytes 2359304 | tf_op jit(solution)/shard_map/ppermute | solution.py:19
  116.3 39.1 %collective-permute-done.2 = bf16[1,2,128,1536]{3,2,1,0:T(8,128)(2,1)S(1)} collective-permute-done((bf16[1,2,128,1536]{3,2,1,0:T(8,128)(2,1)}, bf16[1,2,128,1536]{3,2,1,0:T(8,128)(2,1)S(1)}, u32[]{:S(2)}, u32[]{:S(2)}) %collective-permute-start.2) | collective-permute-done | bytes 786464 | tf_op jit(solution)/shard_map/ppermute | solution.py:35
  155.4 3.9 %collective-permute-start.17 = (bf16[2,1,128,1536]{3,2,1,0:T(8,128)(2,1)}, bf16[2,1,128,1536]{3,2,1,0:T(8,128)(2,1)S(1)}, u32[]{:S(2)}, u32[]{:S(2)}) collective-permute-start(bf16[2,1,128,1536]{3,2,1,0:T(8,128)(2,1)} %slice.9), channel_id=1, source_target_pairs={{0,1},{1,2},{2,3},{3,4},{4,5},{5,6},{6,7},{7,8},{8,9},{9,10},{10,1... | collective-permute-start | bytes 2359304 | tf_op jit(solution)/shard_map/ppermute | solution.py:19
  159.3 38.3 %collective-permute-done.5 = bf16[1,2,128,1536]{3,2,1,0:T(8,128)(2,1)S(1)} collective-permute-done((bf16[1,2,128,1536]{3,2,1,0:T(8,128)(2,1)}, bf16[1,2,128,1536]{3,2,1,0:T(8,128)(2,1)S(1)}, u32[]{:S(2)}, u32[]{:S(2)}) %collective-permute-start.5) | collective-permute-done | bytes 786464 | tf_op jit(solution)/shard_map/ppermute | solution.py:35
  197.6 0.2 maximum_select_fusion.refs_0_
  197.8 1.0 slice.8
  198.8 2.5 %collective-permute-start.14 = (bf16[2,1,128,1536]{3,2,1,0:T(8,128)(2,1)}, bf16[2,1,128,1536]{3,2,1,0:T(8,128)(2,1)S(1)}, u32[]{:S(2)}, u32[]{:S(2)}) collective-permute-start(bf16[2,1,128,1536]{3,2,1,0:T(8,128)(2,1)} %slice.8), channel_id=1, source_target_pairs={{1,0},{2,1},{3,2},{4,3},{5,4},{6,5},{7,6},{8,7},{9,8},{10,9},{11,1... | collective-permute-start | bytes 2359304 | tf_op jit(solution)/shard_map/ppermute | solution.py:19
  201.4 3.1 %collective-permute-start.15 = (bf16[2,1,128,1536]{3,2,1,0:T(8,128)(2,1)}, bf16[2,1,128,1536]{3,2,1,0:T(8,128)(2,1)S(1)}, u32[]{:S(2)}, u32[]{:S(2)}) collective-permute-start(bf16[2,1,128,1536]{3,2,1,0:T(8,128)(2,1)} %slice.8), channel_id=1, source_target_pairs={{0,1},{1,2},{2,3},{3,4},{4,5},{5,6},{6,7},{7,8},{8,9},{9,10},{10,1... | collective-permute-start | bytes 2359304 | tf_op jit(solution)/shard_map/ppermute | solution.py:19
  204.4 3.7 %broadcast_select_fusion = (bf16[2,2,128,1536]{3,2,1,0:T(8,128)(2,1)}, bf16[2,2,128,1536]{3,2,1,0:T(8,128)(2,1)}) fusion(bf16[2,2,128,1536]{3,2,1,0:T(8,128)(2,1)} %collective-permute-done.21, bf16[2,2,128,1536]{3,2,1,0:T(8,128)(2,1)} %collective-permute-done.20, pred[]{:T(512)S(6)} %eq.15), kind=kLoop, calls=%fused_computation.3 | loop fusion | flops 1572864 | bytes 6291457 | tf_op jit(solution)/shard_map/jit(_where)/select_n | solution.py:80
  208.2 14.3 %shard_map.46 = (f32[12,2,128,1]{3,2,1,0:T(8,128)}, f32[12,2,128,1]{3,2,1,0:T(8,128)}, f32[2,128,1536]{2,1,0:T(8,128)}) custom-call(s32[50]{0:T(128)} %reshape_squeeze.3.flags_ref, bf16[2,128,1536]{2,1,0:T(8,128)(2,1)} %q_ref.3, bf16[2,2,128,1536]{3,2,1,0:T(8,128)(2,1)} %pad_maximum_fusion.refs_0_, bf16[2,2,128,1536]{3,2,1,0:T(8,128)(2,1)} %copy-done.2, ...), custom_call_target="tpu_custom_call" | custom-call | flops 3221225472 | bytes 10223616 | tf_op jit(solution)/shard_map/pallas_call | solution.py:216
  222.5 0.9 copy-done.4
  223.4 0.3 copy-done.5
  223.7 0.3 copy-done.6
  224.0 0.2 copy-done.7
  224.2 14.9 %shard_map.47 = bf16[2,128,1536]{2,1,0:T(8,128)(2,1)} custom-call(s32[50]{0:T(128)} %reshape_squeeze.3.flags_ref, bf16[2,128,1536]{2,1,0:T(8,128)(2,1)} %q_ref.3, bf16[2,2,128,1536]{3,2,1,0:T(8,128)(2,1)} %copy-done.1, bf16[2,2,128,1536]{3,2,1,0:T(8,128)(2,1)} %copy-done, bf16[2,1,128,1536]{3,2,1,0:T(8,128)(2,1)} %copy-done.6, ...), custom_call_target="tpu_custom_call" | custom-call | flops 2013265920 | bytes 11796480 | tf_op jit(solution)/shard_map/pallas_call | solution.py:217
  (29 shorter events, 0.1 us)
Async XLA Ops:
  0.0 21.2 %collective-permute-start.10 = (bf16[1,2,128,1536]{3,2,1,0:T(8,128)(2,1)}, bf16[1,2,128,1536]{3,2,1,0:T(8,128)(2,1)}, u32[]{:S(2)}, u32[]{:S(2)}) collective-permute-start(bf16[1,2,128,1536]{3,2,1,0:T(8,128)(2,1)} %bitcast.5), channel_id=1, source_target_pairs={{128,192},{256,320},{384,448},{129,193},{257,321},{385,449},{130,1... | collective-permute-start | bytes 2359304 | tf_op jit(solution)/shard_map/ppermute | solution.py:35
  5.5 15.6 %copy-start.8 = (bf16[2,128,1536]{2,1,0:T(8,128)(2,1)S(1)}, bf16[2,128,1536]{2,1,0:T(8,128)(2,1)}, u32[]{:S(2)}) copy-start(bf16[2,128,1536]{2,1,0:T(8,128)(2,1)} %param.5) | copy-start | bytes 2359300
  5.5 32.5 %copy-start.9 = (bf16[2,128,1536]{2,1,0:T(8,128)(2,1)S(1)}, bf16[2,128,1536]{2,1,0:T(8,128)(2,1)}, u32[]{:S(2)}) copy-start(bf16[2,128,1536]{2,1,0:T(8,128)(2,1)} %param.6) | copy-start | bytes 2359300
  5.6 32.5 %collective-permute-start.7 = (bf16[1,2,128,1536]{3,2,1,0:T(8,128)(2,1)}, bf16[1,2,128,1536]{3,2,1,0:T(8,128)(2,1)}, u32[]{:S(2)}, u32[]{:S(2)}) collective-permute-start(bf16[1,2,128,1536]{3,2,1,0:T(8,128)(2,1)} %bitcast.2), channel_id=1, source_target_pairs={{128,160},{256,288},{384,416},{129,161},{257,289},{385,417},{130,1... | collective-permute-start | bytes 2359304 | tf_op jit(solution)/shard_map/ppermute | solution.py:35
  10.6 37.2 %collective-permute-start.18 = (bf16[2,2,128,1536]{3,2,1,0:T(8,128)(2,1)}, bf16[2,2,128,1536]{3,2,1,0:T(8,128)(2,1)S(1)}, u32[]{:S(2)}, u32[]{:S(2)}) collective-permute-start(bf16[2,2,128,1536]{3,2,1,0:T(8,128)(2,1)} %pad_maximum_fusion.refs_0_), channel_id=1, source_target_pairs={{2,0},{3,1},{4,2},{5,3},{6,4},{7,5},{8,6},{9,7},{10,8},{11,9},{12,... | collective-permute-start | bytes 4718600 | tf_op jit(solution)/shard_map/ppermute | solution.py:19
  13.2 36.9 %collective-permute-start.19 = (bf16[2,2,128,1536]{3,2,1,0:T(8,128)(2,1)}, bf16[2,2,128,1536]{3,2,1,0:T(8,128)(2,1)S(1)}, u32[]{:S(2)}, u32[]{:S(2)}) collective-permute-start(bf16[2,2,128,1536]{3,2,1,0:T(8,128)(2,1)} %pad_maximum_fusion.refs_0_), channel_id=1, source_target_pairs={{0,2},{1,3},{2,4},{3,5},{4,6},{5,7},{6,8},{7,9},{8,10},{9,11},{10,... | collective-permute-start | bytes 4718600 | tf_op jit(solution)/shard_map/ppermute | solution.py:19
  15.9 36.6 %collective-permute-start.13 = (bf16[2,2,128,1536]{3,2,1,0:T(8,128)(2,1)}, bf16[2,2,128,1536]{3,2,1,0:T(8,128)(2,1)}, u32[]{:S(2)}, u32[]{:S(2)}) collective-permute-start(bf16[2,2,128,1536]{3,2,1,0:T(8,128)(2,1)} %pad_maximum_fusion.refs_0_), channel_id=1, source_target_pairs={{32,0},{64,32},{96,64},{160,128},{192,160},{224,192},{288,256},{32... | collective-permute-start | bytes 4718600 | tf_op jit(solution)/shard_map/ppermute | solution.py:35
  21.2 18.4 %collective-permute-start = (bf16[1,2,128,1536]{3,2,1,0:T(8,128)(2,1)S(1)}, bf16[1,2,128,1536]{3,2,1,0:T(8,128)(2,1)}, u32[]{:S(2)}, u32[]{:S(2)}) collective-permute-start(bf16[1,2,128,1536]{3,2,1,0:T(8,128)(2,1)S(1)} %bitcast.4), channel_id=1, source_target_pairs={{96,32},{224,160},{352,288},{97,33},{225,161},{353,289},{98,34},{2... | collective-permute-start | bytes 2359304 | tf_op jit(solution)/shard_map/ppermute | solution.py:35
  38.0 3.1 %collective-permute-start.3 = (bf16[1,2,128,1536]{3,2,1,0:T(8,128)(2,1)S(1)}, bf16[1,2,128,1536]{3,2,1,0:T(8,128)(2,1)}, u32[]{:S(2)}, u32[]{:S(2)}) collective-permute-start(bf16[1,2,128,1536]{3,2,1,0:T(8,128)(2,1)S(1)} %bitcast.7), channel_id=1, source_target_pairs={{96,64},{224,192},{352,320},{97,65},{225,193},{353,321},{98,66},{2... | collective-permute-start | bytes 2359304 | tf_op jit(solution)/shard_map/ppermute | solution.py:35
  39.6 41.1 %collective-permute-start.11 = (bf16[1,2,128,1536]{3,2,1,0:T(8,128)(2,1)}, bf16[1,2,128,1536]{3,2,1,0:T(8,128)(2,1)}, u32[]{:S(2)}, u32[]{:S(2)}) collective-permute-start(bf16[1,2,128,1536]{3,2,1,0:T(8,128)(2,1)} %collective-permute-done.10), channel_id=1, source_target_pairs={{192,64},{320,192},{448,320},{193,65},{321,193},{449,321},{194,66}... | collective-permute-start | bytes 2359304 | tf_op jit(solution)/shard_map/ppermute | solution.py:35
  41.1 41.1 %collective-permute-start.8 = (bf16[1,2,128,1536]{3,2,1,0:T(8,128)(2,1)}, bf16[1,2,128,1536]{3,2,1,0:T(8,128)(2,1)}, u32[]{:S(2)}, u32[]{:S(2)}) collective-permute-start(bf16[1,2,128,1536]{3,2,1,0:T(8,128)(2,1)} %collective-permute-done.7), channel_id=1, source_target_pairs={{160,32},{288,160},{416,288},{161,33},{289,161},{417,289},{162,34}... | collective-permute-start | bytes 2359304 | tf_op jit(solution)/shard_map/ppermute | solution.py:35
  47.8 37.3 %copy-start.2 = (bf16[2,2,128,1536]{3,2,1,0:T(8,128)(2,1)}, bf16[2,2,128,1536]{3,2,1,0:T(8,128)(2,1)S(1)}, u32[]{:S(2)}) copy-start(bf16[2,2,128,1536]{3,2,1,0:T(8,128)(2,1)S(1)} %collective-permute-done.18.refs_1_) | copy-start | bytes 4718596
  47.8 37.3 %collective-permute-start.1 = (bf16[1,2,128,1536]{3,2,1,0:T(8,128)(2,1)}, bf16[1,2,128,1536]{3,2,1,0:T(8,128)(2,1)}, u32[]{:S(2)}, u32[]{:S(2)}) collective-permute-start(bf16[1,2,128,1536]{3,2,1,0:T(8,128)(2,1)} %collective-permute-done), channel_id=1, source_target_pairs={{32,160},{160,288},{288,416},{33,161},{161,289},{289,417},{34,162}... | collective-permute-start | bytes 2359304 | tf_op jit(solution)/shard_map/ppermute | solution.py:35
  50.2 34.9 %copy-start.3 = (bf16[2,2,128,1536]{3,2,1,0:T(8,128)(2,1)}, bf16[2,2,128,1536]{3,2,1,0:T(8,128)(2,1)S(1)}, u32[]{:S(2)}) copy-start(bf16[2,2,128,1536]{3,2,1,0:T(8,128)(2,1)S(1)} %collective-permute-done.19.refs_2_) | copy-start | bytes 4718596
  50.2 41.2 %collective-permute-start.4 = (bf16[1,2,128,1536]{3,2,1,0:T(8,128)(2,1)}, bf16[1,2,128,1536]{3,2,1,0:T(8,128)(2,1)}, u32[]{:S(2)}, u32[]{:S(2)}) collective-permute-start(bf16[1,2,128,1536]{3,2,1,0:T(8,128)(2,1)} %collective-permute-done.3), channel_id=1, source_target_pairs={{64,192},{192,320},{320,448},{65,193},{193,321},{321,449},{66,194}... | collective-permute-start | bytes 2359304 | tf_op jit(solution)/shard_map/ppermute | solution.py:35
  51.7 44.2 %copy-start.10 = (s32[2,1,5,5]{3,1,2,0:T(1,128)S(1)}, s32[2,1,5,5]{3,1,2,0:T(1,128)}, u32[]{:S(2)}) copy-start(s32[2,1,5,5]{3,1,2,0:T(1,128)} %param.7) | copy-start | bytes 604
  52.5 56.9 %collective-permute-start.6 = (bf16[2,2,128,1536]{3,2,1,0:T(8,128)(2,1)}, bf16[2,2,128,1536]{3,2,1,0:T(8,128)(2,1)}, u32[]{:S(2)}, u32[]{:S(2)}) collective-permute-start(bf16[2,2,128,1536]{3,2,1,0:T(8,128)(2,1)} %pad_maximum_fusion.refs_0_), channel_id=1, source_target_pairs={{0,32},{32,64},{64,96},{128,160},{160,192},{192,224},{256,288},{28... | collective-permute-start | bytes 4718600 | tf_op jit(solution)/shard_map/ppermute | solution.py:35
  80.6 12.7 %collective-permute-start.12 = (bf16[1,2,128,1536]{3,2,1,0:T(8,128)(2,1)}, bf16[1,2,128,1536]{3,2,1,0:T(8,128)(2,1)}, u32[]{:S(2)}, u32[]{:S(2)}) collective-permute-start(bf16[1,2,128,1536]{3,2,1,0:T(8,128)(2,1)} %collective-permute-done.11), channel_id=1, source_target_pairs={{64,96},{192,224},{320,352},{65,97},{193,225},{321,353},{66,98},{1... | collective-permute-start | bytes 2359304 | tf_op jit(solution)/shard_map/ppermute | solution.py:35
  82.2 12.4 %collective-permute-start.9 = (bf16[1,2,128,1536]{3,2,1,0:T(8,128)(2,1)}, bf16[1,2,128,1536]{3,2,1,0:T(8,128)(2,1)}, u32[]{:S(2)}, u32[]{:S(2)}) collective-permute-start(bf16[1,2,128,1536]{3,2,1,0:T(8,128)(2,1)} %collective-permute-done.8), channel_id=1, source_target_pairs={{32,96},{160,224},{288,352},{33,97},{161,225},{289,353},{34,98},{1... | collective-permute-start | bytes 2359304 | tf_op jit(solution)/shard_map/ppermute | solution.py:35
  85.1 116.2 %collective-permute-start.20 = (bf16[2,2,128,1536]{3,2,1,0:T(8,128)(2,1)}, bf16[2,2,128,1536]{3,2,1,0:T(8,128)(2,1)}, u32[]{:S(2)}, u32[]{:S(2)}) collective-permute-start(bf16[2,2,128,1536]{3,2,1,0:T(8,128)(2,1)} %pad_maximum_fusion.refs_0_), channel_id=1, source_target_pairs={{0,1},{1,0},{2,3},{3,2},{4,5},{5,4},{6,7},{7,6},{8,9},{9,8},{10,11... | collective-permute-start | bytes 4718600 | tf_op jit(solution)/shard_map/ppermute | solution.py:67
  91.4 113.0 %collective-permute-start.21 = (bf16[2,2,128,1536]{3,2,1,0:T(8,128)(2,1)}, bf16[2,2,128,1536]{3,2,1,0:T(8,128)(2,1)}, u32[]{:S(2)}, u32[]{:S(2)}) collective-permute-start(bf16[2,2,128,1536]{3,2,1,0:T(8,128)(2,1)} %broadcast_select_fusion.2), channel_id=1, source_target_pairs={{0,1},{1,0},{2,3},{3,2},{4,5},{5,4},{6,7},{7,6},{8,9},{9,8},{10,11... | collective-permute-start | bytes 4718600 | tf_op jit(solution)/shard_map/ppermute | solution.py:67
  93.3 62.1 %collective-permute-start.2 = (bf16[1,2,128,1536]{3,2,1,0:T(8,128)(2,1)}, bf16[1,2,128,1536]{3,2,1,0:T(8,128)(2,1)S(1)}, u32[]{:S(2)}, u32[]{:S(2)}) collective-permute-start(bf16[1,2,128,1536]{3,2,1,0:T(8,128)(2,1)} %collective-permute-done.1), channel_id=1, source_target_pairs={{160,128},{288,256},{416,384},{161,129},{289,257},{417,385},{162,1... | collective-permute-start | bytes 2359304 | tf_op jit(solution)/shard_map/ppermute | solution.py:35
  94.6 103.0 %collective-permute-start.5 = (bf16[1,2,128,1536]{3,2,1,0:T(8,128)(2,1)}, bf16[1,2,128,1536]{3,2,1,0:T(8,128)(2,1)S(1)}, u32[]{:S(2)}, u32[]{:S(2)}) collective-permute-start(bf16[1,2,128,1536]{3,2,1,0:T(8,128)(2,1)} %collective-permute-done.4), channel_id=1, source_target_pairs={{192,128},{320,256},{448,384},{193,129},{321,257},{449,385},{194,1... | collective-permute-start | bytes 2359304 | tf_op jit(solution)/shard_map/ppermute | solution.py:35
  98.7 99.1 %copy-start = (bf16[2,2,128,1536]{3,2,1,0:T(8,128)(2,1)}, bf16[2,2,128,1536]{3,2,1,0:T(8,128)(2,1)S(1)}, u32[]{:S(2)}) copy-start(bf16[2,2,128,1536]{3,2,1,0:T(8,128)(2,1)S(1)} %maximum_select_fusion.1.refs_1_) | copy-start | bytes 4718596
  109.5 113.0 %collective-permute-start.16 = (bf16[2,1,128,1536]{3,2,1,0:T(8,128)(2,1)}, bf16[2,1,128,1536]{3,2,1,0:T(8,128)(2,1)S(1)}, u32[]{:S(2)}, u32[]{:S(2)}) collective-permute-start(bf16[2,1,128,1536]{3,2,1,0:T(8,128)(2,1)} %slice.9), channel_id=1, source_target_pairs={{1,0},{2,1},{3,2},{4,3},{5,4},{6,5},{7,6},{8,7},{9,8},{10,9},{11,1... | collective-permute-start | bytes 2359304 | tf_op jit(solution)/shard_map/ppermute | solution.py:19
  155.4 67.1 %collective-permute-start.17 = (bf16[2,1,128,1536]{3,2,1,0:T(8,128)(2,1)}, bf16[2,1,128,1536]{3,2,1,0:T(8,128)(2,1)S(1)}, u32[]{:S(2)}, u32[]{:S(2)}) collective-permute-start(bf16[2,1,128,1536]{3,2,1,0:T(8,128)(2,1)} %slice.9), channel_id=1, source_target_pairs={{0,1},{1,2},{2,3},{3,4},{4,5},{5,6},{6,7},{7,8},{8,9},{9,10},{10,1... | collective-permute-start | bytes 2359304 | tf_op jit(solution)/shard_map/ppermute | solution.py:19
  197.8 10.3 %copy-start.1 = (bf16[2,2,128,1536]{3,2,1,0:T(8,128)(2,1)}, bf16[2,2,128,1536]{3,2,1,0:T(8,128)(2,1)S(1)}, u32[]{:S(2)}) copy-start(bf16[2,2,128,1536]{3,2,1,0:T(8,128)(2,1)S(1)} %maximum_select_fusion.refs_0_) | copy-start | bytes 4718596
  198.8 23.7 %collective-permute-start.14 = (bf16[2,1,128,1536]{3,2,1,0:T(8,128)(2,1)}, bf16[2,1,128,1536]{3,2,1,0:T(8,128)(2,1)S(1)}, u32[]{:S(2)}, u32[]{:S(2)}) collective-permute-start(bf16[2,1,128,1536]{3,2,1,0:T(8,128)(2,1)} %slice.8), channel_id=1, source_target_pairs={{1,0},{2,1},{3,2},{4,3},{5,4},{6,5},{7,6},{8,7},{9,8},{10,9},{11,1... | collective-permute-start | bytes 2359304 | tf_op jit(solution)/shard_map/ppermute | solution.py:19
  201.4 21.2 %collective-permute-start.15 = (bf16[2,1,128,1536]{3,2,1,0:T(8,128)(2,1)}, bf16[2,1,128,1536]{3,2,1,0:T(8,128)(2,1)S(1)}, u32[]{:S(2)}, u32[]{:S(2)}) collective-permute-start(bf16[2,1,128,1536]{3,2,1,0:T(8,128)(2,1)} %slice.8), channel_id=1, source_target_pairs={{0,1},{1,2},{2,3},{3,4},{4,5},{5,6},{6,7},{7,8},{8,9},{9,10},{10,1... | collective-permute-start | bytes 2359304 | tf_op jit(solution)/shard_map/ppermute | solution.py:19
  222.5 0.9 copy-start.4
  222.5 1.2 copy-start.5
  222.5 1.5 copy-start.6
  222.5 1.7 copy-start.7

commit v12 on v10

--- a/solution.py
+++ b/solution.py
@@ -154,83 +154,50 @@
     return jnp.sum(tile_sum, axis=1, keepdims=True), summed
 
 
-def local_kernel(flags_ref, q_ref, *refs):
-    *sources, max_ref, sum_ref, acc_ref = refs
-    for head in range(max_ref.shape[0]):
+def attention_kernel(flags_ref, q_ref, *refs):
+    *sources, o_ref = refs
+    everything = tuple(range(len(sources)))
+    for head in range(HEAD_GROUP):
         lanes = slice(head * HD, (head + 1) * HD)
         for frame in range(q_ref.shape[0]):
             score_list, value_list, row_max = scored_pairs(
-                flags_ref, q_ref[frame, :, lanes], sources, frame, LOCAL, lanes
+                flags_ref, q_ref[frame, :, lanes], sources, frame, everything, lanes
             )
             denominator, summed = weighted_sums(score_list, value_list, row_max)
-            max_ref[head, frame] = row_max
-            sum_ref[head, frame] = denominator
-            acc_ref[frame, :, lanes] = summed
-
-
-def remote_kernel(flags_ref, q_ref, *refs):
-    *sources, max_ref, sum_ref, acc_ref, o_ref = refs
-    for head in range(max_ref.shape[0]):
-        lanes = slice(head * HD, (head + 1) * HD)
-        for frame in range(q_ref.shape[0]):
-            score_list, value_list, remote_max = scored_pairs(
-                flags_ref, q_ref[frame, :, lanes], sources, frame, REMOTE, lanes
-            )
-            local_max = max_ref[head, frame]
-            row_max = jnp.maximum(local_max, remote_max)
-            rescale = jnp.exp(local_max - row_max)
-            denominator, summed = weighted_sums(score_list, value_list, row_max)
-            denominator = denominator + rescale * sum_ref[head, frame]
-            summed = summed + rescale * acc_ref[frame, :, lanes]
             o_ref[frame, :, lanes] = (summed / denominator).astype(o_ref.dtype)
 
 
 def attend(queries, sources, tile_flags):
     frame_count, row_count, feature_width = queries.shape
     head_count = feature_width // HD
-    group = HEAD_GROUP
-    steps = head_count // group
+    steps = head_count // HEAD_GROUP
     flags = tile_flags.reshape(-1).astype(jnp.int32)
+    tile_spec = pl.BlockSpec(
+        (frame_count, row_count, HEAD_GROUP * HD), lambda h, flags: (0, 0, h)
+    )
+
     def source_spec(source):
-        return pl.BlockSpec((2, source.shape[1], row_count, group * HD), lambda h, flags: (0, 0, 0, h))
-
-    tile_spec = pl.BlockSpec((frame_count, row_count, group * HD), lambda h, flags: (0, 0, h))
-    stat_spec = pl.BlockSpec((group, frame_count, row_count, 1), lambda h, flags: (h, 0, 0, 0))
-    stat_shape = jax.ShapeDtypeStruct((head_count, frame_count, row_count, 1), jnp.float32)
-    acc_shape = jax.ShapeDtypeStruct(queries.shape, jnp.float32)
-    local_sources = [sources[i] for i in LOCAL]
-    remote_sources = [sources[i] for i in REMOTE]
-
-    def cost(count, extra):
-        return pl.CostEstimate(
-            flops=4 * frame_count * head_count * count * row_count * row_count * HD,
-            transcendentals=frame_count * head_count * count * row_count * row_count,
-            bytes_accessed=(2 + 4 * extra + 4) * frame_count * row_count * feature_width,
+        return pl.BlockSpec(
+            (2, source.shape[1], row_count, HEAD_GROUP * HD), lambda h, flags: (0, 0, 0, h)
         )
 
-    stats = pl.pallas_call(
-        local_kernel,
+    pairs = len(band_list())
+    cost = pl.CostEstimate(
+        flops=4 * frame_count * head_count * pairs * row_count * row_count * HD,
+        transcendentals=frame_count * head_count * pairs * row_count * row_count,
+        bytes_accessed=(2 + 4 * len(sources)) * frame_count * row_count * feature_width,
+    )
+    return pl.pallas_call(
+        attention_kernel,
         grid_spec=pltpu.PrefetchScalarGridSpec(
             num_scalar_prefetch=1,
             grid=(steps,),
-            in_specs=[tile_spec] + [source_spec(s) for s in local_sources],
-            out_specs=[stat_spec, stat_spec, tile_spec],
-        ),
-        out_shape=[stat_shape, stat_shape, acc_shape],
-        cost_estimate=cost(16, len(local_sources)),
-    )(flags, queries, *local_sources)
-    return pl.pallas_call(
-        remote_kernel,
-        grid_spec=pltpu.PrefetchScalarGridSpec(
-            num_scalar_prefetch=1,
-            grid=(steps,),
-            in_specs=[tile_spec] + [source_spec(s) for s in remote_sources]
-            + [stat_spec, stat_spec, tile_spec],
+            in_specs=[tile_spec] + [source_spec(s) for s in sources],
             out_specs=tile_spec,
         ),
         out_shape=jax.ShapeDtypeStruct(queries.shape, queries.dtype),
-        cost_estimate=cost(10, len(remote_sources)),
-    )(flags, queries, *remote_sources, *stats)
+        cost_estimate=cost,
+    )(flags, queries, *sources)
 
 
 def on_device(queries, keys, values, tile_mask):

time: 240 us -> 271 us (1.13)
  the two profiles are of different devices: /device:TPU:417 before, /device:TPU:152 now
where the time goes in v12:
time: 271 us; the launch traced here: 270 us
  waiting for transfers between devices  185 us (68%)
  starting transfers between devices  52 us (19%)
  Pallas kernels  19.7 us (7%)
  other arithmetic  11 us (4%)
    ppermute x14, waiting for transfers between devices, routed(): return lax.ppermute(block, 'tm', pairs) if pairs else jnp.zeros_like(block)  158 us
    ppermute x6, waiting for transfers between devices, shifted(): return lax.ppermute(block, axis, route)  26.6 us
    ppermute x14, starting transfers between devices, routed(): return lax.ppermute(block, 'tm', pairs) if pairs else jnp.zeros_like(block)  24.6 us
    ppermute x6, starting transfers between devices, shifted(): return lax.ppermute(block, axis, route)  23 us
    pallas_call x1, Pallas kernels, attend(): pl.pallas_call(attention_kernel, grid_spec=pltpu.PrefetchScalarGridSpec(n...  19.7 us
  transfers between devices with their start and end apart: 22, of which 9 were waited for; matrix products, arithmetic and copies ran while one was open for 4% of the time, Pallas kernels for 0%

profile of v12, /device:TPU:152, one launch (start us, length us, event | category | flops | bytes accessed | tf_op | source)
XLA Modules:
  0.0 270.2 jit_solution(3391976581557251442)
XLA Ops:
  0.0 2.8 %pad_maximum_fusion.refs_0_ = bf16[2,2,128,1536]{3,2,1,0:T(8,128)(2,1)} fusion(bf16[1,2,128,1536]{3,2,1,0:T(8,128)(2,1)} %bitcast.2, bf16[1,2,128,1536]{3,2,1,0:T(8,128)(2,1)} %bitcast.5), kind=kLoop, calls=%fused_computation | loop fusion | flops 786432 | bytes 3145728 | tf_op jit(solution)/shard_map/stack | solution.py:204
  2.8 3.5 %collective-permute-start.6 = (bf16[2,2,128,1536]{3,2,1,0:T(8,128)(2,1)}, bf16[2,2,128,1536]{3,2,1,0:T(8,128)(2,1)S(1)}, u32[]{:S(2)}, u32[]{:S(2)}) collective-permute-start(bf16[2,2,128,1536]{3,2,1,0:T(8,128)(2,1)} %pad_maximum_fusion.refs_0_), channel_id=1, source_target_pairs={{0,32},{32,64},{64,96},{128,160},{160,192},{192,224},{256,288},{28... | collective-permute-start | bytes 4718600 | tf_op jit(solution)/shard_map/ppermute | solution.py:42
  6.3 0.7 collective-permute-start.3
  7.1 0.7 collective-permute-start
  7.8 5.2 %collective-permute-start.10 = (bf16[1,2,128,1536]{3,2,1,0:T(8,128)(2,1)S(1)}, bf16[1,2,128,1536]{3,2,1,0:T(8,128)(2,1)S(1)}, u32[]{:S(2)}, u32[]{:S(2)}) collective-permute-start(bf16[1,2,128,1536]{3,2,1,0:T(8,128)(2,1)S(1)} %bitcast.4), channel_id=1, source_target_pairs={{128,192},{256,320},{384,448},{129,193},{257,321},{385,449},{130,1... | collective-permute-start | bytes 2359304 | tf_op jit(solution)/shard_map/ppermute | solution.py:42
  12.9 2.2 collective-permute-start.7
  15.1 0.0 collective-permute-done.3
  15.1 6.7 %collective-permute-start.14 = (bf16[2,2,128,1536]{3,2,1,0:T(8,128)(2,1)}, bf16[2,2,128,1536]{3,2,1,0:T(8,128)(2,1)S(1)}, u32[]{:S(2)}, u32[]{:S(2)}) collective-permute-start(bf16[2,2,128,1536]{3,2,1,0:T(8,128)(2,1)} %pad_maximum_fusion.refs_0_), channel_id=1, source_target_pairs={{2,0},{3,1},{4,2},{5,3},{6,4},{7,5},{8,6},{9,7},{10,8},{11,9},{12,... | collective-permute-start | bytes 4718600 | tf_op jit(solution)/shard_map/ppermute | solution.py:18
  21.9 1.9 collective-permute-start.15
  23.8 34.3 %collective-permute-done.10 = bf16[1,2,128,1536]{3,2,1,0:T(8,128)(2,1)S(1)} collective-permute-done((bf16[1,2,128,1536]{3,2,1,0:T(8,128)(2,1)S(1)}, bf16[1,2,128,1536]{3,2,1,0:T(8,128)(2,1)S(1)}, u32[]{:S(2)}, u32[]{:S(2)}) %collective-permute-start.10) | collective-permute-done | bytes 786464 | tf_op jit(solution)/shard_map/ppermute | solution.py:42
  58.0 1.6 collective-permute-start.4
  59.7 14.1 %collective-permute-done.7 = bf16[1,2,128,1536]{3,2,1,0:T(8,128)(2,1)} collective-permute-done((bf16[1,2,128,1536]{3,2,1,0:T(8,128)(2,1)S(1)}, bf16[1,2,128,1536]{3,2,1,0:T(8,128)(2,1)}, u32[]{:S(2)}, u32[]{:S(2)}) %collective-permute-start.7) | collective-permute-done | bytes 786464 | tf_op jit(solution)/shard_map/ppermute | solution.py:42
  73.8 1.5 collective-permute-start.1
  75.3 0.0 collective-permute-done.6
  75.3 1.6 collective-permute-start.11
  76.9 0.0 collective-permute-done.4
  76.9 1.5 collective-permute-start.8
  78.4 0.0 collective-permute-done.1
  78.4 1.3 collective-permute-start.13
  79.7 0.0 collective-permute-done.11
  79.7 1.3 collective-permute-start.5
  81.1 1.3 collective-permute-start.2
  82.4 7.2 %collective-permute-done.15.refs_4_ = bf16[2,2,128,1536]{3,2,1,0:T(8,128)(2,1)S(1)} collective-permute-done((bf16[2,2,128,1536]{3,2,1,0:T(8,128)(2,1)}, bf16[2,2,128,1536]{3,2,1,0:T(8,128)(2,1)S(1)}, u32[]{:S(2)}, u32[]{:S(2)}) %collective-permute-start.15) | collective-permute-done | bytes 1572896 | tf_op jit(solution)/shard_map/ppermute | solution.py:18
  89.6 1.9 collective-permute-start.16
  91.5 1.3 broadcast_select_fusion.2
  92.8 0.0 collective-permute-done.8
  92.8 2.4 collective-permute-start.17
  95.2 95.4 %collective-permute-done.5 = bf16[1,2,128,1536]{3,2,1,0:T(8,128)(2,1)} collective-permute-done((bf16[1,2,128,1536]{3,2,1,0:T(8,128)(2,1)}, bf16[1,2,128,1536]{3,2,1,0:T(8,128)(2,1)}, u32[]{:S(2)}, u32[]{:S(2)}) %collective-permute-start.5) | collective-permute-done | bytes 786464 | tf_op jit(solution)/shard_map/ppermute | solution.py:42
  190.6 0.7 collective-permute-start.12
  191.4 14.1 %collective-permute-done.2 = bf16[1,2,128,1536]{3,2,1,0:T(8,128)(2,1)} collective-permute-done((bf16[1,2,128,1536]{3,2,1,0:T(8,128)(2,1)}, bf16[1,2,128,1536]{3,2,1,0:T(8,128)(2,1)}, u32[]{:S(2)}, u32[]{:S(2)}) %collective-permute-start.2) | collective-permute-done | bytes 786464 | tf_op jit(solution)/shard_map/ppermute | solution.py:42
  205.5 1.5 collective-permute-start.9
  207.0 1.6 maximum_select_fusion.refs_1_
  208.6 1.0 slice.8
  209.6 4.2 %collective-permute-start.18 = (bf16[2,1,128,1536]{3,2,1,0:T(8,128)(2,1)}, bf16[2,1,128,1536]{3,2,1,0:T(8,128)(2,1)}, u32[]{:S(2)}, u32[]{:S(2)}) collective-permute-start(bf16[2,1,128,1536]{3,2,1,0:T(8,128)(2,1)} %slice.8), channel_id=1, source_target_pairs={{1,0},{2,1},{3,2},{4,3},{5,4},{6,5},{7,6},{8,7},{9,8},{10,9},{11,1... | collective-permute-start | bytes 2359304 | tf_op jit(solution)/shard_map/ppermute | solution.py:18
  213.9 0.0 copy-start.5
  213.9 1.9 collective-permute-start.19
  215.8 2.1 maximum_select_fusion.1.refs_2_
  217.9 0.0 copy-start.8
  217.9 1.0 slice.9
  219.0 6.3 %collective-permute-start.20 = (bf16[2,1,128,1536]{3,2,1,0:T(8,128)(2,1)}, bf16[2,1,128,1536]{3,2,1,0:T(8,128)(2,1)}, u32[]{:S(2)}, u32[]{:S(2)}) collective-permute-start(bf16[2,1,128,1536]{3,2,1,0:T(8,128)(2,1)} %slice.9), channel_id=1, source_target_pairs={{1,0},{2,1},{3,2},{4,3},{5,4},{6,5},{7,6},{8,7},{9,8},{10,9},{11,1... | collective-permute-start | bytes 2359304 | tf_op jit(solution)/shard_map/ppermute | solution.py:18
  225.3 1.9 collective-permute-start.21
  227.3 0.6 reshape_squeeze.3.flags_ref
  227.9 3.2 %broadcast_select_fusion = (bf16[2,2,128,1536]{3,2,1,0:T(8,128)(2,1)}, bf16[2,2,128,1536]{3,2,1,0:T(8,128)(2,1)}) fusion(bf16[2,2,128,1536]{3,2,1,0:T(8,128)(2,1)S(1)} %collective-permute-done.17, bf16[2,2,128,1536]{3,2,1,0:T(8,128)(2,1)} %collective-permute-done.16, pred[]{:T(512)S(6)} %eq.15), kind=kLoop, calls=%fused_computation.3 | loop fusion | flops 1572864 | bytes 6291457 | tf_op jit(solution)/shard_map/jit(_where)/select_n | solution.py:87
  231.1 1.0 collective-permute-done.18.refs_7_
  232.1 6.5 %collective-permute-done.19.refs_8_ = bf16[2,1,128,1536]{3,2,1,0:T(8,128)(2,1)} collective-permute-done((bf16[2,1,128,1536]{3,2,1,0:T(8,128)(2,1)}, bf16[2,1,128,1536]{3,2,1,0:T(8,128)(2,1)}, u32[]{:S(2)}, u32[]{:S(2)}) %collective-permute-start.19) | collective-permute-done | bytes 786464 | tf_op jit(solution)/shard_map/ppermute | solution.py:18
  238.6 9.8 %collective-permute-done.20.refs_9_ = bf16[2,1,128,1536]{3,2,1,0:T(8,128)(2,1)} collective-permute-done((bf16[2,1,128,1536]{3,2,1,0:T(8,128)(2,1)}, bf16[2,1,128,1536]{3,2,1,0:T(8,128)(2,1)}, u32[]{:S(2)}, u32[]{:S(2)}) %collective-permute-start.20) | collective-permute-done | bytes 786464 | tf_op jit(solution)/shard_map/ppermute | solution.py:18
  248.4 2.1 collective-permute-done.21.refs_10_
  250.5 19.7 %shard_map.46 = bf16[2,128,1536]{2,1,0:T(8,128)(2,1)} custom-call(s32[50]{0:T(128)} %reshape_squeeze.3.flags_ref, bf16[2,128,1536]{2,1,0:T(8,128)(2,1)} %q_ref.1, bf16[2,2,128,1536]{3,2,1,0:T(8,128)(2,1)} %pad_maximum_fusion.refs_0_, bf16[2,2,128,1536]{3,2,1,0:T(8,128)(2,1)} %copy-done, bf16[2,2,128,1536]{3,2,1,0:T(8,128)(2,1)} %copy-done.1, ...), custom_call_target="tpu_custom_call" | custom-call | flops 2617245696 | bytes 18087936 | tf_op jit(solution)/shard_map/pallas_call | solution.py:190
  (24 shorter events, 0.1 us)
Async XLA Ops:
  0.0 6.3 %copy-start.6 = (bf16[2,128,1536]{2,1,0:T(8,128)(2,1)S(1)}, bf16[2,128,1536]{2,1,0:T(8,128)(2,1)}, u32[]{:S(2)}) copy-start(bf16[2,128,1536]{2,1,0:T(8,128)(2,1)} %param.6) | copy-start | bytes 2359300
  0.0 7.0 %copy-start.7 = (bf16[2,128,1536]{2,1,0:T(8,128)(2,1)S(1)}, bf16[2,128,1536]{2,1,0:T(8,128)(2,1)}, u32[]{:S(2)}) copy-start(bf16[2,128,1536]{2,1,0:T(8,128)(2,1)} %param.5) | copy-start | bytes 2359300
  2.8 72.5 %collective-permute-start.6 = (bf16[2,2,128,1536]{3,2,1,0:T(8,128)(2,1)}, bf16[2,2,128,1536]{3,2,1,0:T(8,128)(2,1)S(1)}, u32[]{:S(2)}, u32[]{:S(2)}) collective-permute-start(bf16[2,2,128,1536]{3,2,1,0:T(8,128)(2,1)} %pad_maximum_fusion.refs_0_), channel_id=1, source_target_pairs={{0,32},{32,64},{64,96},{128,160},{160,192},{192,224},{256,288},{28... | collective-permute-start | bytes 4718600 | tf_op jit(solution)/shard_map/ppermute | solution.py:42
  6.3 8.8 %collective-permute-start.3 = (bf16[1,2,128,1536]{3,2,1,0:T(8,128)(2,1)S(1)}, bf16[1,2,128,1536]{3,2,1,0:T(8,128)(2,1)S(1)}, u32[]{:S(2)}, u32[]{:S(2)}) collective-permute-start(bf16[1,2,128,1536]{3,2,1,0:T(8,128)(2,1)S(1)} %bitcast.3), channel_id=1, source_target_pairs={{96,64},{224,192},{352,320},{97,65},{225,193},{353,321},{98,66},{2... | collective-permute-start | bytes 2359304 | tf_op jit(solution)/shard_map/ppermute | solution.py:42
  7.1 14.8 %collective-permute-start = (bf16[1,2,128,1536]{3,2,1,0:T(8,128)(2,1)S(1)}, bf16[1,2,128,1536]{3,2,1,0:T(8,128)(2,1)S(1)}, u32[]{:S(2)}, u32[]{:S(2)}) collective-permute-start(bf16[1,2,128,1536]{3,2,1,0:T(8,128)(2,1)S(1)} %bitcast.6), channel_id=1, source_target_pairs={{96,32},{224,160},{352,288},{97,33},{225,161},{353,289},{98,34},{2... | collective-permute-start | bytes 2359304 | tf_op jit(solution)/shard_map/ppermute | solution.py:42
  7.8 50.3 %collective-permute-start.10 = (bf16[1,2,128,1536]{3,2,1,0:T(8,128)(2,1)S(1)}, bf16[1,2,128,1536]{3,2,1,0:T(8,128)(2,1)S(1)}, u32[]{:S(2)}, u32[]{:S(2)}) collective-permute-start(bf16[1,2,128,1536]{3,2,1,0:T(8,128)(2,1)S(1)} %bitcast.4), channel_id=1, source_target_pairs={{128,192},{256,320},{384,448},{129,193},{257,321},{385,449},{130,1... | collective-permute-start | bytes 2359304 | tf_op jit(solution)/shard_map/ppermute | solution.py:42
  12.9 60.8 %collective-permute-start.7 = (bf16[1,2,128,1536]{3,2,1,0:T(8,128)(2,1)S(1)}, bf16[1,2,128,1536]{3,2,1,0:T(8,128)(2,1)}, u32[]{:S(2)}, u32[]{:S(2)}) collective-permute-start(bf16[1,2,128,1536]{3,2,1,0:T(8,128)(2,1)S(1)} %bitcast.7), channel_id=1, source_target_pairs={{128,160},{256,288},{384,416},{129,161},{257,289},{385,417},{130,1... | collective-permute-start | bytes 2359304 | tf_op jit(solution)/shard_map/ppermute | solution.py:42
  15.1 65.9 %collective-permute-start.14 = (bf16[2,2,128,1536]{3,2,1,0:T(8,128)(2,1)}, bf16[2,2,128,1536]{3,2,1,0:T(8,128)(2,1)S(1)}, u32[]{:S(2)}, u32[]{:S(2)}) collective-permute-start(bf16[2,2,128,1536]{3,2,1,0:T(8,128)(2,1)} %pad_maximum_fusion.refs_0_), channel_id=1, source_target_pairs={{2,0},{3,1},{4,2},{5,3},{6,4},{7,5},{8,6},{9,7},{10,8},{11,9},{12,... | collective-permute-start | bytes 4718600 | tf_op jit(solution)/shard_map/ppermute | solution.py:18
  21.9 67.7 %collective-permute-start.15 = (bf16[2,2,128,1536]{3,2,1,0:T(8,128)(2,1)}, bf16[2,2,128,1536]{3,2,1,0:T(8,128)(2,1)S(1)}, u32[]{:S(2)}, u32[]{:S(2)}) collective-permute-start(bf16[2,2,128,1536]{3,2,1,0:T(8,128)(2,1)} %pad_maximum_fusion.refs_0_), channel_id=1, source_target_pairs={{0,2},{1,3},{2,4},{3,5},{4,6},{5,7},{6,8},{7,9},{8,10},{9,11},{10,... | collective-permute-start | bytes 4718600 | tf_op jit(solution)/shard_map/ppermute | solution.py:18
  58.0 18.8 %collective-permute-start.4 = (bf16[1,2,128,1536]{3,2,1,0:T(8,128)(2,1)S(1)}, bf16[1,2,128,1536]{3,2,1,0:T(8,128)(2,1)}, u32[]{:S(2)}, u32[]{:S(2)}) collective-permute-start(bf16[1,2,128,1536]{3,2,1,0:T(8,128)(2,1)S(1)} %collective-permute-done.3), channel_id=1, source_target_pairs={{64,192},{192,320},{320,448},{65,193},{193,321},{321,449},{66,194}... | collective-permute-start | bytes 2359304 | tf_op jit(solution)/shard_map/ppermute | solution.py:42
  73.8 4.7 %collective-permute-start.1 = (bf16[1,2,128,1536]{3,2,1,0:T(8,128)(2,1)S(1)}, bf16[1,2,128,1536]{3,2,1,0:T(8,128)(2,1)}, u32[]{:S(2)}, u32[]{:S(2)}) collective-permute-start(bf16[1,2,128,1536]{3,2,1,0:T(8,128)(2,1)S(1)} %collective-permute-done), channel_id=1, source_target_pairs={{32,160},{160,288},{288,416},{33,161},{161,289},{289,417},{34,162}... | collective-permute-start | bytes 2359304 | tf_op jit(solution)/shard_map/ppermute | solution.py:42
  75.3 5.7 %copy-start.4 = (bf16[2,2,128,1536]{3,2,1,0:T(8,128)(2,1)}, bf16[2,2,128,1536]{3,2,1,0:T(8,128)(2,1)S(1)}, u32[]{:S(2)}) copy-start(bf16[2,2,128,1536]{3,2,1,0:T(8,128)(2,1)S(1)} %collective-permute-done.6) | copy-start | bytes 4718596
  75.3 4.4 %collective-permute-start.11 = (bf16[1,2,128,1536]{3,2,1,0:T(8,128)(2,1)S(1)}, bf16[1,2,128,1536]{3,2,1,0:T(8,128)(2,1)}, u32[]{:S(2)}, u32[]{:S(2)}) collective-permute-start(bf16[1,2,128,1536]{3,2,1,0:T(8,128)(2,1)S(1)} %collective-permute-done.10), channel_id=1, source_target_pairs={{192,64},{320,192},{448,320},{193,65},{321,193},{449,321},{194,66}... | collective-permute-start | bytes 2359304 | tf_op jit(solution)/shard_map/ppermute | solution.py:42
  76.9 15.9 %collective-permute-start.8 = (bf16[1,2,128,1536]{3,2,1,0:T(8,128)(2,1)}, bf16[1,2,128,1536]{3,2,1,0:T(8,128)(2,1)}, u32[]{:S(2)}, u32[]{:S(2)}) collective-permute-start(bf16[1,2,128,1536]{3,2,1,0:T(8,128)(2,1)} %collective-permute-done.7), channel_id=1, source_target_pairs={{160,32},{288,160},{416,288},{161,33},{289,161},{417,289},{162,34}... | collective-permute-start | bytes 2359304 | tf_op jit(solution)/shard_map/ppermute | solution.py:42
  78.4 131.2 %collective-permute-start.13 = (bf16[2,2,128,1536]{3,2,1,0:T(8,128)(2,1)}, bf16[2,2,128,1536]{3,2,1,0:T(8,128)(2,1)}, u32[]{:S(2)}, u32[]{:S(2)}) collective-permute-start(bf16[2,2,128,1536]{3,2,1,0:T(8,128)(2,1)} %pad_maximum_fusion.refs_0_), channel_id=1, source_target_pairs={{32,0},{64,32},{96,64},{160,128},{192,160},{224,192},{288,256},{32... | collective-permute-start | bytes 4718600 | tf_op jit(solution)/shard_map/ppermute | solution.py:42
  79.7 110.9 %collective-permute-start.5 = (bf16[1,2,128,1536]{3,2,1,0:T(8,128)(2,1)}, bf16[1,2,128,1536]{3,2,1,0:T(8,128)(2,1)}, u32[]{:S(2)}, u32[]{:S(2)}) collective-permute-start(bf16[1,2,128,1536]{3,2,1,0:T(8,128)(2,1)} %collective-permute-done.4), channel_id=1, source_target_pairs={{192,128},{320,256},{448,384},{193,129},{321,257},{449,385},{194,1... | collective-permute-start | bytes 2359304 | tf_op jit(solution)/shard_map/ppermute | solution.py:42
  81.1 11.7 %copy-start.2 = (bf16[2,2,128,1536]{3,2,1,0:T(8,128)(2,1)}, bf16[2,2,128,1536]{3,2,1,0:T(8,128)(2,1)S(1)}, u32[]{:S(2)}) copy-start(bf16[2,2,128,1536]{3,2,1,0:T(8,128)(2,1)S(1)} %collective-permute-done.14.refs_3_) | copy-start | bytes 4718596
  81.1 124.4 %collective-permute-start.2 = (bf16[1,2,128,1536]{3,2,1,0:T(8,128)(2,1)}, bf16[1,2,128,1536]{3,2,1,0:T(8,128)(2,1)}, u32[]{:S(2)}, u32[]{:S(2)}) collective-permute-start(bf16[1,2,128,1536]{3,2,1,0:T(8,128)(2,1)} %collective-permute-done.1), channel_id=1, source_target_pairs={{160,128},{288,256},{416,384},{161,129},{289,257},{417,385},{162,1... | collective-permute-start | bytes 2359304 | tf_op jit(solution)/shard_map/ppermute | solution.py:42
  89.6 3.2 %copy-start.3 = (bf16[2,2,128,1536]{3,2,1,0:T(8,128)(2,1)}, bf16[2,2,128,1536]{3,2,1,0:T(8,128)(2,1)S(1)}, u32[]{:S(2)}) copy-start(bf16[2,2,128,1536]{3,2,1,0:T(8,128)(2,1)S(1)} %collective-permute-done.15.refs_4_) | copy-start | bytes 4718596
  89.6 135.7 %collective-permute-start.16 = (bf16[2,2,128,1536]{3,2,1,0:T(8,128)(2,1)}, bf16[2,2,128,1536]{3,2,1,0:T(8,128)(2,1)}, u32[]{:S(2)}, u32[]{:S(2)}) collective-permute-start(bf16[2,2,128,1536]{3,2,1,0:T(8,128)(2,1)} %pad_maximum_fusion.refs_0_), channel_id=1, source_target_pairs={{0,1},{1,0},{2,3},{3,2},{4,5},{5,4},{6,7},{7,6},{8,9},{9,8},{10,11... | collective-permute-start | bytes 4718600 | tf_op jit(solution)/shard_map/ppermute | solution.py:74
  92.8 135.1 %collective-permute-start.17 = (bf16[2,2,128,1536]{3,2,1,0:T(8,128)(2,1)}, bf16[2,2,128,1536]{3,2,1,0:T(8,128)(2,1)S(1)}, u32[]{:S(2)}, u32[]{:S(2)}) collective-permute-start(bf16[2,2,128,1536]{3,2,1,0:T(8,128)(2,1)} %broadcast_select_fusion.2), channel_id=1, source_target_pairs={{0,1},{1,0},{2,3},{3,2},{4,5},{5,4},{6,7},{7,6},{8,9},{9,8},{10,11... | collective-permute-start | bytes 4718600 | tf_op jit(solution)/shard_map/ppermute | solution.py:74
  190.6 23.2 %collective-permute-start.12 = (bf16[1,2,128,1536]{3,2,1,0:T(8,128)(2,1)}, bf16[1,2,128,1536]{3,2,1,0:T(8,128)(2,1)S(1)}, u32[]{:S(2)}, u32[]{:S(2)}) collective-permute-start(bf16[1,2,128,1536]{3,2,1,0:T(8,128)(2,1)} %collective-permute-done.11), channel_id=1, source_target_pairs={{64,96},{192,224},{320,352},{65,97},{193,225},{321,353},{66,98},{1... | collective-permute-start | bytes 2359304 | tf_op jit(solution)/shard_map/ppermute | solution.py:42
  205.5 10.3 %collective-permute-start.9 = (bf16[1,2,128,1536]{3,2,1,0:T(8,128)(2,1)}, bf16[1,2,128,1536]{3,2,1,0:T(8,128)(2,1)}, u32[]{:S(2)}, u32[]{:S(2)}) collective-permute-start(bf16[1,2,128,1536]{3,2,1,0:T(8,128)(2,1)} %collective-permute-done.8), channel_id=1, source_target_pairs={{32,96},{160,224},{288,352},{33,97},{161,225},{289,353},{34,98},{1... | collective-permute-start | bytes 2359304 | tf_op jit(solution)/shard_map/ppermute | solution.py:42
  208.6 9.3 %copy-start = (bf16[2,2,128,1536]{3,2,1,0:T(8,128)(2,1)}, bf16[2,2,128,1536]{3,2,1,0:T(8,128)(2,1)S(1)}, u32[]{:S(2)}) copy-start(bf16[2,2,128,1536]{3,2,1,0:T(8,128)(2,1)S(1)} %maximum_select_fusion.refs_1_) | copy-start | bytes 4718596
  209.6 22.5 %collective-permute-start.18 = (bf16[2,1,128,1536]{3,2,1,0:T(8,128)(2,1)}, bf16[2,1,128,1536]{3,2,1,0:T(8,128)(2,1)}, u32[]{:S(2)}, u32[]{:S(2)}) collective-permute-start(bf16[2,1,128,1536]{3,2,1,0:T(8,128)(2,1)} %slice.8), channel_id=1, source_target_pairs={{1,0},{2,1},{3,2},{4,3},{5,4},{6,5},{7,6},{8,7},{9,8},{10,9},{11,1... | collective-permute-start | bytes 2359304 | tf_op jit(solution)/shard_map/ppermute | solution.py:18
  213.9 1.9 copy-start.5
  213.9 24.7 %collective-permute-start.19 = (bf16[2,1,128,1536]{3,2,1,0:T(8,128)(2,1)}, bf16[2,1,128,1536]{3,2,1,0:T(8,128)(2,1)}, u32[]{:S(2)}, u32[]{:S(2)}) collective-permute-start(bf16[2,1,128,1536]{3,2,1,0:T(8,128)(2,1)} %slice.8), channel_id=1, source_target_pairs={{0,1},{1,2},{2,3},{3,4},{4,5},{5,6},{6,7},{7,8},{8,9},{9,10},{10,1... | collective-permute-start | bytes 2359304 | tf_op jit(solution)/shard_map/ppermute | solution.py:18
  217.9 13.2 %copy-start.1 = (bf16[2,2,128,1536]{3,2,1,0:T(8,128)(2,1)}, bf16[2,2,128,1536]{3,2,1,0:T(8,128)(2,1)S(1)}, u32[]{:S(2)}) copy-start(bf16[2,2,128,1536]{3,2,1,0:T(8,128)(2,1)S(1)} %maximum_select_fusion.1.refs_2_) | copy-start | bytes 4718596
  217.9 9.3 %copy-start.8 = (s32[2,1,5,5]{3,1,2,0:T(1,128)S(1)}, s32[2,1,5,5]{3,1,2,0:T(1,128)}, u32[]{:S(2)}) copy-start(s32[2,1,5,5]{3,1,2,0:T(1,128)} %param.7) | copy-start | bytes 604
  219.0 29.4 %collective-permute-start.20 = (bf16[2,1,128,1536]{3,2,1,0:T(8,128)(2,1)}, bf16[2,1,128,1536]{3,2,1,0:T(8,128)(2,1)}, u32[]{:S(2)}, u32[]{:S(2)}) collective-permute-start(bf16[2,1,128,1536]{3,2,1,0:T(8,128)(2,1)} %slice.9), channel_id=1, source_target_pairs={{1,0},{2,1},{3,2},{4,3},{5,4},{6,5},{7,6},{8,7},{9,8},{10,9},{11,1... | collective-permute-start | bytes 2359304 | tf_op jit(solution)/shard_map/ppermute | solution.py:18
  225.3 25.2 %collective-permute-start.21 = (bf16[2,1,128,1536]{3,2,1,0:T(8,128)(2,1)}, bf16[2,1,128,1536]{3,2,1,0:T(8,128)(2,1)}, u32[]{:S(2)}, u32[]{:S(2)}) collective-permute-start(bf16[2,1,128,1536]{3,2,1,0:T(8,128)(2,1)} %slice.9), channel_id=1, source_target_pairs={{0,1},{1,2},{2,3},{3,4},{4,5},{5,6},{6,7},{7,8},{8,9},{9,10},{10,1... | collective-permute-start | bytes 2359304 | tf_op jit(solution)/shard_map/ppermute | solution.py:18
